TPU v7x, 256 devices: a whole 4x4x8 slice. The times are simulated.
256 devices in a mesh: pipe: 8 (over z), seq: 32 (over y, x, core).
Axes of the slice: x: 4, y: 4, z: 8, core: 2. Of those that a mesh axis runs over, the one named last changes fastest.
Arguments:
- queries: bfloat16 [8, 4096, 8192], P('pipe', 'seq'), may hold values from -47.6 to 47.6
- keys: bfloat16 [8, 4096, 1024], P('pipe', 'seq'), may hold values from -4 to 4
- values: bfloat16 [8, 4096, 1024], P('pipe', 'seq'), may hold values from -6 to 6
- out_grad: bfloat16 [8, 4096, 8192], P('pipe', 'seq'), may hold values from -6 to 6
- window_blocks: int32 [64, 3], replicated, may hold values from 0 to 63, as said below
- global_blocks: int32 [64, 2], replicated, may hold values from 0 to 63, as said below
- random_blocks: int32 [64, 3], replicated, may hold values from 0 to 63
Outputs:
- handed_queries: bfloat16 [8, 4096, 8192], P('pipe', 'seq')
- handed_keys: bfloat16 [8, 4096, 1024], P('pipe', 'seq')
- handed_values: bfloat16 [8, 4096, 1024], P('pipe', 'seq')
Inputs may be any that keep to these rules, and one draw needn't show every extreme that they name: `window_blocks`: row b lists b - 1, b, b + 1; a neighbour that lies in another document of the pack, or outside the sequence, is replaced by b. `global_blocks`: every row lists the same two blocks: one below 64 // 2, and the last block 64 - 1.
All inputs are finite; a program needn't handle non-finite values.
Results may differ from a plain program's by a relative error of at most 0.012.
The roundings to bfloat16 on the way count: a program that leaves them out, or rounds other values in their place, can miss the bound.
Values may be sent and summed in bfloat16 or wider, within the bound.
No kernel may reach another device: no remote copies, remote signals or barrier semaphores. Data moves between devices by JAX's collectives and lax.ppermute only.
A program may use at most 128 MiB of HBM per device.

v0:
```python
import jax
import jax.numpy as jnp
from jax import lax
from jax.sharding import PartitionSpec as P

HEADS = 64
KV = 8
HD = 128
BLOCK = 64


def from_behind(block, axis, distance):
    devices = range(lax.axis_size(axis))
    route = [(i - distance, i) for i in devices if i - distance in devices]
    return lax.ppermute(block, axis, route)


def block_lists(window_blocks, global_blocks, random_blocks):
    listed = jnp.concatenate([window_blocks, global_blocks, random_blocks], axis=1)
    width = listed.shape[1]
    same = listed[:, :, None] == listed[:, None, :]
    earlier = jnp.arange(width)[None, :] < jnp.arange(width)[:, None]
    repeated = jnp.any(jnp.logical_and(same, earlier[None]), axis=2)
    return (listed, jnp.logical_not(repeated))


def block_grads(q_rows, g_rows, k_blocks, v_blocks, listed, live):
    count = listed.shape[0]
    slots = listed.shape[1]
    block = k_blocks.shape[1]
    depth = k_blocks.shape[2]
    scale = depth ** (-0.5)
    k_near = k_blocks[listed].reshape(count, slots * block, depth)
    v_near = v_blocks[listed].reshape(count, slots * block, depth)
    allowed = jnp.repeat(live, block, axis=1)[:, None, :]
    scores = jnp.einsum("grd,gsd->grs", q_rows, k_near, preferred_element_type=jnp.float32) * scale
    scores = jnp.where(allowed, scores, -jnp.inf)
    top = jnp.max(scores, axis=-1, keepdims=True)
    expd = jnp.exp(scores - top)
    probs = expd / jnp.sum(expd, axis=-1, keepdims=True)
    probs_low = probs.astype(jnp.bfloat16)
    attn_out = jnp.einsum(
        "grs,gsd->grd", probs_low, v_near, preferred_element_type=jnp.float32
    ).astype(jnp.bfloat16)
    attn_out = lax.optimization_barrier(attn_out)
    delta = jnp.sum(
        g_rows.astype(jnp.float32) * attn_out.astype(jnp.float32), axis=-1, keepdims=True
    )
    dprobs = jnp.einsum("grd,gsd->grs", g_rows, v_near, preferred_element_type=jnp.float32)
    ds_low = (probs * (dprobs - delta)).astype(jnp.bfloat16)
    grad_q = (
        jnp.einsum("grs,gsd->grd", ds_low, k_near, preferred_element_type=jnp.float32) * scale
    ).astype(jnp.bfloat16)
    dk_slots = (
        jnp.einsum("grs,grd->gsd", ds_low, q_rows, preferred_element_type=jnp.float32) * scale
    )
    dv_slots = jnp.einsum("grs,grd->gsd", probs_low, g_rows, preferred_element_type=jnp.float32)
    return (
        grad_q,
        dk_slots.reshape(count, slots, block, depth),
        dv_slots.reshape(count, slots, block, depth),
    )


def body(queries, keys, values, out_grad, window_blocks, global_blocks, random_blocks):
    lanes = lax.axis_size("seq")
    tok = queries.shape[1]
    repeat = lanes // KV
    q_local = queries[0].reshape(tok, HEADS, HD)
    g_local = out_grad[0].reshape(tok, HEADS, HD)
    q_heads, g_heads = (
        lax.all_to_all(q_local, "seq", split_axis=1, concat_axis=0, tiled=True),
        lax.all_to_all(g_local, "seq", split_axis=1, concat_axis=0, tiled=True),
    )
    k_all, v_all = (
        lax.all_gather(keys[0], "seq", axis=0, tiled=True),
        lax.all_gather(values[0], "seq", axis=0, tiled=True),
    )
    start = lax.axis_index("seq") // repeat * HD
    k_head = lax.dynamic_slice_in_dim(k_all, start, HD, 1)
    v_head = lax.dynamic_slice_in_dim(v_all, start, HD, 1)
    seqlen = q_heads.shape[0]
    per_device = q_heads.shape[1]
    nblocks = seqlen // BLOCK
    listed, live = block_lists(window_blocks, global_blocks, random_blocks)
    turns = 4
    span = nblocks // turns
    rows = BLOCK * per_device
    q_rows = q_heads.reshape(turns, span, rows, HD)
    g_rows = g_heads.reshape(turns, span, rows, HD)
    k_blocks = k_head.reshape(nblocks, BLOCK, HD)
    v_blocks = v_head.reshape(nblocks, BLOCK, HD)

    def step(carry, parts):
        dk_total, dv_total = carry
        q_part, g_part, list_part, live_part = parts
        grad_q, dk_slots, dv_slots = block_grads(
            q_part, g_part, k_blocks, v_blocks, list_part, live_part
        )
        return (
            (dk_total.at[list_part].add(dk_slots), dv_total.at[list_part].add(dv_slots)),
            grad_q,
        )

    zeros = jnp.zeros((nblocks, BLOCK, HD), jnp.float32)
    inputs = (q_rows, g_rows, listed.reshape(turns, span, -1), live.reshape(turns, span, -1))
    (dk_total, dv_total), grad_q = lax.scan(step, (zeros, zeros), inputs)
    dq_heads = grad_q.reshape(seqlen, per_device, HD)
    dq_tokens = lax.all_to_all(dq_heads, "seq", split_axis=0, concat_axis=1, tiled=True)
    dk_parts, dv_parts = (
        lax.all_to_all(
            dk_total.reshape(seqlen, 1, HD), "seq", split_axis=0, concat_axis=1, tiled=True
        ),
        lax.all_to_all(
            dv_total.reshape(seqlen, 1, HD), "seq", split_axis=0, concat_axis=1, tiled=True
        ),
    )
    dk_tokens = jnp.sum(dk_parts.reshape(tok, KV, repeat, HD), axis=2).astype(jnp.bfloat16)
    dv_tokens = jnp.sum(dv_parts.reshape(tok, KV, repeat, HD), axis=2).astype(jnp.bfloat16)
    dq_flat = dq_tokens.reshape(1, tok, HEADS * HD)
    dk_flat = dk_tokens.reshape(1, tok, KV * HD)
    dv_flat = dv_tokens.reshape(1, tok, KV * HD)
    return from_behind((dq_flat, dk_flat, dv_flat), "pipe", -1)


def solution(mesh):
    in_specs = (
        P("pipe", "seq", None),
        P("pipe", "seq", None),
        P("pipe", "seq", None),
        P("pipe", "seq", None),
        P(),
        P(),
        P(),
    )
    out_specs = (P("pipe", "seq", None), P("pipe", "seq", None), P("pipe", "seq", None))
    return jax.shard_map(body, mesh=mesh, in_specs=in_specs, out_specs=out_specs, check_vma=False)
```

profile of v0, /device:TPU:98, one launch (start us, length us, event | category | flops | bytes accessed | tf_op | source)
XLA Modules:
  0.0 614.2 jit_solution(1255116644743728596)
XLA Ops:
  12.7 7.6 %all-to-all-start = ((bf16[128,64,128]{0,2,1:T(8,128)(2,1)}), bf16[128,64,128]{0,2,1:T(8,128)(2,1)S(1)}, u32[]{:S(2)}, u32[]{:S(2)}) async-start(bf16[128,64,128]{0,2,1:T(8,128)(2,1)} %bitcast.124), calls=%async_computation | async-start | bytes 4194304 | tf_op jit(solution)/shard_map/all_to_all | solution.py:72
  24.4 27.5 %all-to-all-done = bf16[128,64,128]{0,2,1:T(8,128)(2,1)S(1)} async-done(((bf16[128,64,128]{0,2,1:T(8,128)(2,1)}), bf16[128,64,128]{0,2,1:T(8,128)(2,1)S(1)}, u32[]{:S(2)}, u32[]{:S(2)}) %all-to-all-start) | async-done | bytes 2097184 | tf_op jit(solution)/shard_map/all_to_all | solution.py:72
  51.9 6.5 %all-to-all-start.1 = ((bf16[128,64,128]{0,2,1:T(8,128)(2,1)}), bf16[128,64,128]{0,2,1:T(8,128)(2,1)}, u32[]{:S(2)}, u32[]{:S(2)}) async-start(bf16[128,64,128]{0,2,1:T(8,128)(2,1)} %bitcast.123), calls=%async_computation.1 | async-start | bytes 4194304 | tf_op jit(solution)/shard_map/all_to_all | solution.py:73
  62.6 39.5 %all-to-all-done.1 = bf16[128,64,128]{0,2,1:T(8,128)(2,1)} async-done(((bf16[128,64,128]{0,2,1:T(8,128)(2,1)}), bf16[128,64,128]{0,2,1:T(8,128)(2,1)}, u32[]{:S(2)}, u32[]{:S(2)}) %all-to-all-start.1) | async-done | bytes 2097184 | tf_op jit(solution)/shard_map/all_to_all | solution.py:73
  102.1 6.2 %copy.88 = bf16[32,128,2,128]{3,2,1,0:T(2,128)(2,1)} copy(bf16[32,128,2,128]{1,3,2,0:T(8,128)(2,1)} %bitcast.18) | data formatting | bytes 4194304 | tf_op jit(solution)/shard_map/all_to_all | solution.py:73
  109.6 54.3 %all-gather.7.cloned.1.call-done = bf16[1,4096,1024]{2,1,0:T(8,128)(2,1)} async-done(((bf16[1,128,1024]{2,1,0:T(8,128)(2,1)}), bf16[1,4096,1024]{2,1,0:T(8,128)(2,1)}) %all-gather.7.cloned.1.call-update) | async-done | bytes 8388624 | tf_op jit(solution)/shard_map/all_gather | solution.py:77
  169.4 292.9 %while.14 = (s32[]{:T(128)}, f32[64,64,128]{2,1,0:T(8,128)}, f32[64,64,128]{2,1,0:T(8,128)}, bf16[4,16,128,128]{3,2,1,0:T(8,128)(2,1)}, s32[4,16,8]{1,0,2:T(4,12...) while((s32[]{:T(128)}, f32[64,64,128]{2,1,0:T(8,128)}, ...), condition=%wide.region_7.8_spmd, body=%wide.region_1.7_spmd.sunk | while | flops 1628176256 | bytes 138499472 | solution.py:107
  174.9 4.9 fusion.64
  194.9 20.0 %scatter_fusion = f32[64,64,128]{2,1,0:T(8,128)} fusion(f32[64,64,128]{2,1,0:T(8,128)} %get-tuple-element.221, s32[128]{0:T(128)S(1)} %reshape.204, f32[128,64,128]{2,1,0:T(8,128)} %bitcast.110), kind=kCustom, calls=%fused_computation.2.clone.1 | custom fusion | flops 1048576 | bytes 12583424 | tf_op jit(solution)/shard_map/while/body/eval_jaxpr/scatter-add | solution.py:101
  222.4 20.2 %scatter_fusion.1 = f32[64,64,128]{2,1,0:T(8,128)} fusion(f32[64,64,128]{2,1,0:T(8,128)} %get-tuple-element.222, s32[128]{0:T(128)S(1)} %reshape.204, f32[128,64,128]{2,1,0:T(8,128)} %bitcast.109), kind=kCustom, calls=%fused_computation.3.clone.1 | custom fusion | flops 1048576 | bytes 12583424 | tf_op jit(solution)/shard_map/while/body/eval_jaxpr/scatter-add | solution.py:101
  248.1 4.9 fusion.64
  268.1 20.0 %scatter_fusion = f32[64,64,128]{2,1,0:T(8,128)} fusion(f32[64,64,128]{2,1,0:T(8,128)} %get-tuple-element.221, s32[128]{0:T(128)S(1)} %reshape.204, f32[128,64,128]{2,1,0:T(8,128)} %bitcast.110), kind=kCustom, calls=%fused_computation.2.clone.1 | custom fusion | flops 1048576 | bytes 12583424 | tf_op jit(solution)/shard_map/while/body/eval_jaxpr/scatter-add | solution.py:101
  295.6 20.2 %scatter_fusion.1 = f32[64,64,128]{2,1,0:T(8,128)} fusion(f32[64,64,128]{2,1,0:T(8,128)} %get-tuple-element.222, s32[128]{0:T(128)S(1)} %reshape.204, f32[128,64,128]{2,1,0:T(8,128)} %bitcast.109), kind=kCustom, calls=%fused_computation.3.clone.1 | custom fusion | flops 1048576 | bytes 12583424 | tf_op jit(solution)/shard_map/while/body/eval_jaxpr/scatter-add | solution.py:101
  321.4 4.9 fusion.64
  341.4 20.0 %scatter_fusion = f32[64,64,128]{2,1,0:T(8,128)} fusion(f32[64,64,128]{2,1,0:T(8,128)} %get-tuple-element.221, s32[128]{0:T(128)S(1)} %reshape.204, f32[128,64,128]{2,1,0:T(8,128)} %bitcast.110), kind=kCustom, calls=%fused_computation.2.clone.1 | custom fusion | flops 1048576 | bytes 12583424 | tf_op jit(solution)/shard_map/while/body/eval_jaxpr/scatter-add | solution.py:101
  368.9 20.2 %scatter_fusion.1 = f32[64,64,128]{2,1,0:T(8,128)} fusion(f32[64,64,128]{2,1,0:T(8,128)} %get-tuple-element.222, s32[128]{0:T(128)S(1)} %reshape.204, f32[128,64,128]{2,1,0:T(8,128)} %bitcast.109), kind=kCustom, calls=%fused_computation.3.clone.1 | custom fusion | flops 1048576 | bytes 12583424 | tf_op jit(solution)/shard_map/while/body/eval_jaxpr/scatter-add | solution.py:101
  394.6 4.9 fusion.64
  414.6 20.0 %scatter_fusion = f32[64,64,128]{2,1,0:T(8,128)} fusion(f32[64,64,128]{2,1,0:T(8,128)} %get-tuple-element.221, s32[128]{0:T(128)S(1)} %reshape.204, f32[128,64,128]{2,1,0:T(8,128)} %bitcast.110), kind=kCustom, calls=%fused_computation.2.clone.1 | custom fusion | flops 1048576 | bytes 12583424 | tf_op jit(solution)/shard_map/while/body/eval_jaxpr/scatter-add | solution.py:101
  442.1 20.2 %scatter_fusion.1 = f32[64,64,128]{2,1,0:T(8,128)} fusion(f32[64,64,128]{2,1,0:T(8,128)} %get-tuple-element.222, s32[128]{0:T(128)S(1)} %reshape.204, f32[128,64,128]{2,1,0:T(8,128)} %bitcast.109), kind=kCustom, calls=%fused_computation.3.clone.1 | custom fusion | flops 1048576 | bytes 12583424 | tf_op jit(solution)/shard_map/while/body/eval_jaxpr/scatter-add | solution.py:101
  462.2 33.3 %all_to_all.75 = bf16[4096,2,128]{2,1,0:T(2,128)(2,1)} all-to-all(bf16[4096,2,128]{2,1,0:T(2,128)(2,1)} %bitcast.126), channel_id=1, replica_groups=mesh['pipe'=8,'seq'=32] {'seq'}, dimensions={0} | all-to-all | bytes 4194304 | tf_op jit(solution)/shard_map/all_to_all | solution.py:109
  495.5 32.3 %all_to_all.76 = f32[4096,1,128]{2,1,0:T(1,128)} all-to-all(f32[4096,1,128]{2,1,0:T(1,128)S(1)} %bitcast.111), channel_id=1, replica_groups=mesh['pipe'=8,'seq'=32] {'seq'}, dimensions={0} | all-to-all | bytes 4194304 | tf_op jit(solution)/shard_map/all_to_all | solution.py:111
  527.8 5.1 all-to-all-start.4
  546.9 14.0 %all-to-all-done.4 = f32[4096,1,128]{2,1,0:T(1,128)S(1)} async-done(((f32[4096,1,128]{2,1,0:T(1,128)}), f32[4096,1,128]{2,1,0:T(1,128)S(1)}, u32[]{:S(2)}, u32[]{:S(2)}) %all-to-all-start.4) | async-done | bytes 2097184 | tf_op jit(solution)/shard_map/all_to_all | solution.py:114
  563.6 34.0 %collective-permute-done.1 = bf16[1,128,1024]{1,2,0:T(8,128)(2,1)S(1)} collective-permute-done((bf16[1,128,1024]{1,2,0:T(8,128)(2,1)S(1)}, bf16[1,128,1024]{1,2,0:T(8,128)(2,1)S(1)}, u32[]{:S(2)}, u32[]{:S(2)}) %collective-permute-start.1) | collective-permute-done | bytes 262176 | tf_op jit(solution)/shard_map/ppermute | solution.py:15
  (158 shorter events, 158.8 us)
Async XLA Ops:
  7.2 101.2 %all-gather.5.cloned.1.call-start = ((), (), s32[]{:S(2)}) async-start(), calls=%async_computation.5 | async-start | bytes 8650752 | tf_op jit(solution)/shard_map/all_gather | solution.py:76
  7.9 156.0 %all-gather.7.cloned.1.call-start = ((), (), s32[]{:S(2)}) async-start(), calls=%async_computation.6 | async-start | bytes 8650752 | tf_op jit(solution)/shard_map/all_gather | solution.py:77
  12.7 39.2 %all-to-all-start = ((bf16[128,64,128]{0,2,1:T(8,128)(2,1)}), bf16[128,64,128]{0,2,1:T(8,128)(2,1)S(1)}, u32[]{:S(2)}, u32[]{:S(2)}) async-start(bf16[128,64,128]{0,2,1:T(8,128)(2,1)} %bitcast.124), calls=%async_computation | async-start | bytes 4194304 | tf_op jit(solution)/shard_map/all_to_all | solution.py:72
  51.9 6.6 %copy-start.6 = (s32[64,3]{0,1:T(4,128)S(1)}, s32[64,3]{0,1:T(4,128)}, u32[]{:S(2)}) copy-start(s32[64,3]{0,1:T(4,128)} %param.15) | copy-start | bytes 2308
  51.9 6.6 %copy-start.7 = (s32[64,3]{0,1:T(4,128)S(1)}, s32[64,3]{0,1:T(4,128)}, u32[]{:S(2)}) copy-start(s32[64,3]{0,1:T(4,128)} %param.13) | copy-start | bytes 2308
  51.9 6.6 %copy-start.8 = (s32[64,2]{0,1:T(2,128)S(1)}, s32[64,2]{0,1:T(2,128)}, u32[]{:S(2)}) copy-start(s32[64,2]{0,1:T(2,128)} %param.14) | copy-start | bytes 1540
  51.9 50.2 %all-to-all-start.1 = ((bf16[128,64,128]{0,2,1:T(8,128)(2,1)}), bf16[128,64,128]{0,2,1:T(8,128)(2,1)}, u32[]{:S(2)}, u32[]{:S(2)}) async-start(bf16[128,64,128]{0,2,1:T(8,128)(2,1)} %bitcast.123), calls=%async_computation.1 | async-start | bytes 4194304 | tf_op jit(solution)/shard_map/all_to_all | solution.py:73
  170.5 4.1 copy-start.1
  185.1 2.9 copy-start.2
  190.7 4.2 copy-start.4
  243.7 4.1 copy-start.1
  258.4 2.9 copy-start.2
  263.9 4.2 copy-start.4
  317.0 4.1 copy-start.1
  331.6 2.9 copy-start.2
  337.2 4.2 copy-start.4
  390.2 4.1 copy-start.1
  404.8 2.9 copy-start.2
  410.4 4.2 copy-start.4
  462.2 33.3 %copy-start = (f32[64,64,128]{2,1,0:T(8,128)S(1)}, f32[64,64,128]{2,1,0:T(8,128)}, u32[]{:S(2)}) copy-start(f32[64,64,128]{2,1,0:T(8,128)} %get-tuple-element.58) | copy-start | bytes 6291460
  527.8 33.2 %all-to-all-start.4 = ((f32[4096,1,128]{2,1,0:T(1,128)}), f32[4096,1,128]{2,1,0:T(1,128)S(1)}, u32[]{:S(2)}, u32[]{:S(2)}) async-start(f32[4096,1,128]{2,1,0:T(1,128)} %bitcast.30), calls=%async_computation.4 | async-start | bytes 4194304 | tf_op jit(solution)/shard_map/all_to_all | solution.py:114
  540.2 63.0 %collective-permute-start = (bf16[1,128,8192]{1,2,0:T(8,128)(2,1)}, bf16[1,128,8192]{1,2,0:T(8,128)(2,1)}, u32[]{:S(2)}, u32[]{:S(2)}) collective-permute-start(bf16[1,128,8192]{1,2,0:T(8,128)(2,1)} %bitcast.127), channel_id=1, source_target_pairs={{32,0},{64,32},{96,64},{128,96},{160,128},{192,160},{224,192},{33,... | collective-permute-start | bytes 6291464 | tf_op jit(solution)/shard_map/ppermute | solution.py:15
  544.5 53.1 %collective-permute-start.1 = (bf16[1,128,1024]{1,2,0:T(8,128)(2,1)S(1)}, bf16[1,128,1024]{1,2,0:T(8,128)(2,1)S(1)}, u32[]{:S(2)}, u32[]{:S(2)}) collective-permute-start(bf16[1,128,1024]{1,2,0:T(8,128)(2,1)S(1)} %bitcast.129), channel_id=1, source_target_pairs={{32,0},{64,32},{96,64},{128,96},{160,128},{192,160},{224,192},{33,... | collective-permute-start | bytes 786440 | tf_op jit(solution)/shard_map/ppermute | solution.py:15
  561.3 41.1 %collective-permute-start.2 = (bf16[1,128,1024]{1,2,0:T(8,128)(2,1)S(1)}, bf16[1,128,1024]{1,2,0:T(8,128)(2,1)S(1)}, u32[]{:S(2)}, u32[]{:S(2)}) collective-permute-start(bf16[1,128,1024]{1,2,0:T(8,128)(2,1)S(1)} %bitcast.130), channel_id=1, source_target_pairs={{32,0},{64,32},{96,64},{128,96},{160,128},{192,160},{224,192},{33,... | collective-permute-start | bytes 786440 | tf_op jit(solution)/shard_map/ppermute | solution.py:15
  (8 other events, 17.5 us)
Sparse Core Ops, SparseCore 0:
  10.5 92.7 all-gather.4
  105.9 57.9 all-gather.6
where the time goes:
time: 618 us; the launch traced here: 614 us
  other arithmetic  185 us (30%)
  waiting for transfers between devices  175 us (28%)
  matrix products  83.6 us (14%)
  blocking collectives  65.6 us (11%)
  local copies, waits for them, and re-layouts  63.9 us (10%)
  starting transfers between devices  26.4 us (4%)
  between operations  14.2 us (2%)
    scatter-add x4, other arithmetic, step(): dv_total.at[list_part].add(dv_slots)  80.7 us
    scatter-add x4, other arithmetic, step(): dk_total.at[list_part].add(dk_slots)  80.1 us
    all_gather x1, waiting for transfers between devices, body(): lax.all_gather(values[0], 'seq', axis=0, tiled=True)  54.3 us
    all_to_all x1, waiting for transfers between devices, body(): lax.all_to_all(g_local, 'seq', split_axis=1, concat_axis=0, tiled=True)  39.5 us
    ppermute x3, waiting for transfers between devices, from_behind(): return lax.ppermute(block, axis, route)  37.9 us
    all_to_all x1, blocking collectives, body(): lax.all_to_all(dq_heads, 'seq', split_axis=0, concat_axis=1, tiled=True)  33.3 us
    all_to_all x1, blocking collectives, body(): lax.all_to_all(dk_total.reshape(seqlen, 1, HD), 'seq', split_axis=0, conc...  32.3 us
    all_to_all x1, waiting for transfers between devices, body(): lax.all_to_all(q_local, 'seq', split_axis=1, concat_axis=0, tiled=True)  27.5 us
  transfers between devices with their start and end apart: 8, of which 6 were waited for; matrix products, arithmetic and copies ran while one was open for 5% of the time, Pallas kernels for 0%

commit v1 on v0

v1 whole, which is shorter than its diff:
```python
import functools

import jax
import jax.numpy as jnp
from jax import lax
from jax.experimental import pallas as pl
from jax.experimental.pallas import tpu as pltpu
from jax.sharding import PartitionSpec as P

HEADS = 64
KV = 8
HD = 128
BLOCK = 64
INTERPRET = False


def from_behind(block, axis, distance):
    devices = range(lax.axis_size(axis))
    route = [(i - distance, i) for i in devices if i - distance in devices]
    return lax.ppermute(block, axis, route)


def block_lists(window_blocks, global_blocks, random_blocks):
    listed = jnp.concatenate([window_blocks, global_blocks, random_blocks], axis=1)
    width = listed.shape[1]
    same = listed[:, :, None] == listed[:, None, :]
    earlier = jnp.arange(width)[None, :] < jnp.arange(width)[:, None]
    repeated = jnp.any(jnp.logical_and(same, earlier[None]), axis=2)
    return (listed, jnp.logical_not(repeated))


def grads_kernel(slots, rows, listed_ref, live_ref, q_ref, g_ref, k_ref, v_ref,
                 dq_ref, dkv_ref, kc_ref, vc_ref):
    b = pl.program_id(0)
    scale = HD ** (-0.5)
    width = slots * BLOCK

    @pl.when(b == 0)
    def _():
        dkv_ref[...] = jnp.zeros(dkv_ref.shape, dkv_ref.dtype)

    starts = []
    lives = []
    for j in range(slots):
        start = pl.multiple_of(listed_ref[b * slots + j] * BLOCK, BLOCK)
        starts.append(start)
        lives.append(live_ref[b * slots + j])
        kc_ref[j * BLOCK:(j + 1) * BLOCK, :] = k_ref[pl.ds(start, BLOCK), :]
        vc_ref[j * BLOCK:(j + 1) * BLOCK, :] = v_ref[pl.ds(start, BLOCK), :]

    q = q_ref[...]
    g = g_ref[...]
    kc = kc_ref[...]
    vc = vc_ref[...]
    col = lax.broadcasted_iota(jnp.int32, (1, width), 1)
    live_cols = jnp.zeros((1, width), jnp.int32)
    for j in range(slots):
        inside = jnp.logical_and(col >= j * BLOCK, col < (j + 1) * BLOCK)
        live_cols = jnp.where(inside, lives[j], live_cols)
    nt = (((1,), (1,)), ((), ()))
    tn = (((0,), (0,)), ((), ()))
    scores = lax.dot_general(q, kc, nt, preferred_element_type=jnp.float32) * scale
    scores = jnp.where(live_cols != 0, scores, -jnp.inf)
    top = jnp.max(scores, axis=-1, keepdims=True)
    expd = jnp.exp(scores - top)
    probs = expd / jnp.sum(expd, axis=-1, keepdims=True)
    probs_low = probs.astype(jnp.bfloat16)
    attn = jnp.dot(probs_low, vc, preferred_element_type=jnp.float32)
    attn = attn.astype(jnp.bfloat16).astype(jnp.float32)
    delta = jnp.sum(g.astype(jnp.float32) * attn, axis=-1, keepdims=True)
    dprobs = lax.dot_general(g, vc, nt, preferred_element_type=jnp.float32)
    ds_low = (probs * (dprobs - delta)).astype(jnp.bfloat16)
    dq = jnp.dot(ds_low, kc, preferred_element_type=jnp.float32) * scale
    dq_ref[...] = dq.astype(jnp.bfloat16)
    dk_slots = lax.dot_general(ds_low, q, tn, preferred_element_type=jnp.float32) * scale
    dv_slots = lax.dot_general(probs_low, g, tn, preferred_element_type=jnp.float32)
    for j in range(slots):
        @pl.when(lives[j] != 0)
        def _():
            window = pl.ds(starts[j], BLOCK)
            dkv_ref[0, window, :] += dk_slots[j * BLOCK:(j + 1) * BLOCK, :]
            dkv_ref[1, window, :] += dv_slots[j * BLOCK:(j + 1) * BLOCK, :]


def block_grads(q_rows, g_rows, k_head, v_head, listed, live):
    nblocks, slots = listed.shape
    seqlen = k_head.shape[0]
    rows = q_rows.shape[0] // nblocks
    kernel = functools.partial(grads_kernel, slots, rows)
    grid_spec = pltpu.PrefetchScalarGridSpec(
        num_scalar_prefetch=2,
        grid=(nblocks,),
        in_specs=[
            pl.BlockSpec((rows, HD), lambda b, *_: (b, 0)),
            pl.BlockSpec((rows, HD), lambda b, *_: (b, 0)),
            pl.BlockSpec((seqlen, HD), lambda b, *_: (0, 0)),
            pl.BlockSpec((seqlen, HD), lambda b, *_: (0, 0)),
        ],
        out_specs=[
            pl.BlockSpec((rows, HD), lambda b, *_: (b, 0)),
            pl.BlockSpec((2, seqlen, HD), lambda b, *_: (0, 0, 0)),
        ],
        scratch_shapes=[
            pltpu.VMEM((slots * BLOCK, HD), jnp.bfloat16),
            pltpu.VMEM((slots * BLOCK, HD), jnp.bfloat16),
        ],
    )
    return pl.pallas_call(
        kernel,
        grid_spec=grid_spec,
        out_shape=[
            jax.ShapeDtypeStruct(q_rows.shape, jnp.bfloat16),
            jax.ShapeDtypeStruct((2, seqlen, HD), jnp.float32),
        ],
        compiler_params=pltpu.CompilerParams(dimension_semantics=("arbitrary",)),
        interpret=INTERPRET,
    )(listed.reshape(-1), live.reshape(-1).astype(jnp.int32), q_rows, g_rows, k_head, v_head)


def body(queries, keys, values, out_grad, window_blocks, global_blocks, random_blocks):
    lanes = lax.axis_size("seq")
    tok = queries.shape[1]
    repeat = lanes // KV
    q_local = queries[0].reshape(tok, HEADS, HD)
    g_local = out_grad[0].reshape(tok, HEADS, HD)
    q_heads, g_heads = (
        lax.all_to_all(q_local, "seq", split_axis=1, concat_axis=0, tiled=True),
        lax.all_to_all(g_local, "seq", split_axis=1, concat_axis=0, tiled=True),
    )
    k_rep = jnp.repeat(keys[0].reshape(tok, KV, HD), repeat, axis=1)
    v_rep = jnp.repeat(values[0].reshape(tok, KV, HD), repeat, axis=1)
    kv_send = jnp.stack([k_rep, v_rep], axis=2)
    kv_head = lax.all_to_all(kv_send, "seq", split_axis=1, concat_axis=0, tiled=True)
    k_head = kv_head[:, 0, 0, :]
    v_head = kv_head[:, 0, 1, :]
    seqlen = q_heads.shape[0]
    per_device = q_heads.shape[1]
    listed, live = block_lists(window_blocks, global_blocks, random_blocks)
    q_rows = q_heads.reshape(seqlen * per_device, HD)
    g_rows = g_heads.reshape(seqlen * per_device, HD)
    dq_rows, dkv = block_grads(q_rows, g_rows, k_head, v_head, listed, live)
    dq_heads = dq_rows.reshape(seqlen, per_device, HD)
    dq_tokens = lax.all_to_all(dq_heads, "seq", split_axis=0, concat_axis=1, tiled=True)
    dkv_parts = lax.all_to_all(dkv, "seq", split_axis=1, concat_axis=0, tiled=True)
    dkv_sum = jnp.sum(dkv_parts.reshape(KV, repeat, 2, tok, HD), axis=1).astype(jnp.bfloat16)
    dk_tokens = dkv_sum[:, 0].transpose(1, 0, 2)
    dv_tokens = dkv_sum[:, 1].transpose(1, 0, 2)
    dq_flat = dq_tokens.reshape(1, tok, HEADS * HD)
    dk_flat = dk_tokens.reshape(1, tok, KV * HD)
    dv_flat = dv_tokens.reshape(1, tok, KV * HD)
    return from_behind((dq_flat, dk_flat, dv_flat), "pipe", -1)


def solution(mesh):
    in_specs = (
        P("pipe", "seq", None),
        P("pipe", "seq", None),
        P("pipe", "seq", None),
        P("pipe", "seq", None),
        P(),
        P(),
        P(),
    )
    out_specs = (P("pipe", "seq", None), P("pipe", "seq", None), P("pipe", "seq", None))
    return jax.shard_map(body, mesh=mesh, in_specs=in_specs, out_specs=out_specs, check_vma=False)
```

time: 618 us -> 301 us (0.49)
  other arithmetic: 185 us -> 6.65 us
  matrix products: 83.6 us -> 0 us
  Pallas kernels: 0 us -> 66.4 us
  blocking collectives: 65.6 us -> 0 us
  waiting for transfers between devices: 175 us -> 137 us
  local copies, waits for them, and re-layouts: 63.9 us -> 48.1 us
  starting transfers between devices: 26.4 us -> 40.4 us
  between operations: 14.2 us -> 0.83 us
    scatter-add x8 -> x0, other arithmetic: 161 us -> none  [the longest x4 80.7 us: step(): dv_total.at[list_part].add(dv_slots)]
    dot_general x24 -> x0, matrix products: 83.6 us -> none  [the longest x4 16.7 us: block_grads(): jnp.einsum('grs,grd->gsd', ds_low, q_rows, preferred_element_type=jnp.flo...]
    all_to_all x1 -> x3, waiting for transfers between devices: 14 us -> 84.2 us  [the longest x1 41.1 us: body(): lax.all_to_all(dkv, 'seq', split_axis=1, concat_axis=0, tiled=True)]
    pallas_call x0 -> x1, Pallas kernels: none -> 66.4 us  [block_grads(): pl.pallas_call(kernel, grid_spec=grid_spec, out_shape=[jax.ShapeDtypeStru...]
    all_to_all x2 -> x0, blocking collectives: 65.6 us -> none  [the longest x1 33.3 us: body(): lax.all_to_all(dq_heads, 'seq', split_axis=0, concat_axis=1, tiled=True)]
    all_gather x2 -> x0, waiting for transfers between devices: 54.3 us -> none  [the longest x1 54.3 us: body(): lax.all_gather(values[0], 'seq', axis=0, tiled=True)]
    ppermute x3, waiting for transfers between devices: 37.9 us -> 11.8 us  [from_behind(): return lax.ppermute(block, axis, route)]
    all_to_all x1, waiting for transfers between devices: 39.5 us -> 17.1 us  [body(): lax.all_to_all(g_local, 'seq', split_axis=1, concat_axis=0, tiled=True)]
  transfers between devices with their start and end apart: 8 -> 8, of which waited for: 6 -> 7; matrix products, arithmetic and copies ran while one was open for 5% -> 14% of each run, Pallas kernels for 0% -> 0%
where the time goes in v1:
time: 301 us; the launch traced here: 300 us
  waiting for transfers between devices  137 us (46%)
  Pallas kernels  66.4 us (22%)
  local copies, waits for them, and re-layouts  48.1 us (16%)
  starting transfers between devices  40.4 us (13%)
  other arithmetic  6.65 us (2%)
    pallas_call x1, Pallas kernels, block_grads(): pl.pallas_call(kernel, grid_spec=grid_spec, out_shape=[jax.ShapeDtypeStru...  66.4 us
    all_to_all x1, waiting for transfers between devices, body(): lax.all_to_all(dkv, 'seq', split_axis=1, concat_axis=0, tiled=True)  41.1 us
    all_to_all x1, waiting for transfers between devices, body(): lax.all_to_all(q_local, 'seq', split_axis=1, concat_axis=0, tiled=True)  24 us
    all_to_all x1, waiting for transfers between devices, body(): lax.all_to_all(kv_send, 'seq', split_axis=1, concat_axis=0, tiled=True)  23.8 us
    all_to_all x1, waiting for transfers between devices, body(): lax.all_to_all(dq_heads, 'seq', split_axis=0, concat_axis=1, tiled=True)  19.2 us
    all_to_all x1, waiting for transfers between devices, body(): lax.all_to_all(g_local, 'seq', split_axis=1, concat_axis=0, tiled=True)  17.1 us
    unnamed x15, local copies, waits for them, and re-layouts  13.2 us
    ppermute x3, waiting for transfers between devices, from_behind(): return lax.ppermute(block, axis, route)  11.8 us
  transfers between devices with their start and end apart: 8, of which 7 were waited for; matrix products, arithmetic and copies ran while one was open for 14% of the time, Pallas kernels for 0%

profile of v1, /device:TPU:98, one launch (start us, length us, event | category | flops | bytes accessed | tf_op | source)
XLA Modules:
  0.0 299.6 jit_solution(617145214445097860)
XLA Ops:
  4.7 7.6 %all-to-all-start.2 = ((bf16[128,32,2,128]{3,0,2,1:T(8,128)(2,1)}), bf16[128,32,2,128]{3,0,2,1:T(8,128)(2,1)S(1)}, u32[]{:S(2)}, u32[]{:S(2)}) async-start(bf16[128,32,2,128]{3,0,2,1:T(8,128)(2,1)} %pad_maximum_fusion), calls=%async_computation.2 | async-start | bytes 4194304 | tf_op jit(solution)/shard_map/all_to_all | solution.py:133
  12.3 4.1 %copy.71 = bf16[1,128,8192]{1,2,0:T(8,128)(2,1)} copy(bf16[1,128,8192]{2,1,0:T(8,128)(2,1)} %param.7) | data formatting | bytes 4194304 | tf_op args[0]
  16.4 23.8 %all-to-all-done.2 = bf16[128,32,2,128]{3,0,2,1:T(8,128)(2,1)S(1)} async-done(((bf16[128,32,2,128]{3,0,2,1:T(8,128)(2,1)}), bf16[128,32,2,128]{3,0,2,1:T(8,128)(2,1)S(1)}, u32[]{:S(2)}, u32[]{:S(2)}) %all-to-all-start.2) | async-done | bytes 2097184 | tf_op jit(solution)/shard_map/all_to_all | solution.py:133
  40.3 6.7 %all-to-all-start = ((bf16[128,64,128]{0,2,1:T(8,128)(2,1)}), bf16[128,64,128]{0,2,1:T(8,128)(2,1)}, u32[]{:S(2)}, u32[]{:S(2)}) async-start(bf16[128,64,128]{0,2,1:T(8,128)(2,1)} %bitcast.51), calls=%async_computation | async-start | bytes 4194304 | tf_op jit(solution)/shard_map/all_to_all | solution.py:127
  47.0 4.1 %copy.74 = bf16[1,128,8192]{1,2,0:T(8,128)(2,1)} copy(bf16[1,128,8192]{2,1,0:T(8,128)(2,1)} %param.10) | data formatting | bytes 4194304 | tf_op args[3]
  51.1 24.0 %all-to-all-done = bf16[128,64,128]{0,2,1:T(8,128)(2,1)} async-done(((bf16[128,64,128]{0,2,1:T(8,128)(2,1)}), bf16[128,64,128]{0,2,1:T(8,128)(2,1)}, u32[]{:S(2)}, u32[]{:S(2)}) %all-to-all-start) | async-done | bytes 2097184 | tf_op jit(solution)/shard_map/all_to_all | solution.py:127
  75.1 6.9 %all-to-all-start.1 = ((bf16[128,64,128]{0,2,1:T(8,128)(2,1)}), bf16[128,64,128]{0,2,1:T(8,128)(2,1)}, u32[]{:S(2)}, u32[]{:S(2)}) async-start(bf16[128,64,128]{0,2,1:T(8,128)(2,1)} %bitcast.49), calls=%async_computation.1 | async-start | bytes 4194304 | tf_op jit(solution)/shard_map/all_to_all | solution.py:128
  85.1 6.3 %copy.73 = bf16[32,128,2,128]{3,2,1,0:T(2,128)(2,1)} copy(bf16[32,128,2,128]{1,3,2,0:T(8,128)(2,1)} %bitcast.3) | data formatting | bytes 4194304 | tf_op jit(solution)/shard_map/all_to_all | solution.py:127
  92.9 17.1 %all-to-all-done.1 = bf16[128,64,128]{0,2,1:T(8,128)(2,1)} async-done(((bf16[128,64,128]{0,2,1:T(8,128)(2,1)}), bf16[128,64,128]{0,2,1:T(8,128)(2,1)}, u32[]{:S(2)}, u32[]{:S(2)}) %all-to-all-start.1) | async-done | bytes 2097184 | tf_op jit(solution)/shard_map/all_to_all | solution.py:128
  110.1 6.2 %copy.76 = bf16[32,128,2,128]{3,2,1,0:T(2,128)(2,1)} copy(bf16[32,128,2,128]{1,3,2,0:T(8,128)(2,1)} %bitcast.8) | data formatting | bytes 4194304 | tf_op jit(solution)/shard_map/all_to_all | solution.py:128
  116.2 66.4 %shard_map.94 = (bf16[8192,128]{1,0:T(8,128)(2,1)}, f32[2,4096,128]{2,1,0:T(8,128)}) custom-call(s32[512]{0:T(512)} %reshape.53.listed_ref, s32[512]{0:T(512)} %reshape.61.live_ref, bf16[8192,128]{1,0:T(8,128)(2,1)} %bitcast.54, bf16[8192,128]{1,0:T(8,128)(2,1)} %bitcast.55, bf16[4096,128]{1,0:T(8,128)(2,1)} %get-tuple-element.14.k_ref, ...), custom_call_target="tpu_custom_call" | custom-call | tf_op jit(solution)/shard_map/pallas_call | solution.py:108
  182.7 6.1 %all-to-all-start.3 = ((bf16[4096,2,128]{2,1,0:T(2,128)(2,1)}), bf16[4096,2,128]{2,1,0:T(2,128)(2,1)S(1)}, u32[]{:S(2)}, u32[]{:S(2)}) async-start(bf16[4096,2,128]{2,1,0:T(2,128)(2,1)} %bitcast.58), calls=%async_computation.3 | async-start | bytes 4194304 | tf_op jit(solution)/shard_map/all_to_all | solution.py:143
  188.7 8.8 %copy.81 = f32[2,4096,128]{2,0,1:T(2,128)} copy(f32[2,4096,128]{2,1,0:T(8,128)} %get-tuple-element.6) | data formatting | bytes 8388608 | tf_op jit(solution)/shard_map/pallas_call | solution.py:108
  197.5 19.2 %all-to-all-done.3 = bf16[4096,2,128]{2,1,0:T(2,128)(2,1)S(1)} async-done(((bf16[4096,2,128]{2,1,0:T(2,128)(2,1)}), bf16[4096,2,128]{2,1,0:T(2,128)(2,1)S(1)}, u32[]{:S(2)}, u32[]{:S(2)}) %all-to-all-start.3) | async-done | bytes 2097184 | tf_op jit(solution)/shard_map/all_to_all | solution.py:143
  216.8 6.9 %all-to-all-start.4 = ((f32[2,4096,128]{2,0,1:T(2,128)}), f32[2,4096,128]{2,0,1:T(2,128)}, u32[]{:S(2)}, u32[]{:S(2)}) async-start(f32[2,4096,128]{2,0,1:T(2,128)} %copy.81), calls=%async_computation.4 | async-start | bytes 8388608 | tf_op jit(solution)/shard_map/all_to_all | solution.py:144
  223.6 3.7 %copy.95 = bf16[32,128,2,128]{3,2,0,1:T(2,128)(2,1)} copy(bf16[32,128,2,128]{3,2,1,0:T(2,128)(2,1)S(1)} %bitcast.50) | data formatting | bytes 4194304 | tf_op jit(solution)/shard_map/all_to_all | solution.py:143
  227.3 4.5 %reshape.57 = bf16[1,128,8192]{2,1,0:T(8,128)(2,1)} reshape(bf16[128,32,2,128]{3,2,1,0:T(2,128)(2,1)} %bitcast.53) | data formatting | bytes 4194304 | tf_op jit(solution)/shard_map/reshape | solution.py:148
  231.8 2.2 collective-permute-start
  234.0 41.1 %all-to-all-done.4 = f32[2,4096,128]{2,0,1:T(2,128)} async-done(((f32[2,4096,128]{2,0,1:T(2,128)}), f32[2,4096,128]{2,0,1:T(2,128)}, u32[]{:S(2)}, u32[]{:S(2)}) %all-to-all-start.4) | async-done | bytes 4194336 | tf_op jit(solution)/shard_map/all_to_all | solution.py:144
  275.2 5.0 %reduce = bf16[8,2,128,128]{3,1,2,0:T(2,128)(2,1)S(1)} reduce(f32[8,4,2,128,128]{4,2,3,1,0:T(2,128)} %bitcast.23, f32[]{:T(128)} %constant.1.clone.1), dimensions={1}, to_apply=%region_1.0 | reduce | flops 786432 | bytes 4718596
  280.7 2.0 collective-permute-start.1
  282.7 2.0 collective-permute-start.2
  284.8 8.2 %collective-permute-done.1 = bf16[1,128,1024]{1,2,0:T(8,128)(2,1)S(1)} collective-permute-done((bf16[1,128,1024]{1,2,0:T(8,128)(2,1)S(1)}, bf16[1,128,1024]{1,2,0:T(8,128)(2,1)S(1)}, u32[]{:S(2)}, u32[]{:S(2)}) %collective-permute-start.1) | collective-permute-done | bytes 262176 | tf_op jit(solution)/shard_map/ppermute | solution.py:20
  293.8 3.6 %collective-permute-done.2 = bf16[1,128,1024]{1,2,0:T(8,128)(2,1)S(1)} collective-permute-done((bf16[1,128,1024]{1,2,0:T(8,128)(2,1)S(1)}, bf16[1,128,1024]{1,2,0:T(8,128)(2,1)S(1)}, u32[]{:S(2)}, u32[]{:S(2)}) %collective-permute-start.2) | collective-permute-done | bytes 262176 | tf_op jit(solution)/shard_map/ppermute | solution.py:20
  (33 shorter events, 12.2 us)
Async XLA Ops:
  4.7 35.5 %all-to-all-start.2 = ((bf16[128,32,2,128]{3,0,2,1:T(8,128)(2,1)}), bf16[128,32,2,128]{3,0,2,1:T(8,128)(2,1)S(1)}, u32[]{:S(2)}, u32[]{:S(2)}) async-start(bf16[128,32,2,128]{3,0,2,1:T(8,128)(2,1)} %pad_maximum_fusion), calls=%async_computation.2 | async-start | bytes 4194304 | tf_op jit(solution)/shard_map/all_to_all | solution.py:133
  40.3 34.8 %all-to-all-start = ((bf16[128,64,128]{0,2,1:T(8,128)(2,1)}), bf16[128,64,128]{0,2,1:T(8,128)(2,1)}, u32[]{:S(2)}, u32[]{:S(2)}) async-start(bf16[128,64,128]{0,2,1:T(8,128)(2,1)} %bitcast.51), calls=%async_computation | async-start | bytes 4194304 | tf_op jit(solution)/shard_map/all_to_all | solution.py:127
  75.1 6.9 %copy-start.1 = (s32[64,3]{0,1:T(4,128)S(1)}, s32[64,3]{0,1:T(4,128)}, u32[]{:S(2)}) copy-start(s32[64,3]{0,1:T(4,128)} %param.13) | copy-start | bytes 2308
  75.1 6.9 %copy-start.2 = (s32[64,3]{0,1:T(4,128)S(1)}, s32[64,3]{0,1:T(4,128)}, u32[]{:S(2)}) copy-start(s32[64,3]{0,1:T(4,128)} %param.11) | copy-start | bytes 2308
  75.1 6.9 %copy-start.3 = (s32[64,2]{0,1:T(2,128)S(1)}, s32[64,2]{0,1:T(2,128)}, u32[]{:S(2)}) copy-start(s32[64,2]{0,1:T(2,128)} %param.12) | copy-start | bytes 1540
  75.1 35.0 %all-to-all-start.1 = ((bf16[128,64,128]{0,2,1:T(8,128)(2,1)}), bf16[128,64,128]{0,2,1:T(8,128)(2,1)}, u32[]{:S(2)}, u32[]{:S(2)}) async-start(bf16[128,64,128]{0,2,1:T(8,128)(2,1)} %bitcast.49), calls=%async_computation.1 | async-start | bytes 4194304 | tf_op jit(solution)/shard_map/all_to_all | solution.py:128
  85.1 6.3 %copy-start = (bf16[32,128,1,2,128]{4,1,0,3,2:T(8,128)(2,1)S(1)}, bf16[32,128,1,2,128]{4,1,0,3,2:T(8,128)(2,1)}, u32[]{:S(2)}) copy-start(bf16[32,128,1,2,128]{4,1,0,3,2:T(8,128)(2,1)} %copy.79) | copy-start | bytes 6291460
  182.7 34.1 %all-to-all-start.3 = ((bf16[4096,2,128]{2,1,0:T(2,128)(2,1)}), bf16[4096,2,128]{2,1,0:T(2,128)(2,1)S(1)}, u32[]{:S(2)}, u32[]{:S(2)}) async-start(bf16[4096,2,128]{2,1,0:T(2,128)(2,1)} %bitcast.58), calls=%async_computation.3 | async-start | bytes 4194304 | tf_op jit(solution)/shard_map/all_to_all | solution.py:143
  216.8 58.4 %all-to-all-start.4 = ((f32[2,4096,128]{2,0,1:T(2,128)}), f32[2,4096,128]{2,0,1:T(2,128)}, u32[]{:S(2)}, u32[]{:S(2)}) async-start(f32[2,4096,128]{2,0,1:T(2,128)} %copy.81), calls=%async_computation.4 | async-start | bytes 8388608 | tf_op jit(solution)/shard_map/all_to_all | solution.py:144
  231.8 52.9 %collective-permute-start = (bf16[1,128,8192]{2,1,0:T(8,128)(2,1)}, bf16[1,128,8192]{2,1,0:T(8,128)(2,1)S(1)}, u32[]{:S(2)}, u32[]{:S(2)}) collective-permute-start(bf16[1,128,8192]{2,1,0:T(8,128)(2,1)} %reshape.57), channel_id=1, source_target_pairs={{32,0},{64,32},{96,64},{128,96},{160,128},{192,160},{224,192},{33,... | collective-permute-start | bytes 6291464 | tf_op jit(solution)/shard_map/ppermute | solution.py:20
  280.7 12.3 %collective-permute-start.1 = (bf16[1,128,1024]{1,2,0:T(8,128)(2,1)S(1)}, bf16[1,128,1024]{1,2,0:T(8,128)(2,1)S(1)}, u32[]{:S(2)}, u32[]{:S(2)}) collective-permute-start(bf16[1,128,1024]{1,2,0:T(8,128)(2,1)S(1)} %bitcast.64), channel_id=1, source_target_pairs={{32,0},{64,32},{96,64},{128,96},{160,128},{192,160},{224,192},{33,... | collective-permute-start | bytes 786440 | tf_op jit(solution)/shard_map/ppermute | solution.py:20
  282.7 14.7 %collective-permute-start.2 = (bf16[1,128,1024]{1,2,0:T(8,128)(2,1)S(1)}, bf16[1,128,1024]{1,2,0:T(8,128)(2,1)S(1)}, u32[]{:S(2)}, u32[]{:S(2)}) collective-permute-start(bf16[1,128,1024]{1,2,0:T(8,128)(2,1)S(1)} %bitcast.63), channel_id=1, source_target_pairs={{32,0},{64,32},{96,64},{128,96},{160,128},{192,160},{224,192},{33,... | collective-permute-start | bytes 786440 | tf_op jit(solution)/shard_map/ppermute | solution.py:20

commit v2 on v1

--- a/solution.py
+++ b/solution.py
@@ -29,15 +29,21 @@
     return (listed, jnp.logical_not(repeated))
 
 
-def grads_kernel(slots, rows, listed_ref, live_ref, q_ref, g_ref, k_ref, v_ref,
-                 dq_ref, dkv_ref, kc_ref, vc_ref):
+def grads_kernel(slots, chained, listed_ref, live_ref, q_ref, g_ref, k_ref, v_ref, *refs):
+    if chained:
+        dkv_in_ref, dq_ref, dkv_ref, kc_ref, vc_ref = refs
+    else:
+        dq_ref, dkv_ref, kc_ref, vc_ref = refs
     b = pl.program_id(0)
     scale = HD ** (-0.5)
     width = slots * BLOCK
 
     @pl.when(b == 0)
     def _():
-        dkv_ref[...] = jnp.zeros(dkv_ref.shape, dkv_ref.dtype)
+        if chained:
+            dkv_ref[...] = dkv_in_ref[...]
+        else:
+            dkv_ref[...] = jnp.zeros(dkv_ref.shape, dkv_ref.dtype)
 
     starts = []
     lives = []
@@ -82,20 +88,27 @@
             dkv_ref[1, window, :] += dv_slots[j * BLOCK:(j + 1) * BLOCK, :]
 
 
-def block_grads(q_rows, g_rows, k_head, v_head, listed, live):
+def block_grads(qg_rows, kv_head, listed, live, dkv_in=None):
     nblocks, slots = listed.shape
-    seqlen = k_head.shape[0]
-    rows = q_rows.shape[0] // nblocks
-    kernel = functools.partial(grads_kernel, slots, rows)
+    seqlen = kv_head.shape[1]
+    rows = qg_rows.shape[1] // nblocks
+    chained = dkv_in is not None
+    width = slots * BLOCK
+    kernel = functools.partial(grads_kernel, slots, chained)
+    in_specs = [
+        pl.BlockSpec((None, rows, HD), lambda b, *_: (0, b, 0)),
+        pl.BlockSpec((None, rows, HD), lambda b, *_: (1, b, 0)),
+        pl.BlockSpec((None, seqlen, HD), lambda b, *_: (0, 0, 0)),
+        pl.BlockSpec((None, seqlen, HD), lambda b, *_: (1, 0, 0)),
+    ]
+    operands = [qg_rows, qg_rows, kv_head, kv_head]
+    if chained:
+        in_specs.append(pl.BlockSpec((2, seqlen, HD), lambda b, *_: (0, 0, 0)))
+        operands.append(dkv_in)
     grid_spec = pltpu.PrefetchScalarGridSpec(
         num_scalar_prefetch=2,
         grid=(nblocks,),
-        in_specs=[
-            pl.BlockSpec((rows, HD), lambda b, *_: (b, 0)),
-            pl.BlockSpec((rows, HD), lambda b, *_: (b, 0)),
-            pl.BlockSpec((seqlen, HD), lambda b, *_: (0, 0)),
-            pl.BlockSpec((seqlen, HD), lambda b, *_: (0, 0)),
-        ],
+        in_specs=in_specs,
         out_specs=[
             pl.BlockSpec((rows, HD), lambda b, *_: (b, 0)),
             pl.BlockSpec((2, seqlen, HD), lambda b, *_: (0, 0, 0)),
@@ -109,42 +122,49 @@
         kernel,
         grid_spec=grid_spec,
         out_shape=[
-            jax.ShapeDtypeStruct(q_rows.shape, jnp.bfloat16),
+            jax.ShapeDtypeStruct(qg_rows.shape[1:], jnp.bfloat16),
             jax.ShapeDtypeStruct((2, seqlen, HD), jnp.float32),
         ],
         compiler_params=pltpu.CompilerParams(dimension_semantics=("arbitrary",)),
+        cost_estimate=pl.CostEstimate(
+            flops=12 * nblocks * rows * width * HD,
+            transcendentals=nblocks * rows * width,
+            bytes_accessed=4 * qg_rows.size + 4 * kv_head.size + 16 * seqlen * HD,
+        ),
         interpret=INTERPRET,
-    )(listed.reshape(-1), live.reshape(-1).astype(jnp.int32), q_rows, g_rows, k_head, v_head)
+    )(listed.reshape(-1), live.reshape(-1).astype(jnp.int32), *operands)
+
+
+SEQ = ("y", "xh", "xl", "core")
+NEAR = ("xl", "core")
+FAR = ("y", "xh")
 
 
 def body(queries, keys, values, out_grad, window_blocks, global_blocks, random_blocks):
-    lanes = lax.axis_size("seq")
+    lanes = lax.axis_size(SEQ)
+    near = lax.axis_size(NEAR)
+    far = lax.axis_size(FAR)
     tok = queries.shape[1]
-    repeat = lanes // KV
-    q_local = queries[0].reshape(tok, HEADS, HD)
-    g_local = out_grad[0].reshape(tok, HEADS, HD)
-    q_heads, g_heads = (
-        lax.all_to_all(q_local, "seq", split_axis=1, concat_axis=0, tiled=True),
-        lax.all_to_all(g_local, "seq", split_axis=1, concat_axis=0, tiled=True),
-    )
-    k_rep = jnp.repeat(keys[0].reshape(tok, KV, HD), repeat, axis=1)
-    v_rep = jnp.repeat(values[0].reshape(tok, KV, HD), repeat, axis=1)
-    kv_send = jnp.stack([k_rep, v_rep], axis=2)
-    kv_head = lax.all_to_all(kv_send, "seq", split_axis=1, concat_axis=0, tiled=True)
-    k_head = kv_head[:, 0, 0, :]
-    v_head = kv_head[:, 0, 1, :]
-    seqlen = q_heads.shape[0]
-    per_device = q_heads.shape[1]
+    seqlen = tok * lanes
+    per_device = HEADS // lanes
+    kv_local = jnp.stack([keys[0].reshape(tok, KV, HD), values[0].reshape(tok, KV, HD)])
+    kv_send = kv_local.transpose(2, 0, 1, 3)
+    kv_far = lax.all_to_all(kv_send, FAR, split_axis=0, concat_axis=0, tiled=True)
+    kv_all = lax.all_gather(kv_far, NEAR, axis=0, tiled=False)
+    kv_head = kv_all.transpose(2, 1, 0, 3, 4).reshape(2, seqlen, HD)
     listed, live = block_lists(window_blocks, global_blocks, random_blocks)
-    q_rows = q_heads.reshape(seqlen * per_device, HD)
-    g_rows = g_heads.reshape(seqlen * per_device, HD)
-    dq_rows, dkv = block_grads(q_rows, g_rows, k_head, v_head, listed, live)
+    qg_local = jnp.stack([queries[0].reshape(tok, HEADS, HD), out_grad[0].reshape(tok, HEADS, HD)])
+    qg_heads = lax.all_to_all(qg_local, SEQ, split_axis=2, concat_axis=1, tiled=True)
+    qg_rows = qg_heads.reshape(2, seqlen * per_device, HD)
+    dq_rows, dkv = block_grads(qg_rows, kv_head, listed, live)
     dq_heads = dq_rows.reshape(seqlen, per_device, HD)
-    dq_tokens = lax.all_to_all(dq_heads, "seq", split_axis=0, concat_axis=1, tiled=True)
-    dkv_parts = lax.all_to_all(dkv, "seq", split_axis=1, concat_axis=0, tiled=True)
-    dkv_sum = jnp.sum(dkv_parts.reshape(KV, repeat, 2, tok, HD), axis=1).astype(jnp.bfloat16)
-    dk_tokens = dkv_sum[:, 0].transpose(1, 0, 2)
-    dv_tokens = dkv_sum[:, 1].transpose(1, 0, 2)
+    dq_tokens = lax.all_to_all(dq_heads, SEQ, split_axis=0, concat_axis=1, tiled=True)
+    dkv_grouped = dkv.reshape(2, far, near, tok, HD).transpose(2, 0, 1, 3, 4)
+    dkv_part = lax.psum_scatter(dkv_grouped, NEAR, scatter_dimension=0, tiled=True)
+    dkv_low = dkv_part.reshape(2, far, tok, HD).astype(jnp.bfloat16)
+    dkv_tokens = lax.all_to_all(dkv_low, FAR, split_axis=1, concat_axis=1, tiled=True)
+    dk_tokens = dkv_tokens[0].transpose(1, 0, 2)
+    dv_tokens = dkv_tokens[1].transpose(1, 0, 2)
     dq_flat = dq_tokens.reshape(1, tok, HEADS * HD)
     dk_flat = dk_tokens.reshape(1, tok, KV * HD)
     dv_flat = dv_tokens.reshape(1, tok, KV * HD)
@@ -152,14 +172,10 @@
 
 
 def solution(mesh):
-    in_specs = (
-        P("pipe", "seq", None),
-        P("pipe", "seq", None),
-        P("pipe", "seq", None),
-        P("pipe", "seq", None),
-        P(),
-        P(),
-        P(),
-    )
-    out_specs = (P("pipe", "seq", None), P("pipe", "seq", None), P("pipe", "seq", None))
-    return jax.shard_map(body, mesh=mesh, in_specs=in_specs, out_specs=out_specs, check_vma=False)
+    pipe, lanes = mesh.devices.shape
+    fine = mesh.devices.reshape(pipe, lanes // 8, 2, 2, 2)
+    sub = jax.sharding.Mesh(fine, ("pipe",) + SEQ)
+    block = P("pipe", SEQ, None)
+    in_specs = (block, block, block, block, P(), P(), P())
+    out_specs = (block, block, block)
+    return jax.shard_map(body, mesh=sub, in_specs=in_specs, out_specs=out_specs, check_vma=False)

time: 301 us -> 348 us (1.16)
  blocking collectives: 0 us -> 92.5 us
  waiting for transfers between devices: 137 us -> 100 us
  starting transfers between devices: 40.4 us -> 25.9 us
  between operations: 0.83 us -> 14.2 us
  other arithmetic: 6.65 us -> 2.15 us
  local copies, waits for them, and re-layouts: 48.1 us -> 44.2 us
    all_to_all x5 -> x3, waiting for transfers between devices: 125 us -> 39.8 us  [the longest x1 27.3 us: body(): lax.all_to_all(dq_heads, SEQ, split_axis=0, concat_axis=1, tiled=True)]
    unnamed x0 -> x1, blocking collectives: none -> 76.8 us
    all_gather x0 -> x1, waiting for transfers between devices: none -> 49.8 us  [body(): kv_all = lax.all_gather(kv_far, NEAR, axis=0, tiled=False)]
    all_to_all x0 -> x1, blocking collectives: none -> 15.7 us  [body(): lax.all_to_all(dkv_low, FAR, split_axis=1, concat_axis=1, tiled=True)]
    all_to_all x5 -> x3, starting transfers between devices: 34.2 us -> 19.9 us  [the longest x1 8.96 us: body(): lax.all_to_all(qg_local, SEQ, split_axis=2, concat_axis=1, tiled=True)]
    pallas_call x1 -> x0, local copies, waits for them, and re-layouts: 8.79 us -> none  [block_grads(): pl.pallas_call(kernel, grid_spec=grid_spec, out_shape=[jax.ShapeDtypeStru...]
    unnamed x1 -> x0, other arithmetic: 5 us -> none
    transpose x3 -> x2, local copies, waits for them, and re-layouts: 0.4 us -> 4 us  [the longest x1 3.16 us: body(): kv_head = kv_all.transpose(2, 1, 0, 3, 4).reshape(2, seqlen, HD)]
  transfers between devices with their start and end apart: 8 -> 7, of which waited for: 7 -> 5; matrix products, arithmetic and copies ran while one was open for 14% -> 6% of each run, Pallas kernels for 0% -> 0%
where the time goes in v2:
time: 348 us; the launch traced here: 346 us
  waiting for transfers between devices  100 us (29%)
  blocking collectives  92.5 us (27%)
  Pallas kernels  66.6 us (19%)
  local copies, waits for them, and re-layouts  44.2 us (13%)
  starting transfers between devices  25.9 us (7%)
  between operations  14.2 us (4%)
    unnamed x1, blocking collectives  76.8 us
    pallas_call x1, Pallas kernels, block_grads(): pl.pallas_call(kernel, grid_spec=grid_spec, out_shape=[jax.ShapeDtypeStru...  66.6 us
    all_gather x1, waiting for transfers between devices, body(): kv_all = lax.all_gather(kv_far, NEAR, axis=0, tiled=False)  49.8 us
    all_to_all x1, waiting for transfers between devices, body(): lax.all_to_all(dq_heads, SEQ, split_axis=0, concat_axis=1, tiled=True)  27.3 us
    all_to_all x1, blocking collectives, body(): lax.all_to_all(dkv_low, FAR, split_axis=1, concat_axis=1, tiled=True)  15.7 us
    unnamed x18, local copies, waits for them, and re-layouts  15.3 us
    all_to_all x1, waiting for transfers between devices, body(): lax.all_to_all(qg_local, SEQ, split_axis=2, concat_axis=1, tiled=True)  12.5 us
    all_to_all x1, local copies, waits for them, and re-layouts, body(): lax.all_to_all(qg_local, SEQ, split_axis=2, concat_axis=1, tiled=True)  11.2 us
  transfers between devices with their start and end apart: 7, of which 5 were waited for; matrix products, arithmetic and copies ran while one was open for 6% of the time, Pallas kernels for 0%

profile of v2, /device:TPU:98, one launch (start us, length us, event | category | flops | bytes accessed | tf_op | source)
XLA Modules:
  0.0 345.9 jit_solution(11512331328675342708)
XLA Ops:
  8.3 1.1 copy.98
  10.3 6.0 %all-to-all-start.1 = ((bf16[8,2,128,128]{2,3,1,0:T(8,128)(2,1)}), bf16[8,2,128,128]{2,3,1,0:T(8,128)(2,1)S(1)}, u32[]{:S(2)}, u32[]{:S(2)}) async-start(bf16[8,2,128,128]{2,3,1,0:T(8,128)(2,1)} %copy.99), calls=%async_computation.1 | async-start | bytes 1048576 | tf_op jit(solution)/shard_map/all_to_all | solution.py:152
  16.3 3.2 copy.92
  19.6 4.1 %copy.93 = bf16[1,128,8192]{1,2,0:T(8,128)(2,1)} copy(bf16[1,128,8192]{2,1,0:T(8,128)(2,1)} %param.10) | data formatting | bytes 4194304 | tf_op args[3]
  23.6 2.0 pad_maximum_fusion
  25.6 2.3 copy.94
  27.9 9.0 %all-to-all-start = ((bf16[2,128,64,128]{1,3,0,2:T(8,128)(2,1)}), bf16[2,128,64,128]{1,3,0,2:T(8,128)(2,1)}, u32[]{:S(2)}, u32[]{:S(2)}) async-start(bf16[2,128,64,128]{1,3,0,2:T(8,128)(2,1)} %copy.94), calls=%async_computation | async-start | bytes 8388608 | tf_op jit(solution)/shard_map/all_to_all | solution.py:157
  39.7 49.8 %all-gather.3.cloned.1.call-done = bf16[32,2,128,128]{3,2,1,0:T(8,128)(2,1)} async-done(((bf16[8,2,128,128]{3,2,1,0:T(8,128)(2,1)}), bf16[32,2,128,128]{3,2,1,0:T(8,128)(2,1)}) %all-gather.3.cloned.1.call-update) | async-done | bytes 2097168 | tf_op jit(solution)/shard_map/all_gather | solution.py:153
  89.5 3.2 copy.101
  92.6 12.5 %all-to-all-done = bf16[2,128,64,128]{1,3,0,2:T(8,128)(2,1)} async-done(((bf16[2,128,64,128]{1,3,0,2:T(8,128)(2,1)}), bf16[2,128,64,128]{1,3,0,2:T(8,128)(2,1)}, u32[]{:S(2)}, u32[]{:S(2)}) %all-to-all-start) | async-done | bytes 4194336 | tf_op jit(solution)/shard_map/all_to_all | solution.py:157
  105.1 11.2 %copy.96 = bf16[2,32,128,2,128]{4,3,2,1,0:T(2,128)(2,1)} copy(bf16[2,32,128,2,128]{2,4,0,3,1:T(8,128)(2,1)} %bitcast.10) | data formatting | bytes 8388608 | tf_op jit(solution)/shard_map/all_to_all | solution.py:157
  116.3 66.6 %shard_map.94 = (bf16[8192,128]{1,0:T(8,128)(2,1)}, f32[2,4096,128]{2,1,0:T(8,128)}) custom-call(s32[512]{0:T(512)} %reshape.53.listed_ref, s32[512]{0:T(512)} %reshape.61.live_ref, bf16[2,8192,128]{2,1,0:T(8,128)(2,1)} %bitcast.46, bf16[2,8192,128]{2,1,0:T(8,128)(2,1)} %bitcast.47, bf16[2,4096,128]{2,1,0:T(8,128)(2,1)} %bitcast.50, ...), custom_call_target="tpu_custom_call" | custom-call | flops 6442450944 | bytes 20971520 | tf_op jit(solution)/shard_map/pallas_call | solution.py:121
  182.8 4.9 %all-to-all-start.2 = ((bf16[4096,2,128]{2,1,0:T(2,128)(2,1)}), bf16[4096,2,128]{2,1,0:T(2,128)(2,1)S(1)}, u32[]{:S(2)}, u32[]{:S(2)}) async-start(bf16[4096,2,128]{2,1,0:T(2,128)(2,1)} %bitcast.49), calls=%async_computation.2 | async-start | bytes 4194304 | tf_op jit(solution)/shard_map/all_to_all | solution.py:161
  188.3 27.3 %all-to-all-done.2 = bf16[4096,2,128]{2,1,0:T(2,128)(2,1)S(1)} async-done(((bf16[4096,2,128]{2,1,0:T(2,128)(2,1)}), bf16[4096,2,128]{2,1,0:T(2,128)(2,1)S(1)}, u32[]{:S(2)}, u32[]{:S(2)}) %all-to-all-start.2) | async-done | bytes 2097184 | tf_op jit(solution)/shard_map/all_to_all | solution.py:161
  215.6 3.7 %copy.114 = bf16[32,128,2,128]{3,2,0,1:T(2,128)(2,1)} copy(bf16[32,128,2,128]{3,2,1,0:T(2,128)(2,1)S(1)} %bitcast.41) | data formatting | bytes 4194304 | tf_op jit(solution)/shard_map/all_to_all | solution.py:161
  219.3 4.5 %reshape.57 = bf16[1,128,8192]{2,1,0:T(8,128)(2,1)} reshape(bf16[128,32,2,128]{3,2,1,0:T(2,128)(2,1)} %bitcast.42) | data formatting | bytes 4194304 | tf_op jit(solution)/shard_map/reshape | solution.py:168
  223.8 2.0 collective-permute-start
  225.8 76.8 %all-reduce.2 = bf16[4,2,8,128,128]{4,3,0,2,1:T(8,128)(2,1)S(1)} all-reduce(f32[4,2,8,128,128]{4,3,0,2,1:T(8,128)} %bitcast.45), channel_id=3, replica_groups=mesh['pipe'=8,'y'=4,'xh'=2,'xl'=2,'core'=2] {'xl','core'}, use_global_device_ids=true, to_apply=%region_1.0.clone | all-reduce | flops 1048576 | bytes 6291456
  303.4 15.7 %all_to_all.40 = bf16[2,8,128,128]{3,2,0,1:T(8,128)(2,1)S(1)} all-to-all(bf16[2,8,128,128]{3,2,0,1:T(8,128)(2,1)S(1)} %copy.103), channel_id=1, replica_groups=mesh['pipe'=8,'y'=4,'xh'=2,'xl'=2,'core'=2] {'y','xh'}, dimensions={1} | all-to-all | bytes 1048576 | tf_op jit(solution)/shard_map/all_to_all | solution.py:165
  319.3 2.0 collective-permute-start.1
  321.5 2.0 collective-permute-start.2
  323.6 8.1 %collective-permute-done.1 = bf16[1,128,1024]{1,2,0:T(8,128)(2,1)S(1)} collective-permute-done((bf16[1,128,1024]{1,2,0:T(8,128)(2,1)S(1)}, bf16[1,128,1024]{1,2,0:T(8,128)(2,1)S(1)}, u32[]{:S(2)}, u32[]{:S(2)}) %collective-permute-start.1) | collective-permute-done | bytes 262176 | tf_op jit(solution)/shard_map/ppermute | solution.py:20
  332.5 2.6 collective-permute-done.2
  336.0 3.1 copy.118
  (32 shorter events, 8.2 us)
Async XLA Ops:
  10.3 17.6 %all-to-all-start.1 = ((bf16[8,2,128,128]{2,3,1,0:T(8,128)(2,1)}), bf16[8,2,128,128]{2,3,1,0:T(8,128)(2,1)S(1)}, u32[]{:S(2)}, u32[]{:S(2)}) async-start(bf16[8,2,128,128]{2,3,1,0:T(8,128)(2,1)} %copy.99), calls=%async_computation.1 | async-start | bytes 1048576 | tf_op jit(solution)/shard_map/all_to_all | solution.py:152
  27.9 10.1 %copy-start = (s32[64,3]{0,1:T(4,128)S(1)}, s32[64,3]{0,1:T(4,128)}, u32[]{:S(2)}) copy-start(s32[64,3]{0,1:T(4,128)} %param.13) | copy-start | bytes 2308
  27.9 10.1 %copy-start.1 = (s32[64,3]{0,1:T(4,128)S(1)}, s32[64,3]{0,1:T(4,128)}, u32[]{:S(2)}) copy-start(s32[64,3]{0,1:T(4,128)} %param.11) | copy-start | bytes 2308
  27.9 10.1 %copy-start.2 = (s32[64,2]{0,1:T(2,128)S(1)}, s32[64,2]{0,1:T(2,128)}, u32[]{:S(2)}) copy-start(s32[64,2]{0,1:T(2,128)} %param.12) | copy-start | bytes 1540
  27.9 77.2 %all-to-all-start = ((bf16[2,128,64,128]{1,3,0,2:T(8,128)(2,1)}), bf16[2,128,64,128]{1,3,0,2:T(8,128)(2,1)}, u32[]{:S(2)}, u32[]{:S(2)}) async-start(bf16[2,128,64,128]{1,3,0,2:T(8,128)(2,1)} %copy.94), calls=%async_computation | async-start | bytes 8388608 | tf_op jit(solution)/shard_map/all_to_all | solution.py:157
  36.9 52.5 %all-gather.3.cloned.1.call-start = ((), (), s32[]{:S(2)}) async-start(), calls=%async_computation.4 | async-start | bytes 2621440 | tf_op jit(solution)/shard_map/all_gather | solution.py:153
  182.8 4.9 %copy-start.3 = (u32[256]{0:T(256)S(1)}, u32[256]{0:T(256)}, u32[]{:S(2)}) copy-start(u32[256]{0:T(256)} %constant.8) | copy-start | bytes 3076
  182.8 32.8 %all-to-all-start.2 = ((bf16[4096,2,128]{2,1,0:T(2,128)(2,1)}), bf16[4096,2,128]{2,1,0:T(2,128)(2,1)S(1)}, u32[]{:S(2)}, u32[]{:S(2)}) async-start(bf16[4096,2,128]{2,1,0:T(2,128)(2,1)} %bitcast.49), calls=%async_computation.2 | async-start | bytes 4194304 | tf_op jit(solution)/shard_map/all_to_all | solution.py:161
  223.8 112.2 %collective-permute-start = (bf16[1,128,8192]{2,1,0:T(8,128)(2,1)}, bf16[1,128,8192]{2,1,0:T(8,128)(2,1)}, u32[]{:S(2)}, u32[]{:S(2)}) collective-permute-start(bf16[1,128,8192]{2,1,0:T(8,128)(2,1)} %reshape.57), channel_id=1, source_target_pairs={{32,0},{64,32},{96,64},{128,96},{160,128},{192,160},{224,192},{33,... | collective-permute-start | bytes 6291464 | tf_op jit(solution)/shard_map/ppermute | solution.py:20
  319.3 12.3 %collective-permute-start.1 = (bf16[1,128,1024]{1,2,0:T(8,128)(2,1)S(1)}, bf16[1,128,1024]{1,2,0:T(8,128)(2,1)S(1)}, u32[]{:S(2)}, u32[]{:S(2)}) collective-permute-start(bf16[1,128,1024]{1,2,0:T(8,128)(2,1)S(1)} %bitcast.54), channel_id=1, source_target_pairs={{32,0},{64,32},{96,64},{128,96},{160,128},{192,160},{224,192},{33,... | collective-permute-start | bytes 786440 | tf_op jit(solution)/shard_map/ppermute | solution.py:20
  321.5 13.6 %collective-permute-start.2 = (bf16[1,128,1024]{1,2,0:T(8,128)(2,1)S(1)}, bf16[1,128,1024]{1,2,0:T(8,128)(2,1)S(1)}, u32[]{:S(2)}, u32[]{:S(2)}) collective-permute-start(bf16[1,128,1024]{1,2,0:T(8,128)(2,1)S(1)} %bitcast.55), channel_id=1, source_target_pairs={{32,0},{64,32},{96,64},{128,96},{160,128},{192,160},{224,192},{33,... | collective-permute-start | bytes 786440 | tf_op jit(solution)/shard_map/ppermute | solution.py:20
Sparse Core Ops, SparseCore 0:
  40.1 49.3 all-gather.2

commit v3 on v1

v3 whole, which is shorter than its diff:
```python
import functools

import jax
import jax.numpy as jnp
from jax import lax
from jax.experimental import pallas as pl
from jax.experimental.pallas import tpu as pltpu
from jax.sharding import PartitionSpec as P

HEADS = 64
KV = 8
HD = 128
BLOCK = 64
INTERPRET = False


def from_behind(block, axis, distance):
    devices = range(lax.axis_size(axis))
    route = [(i - distance, i) for i in devices if i - distance in devices]
    return lax.ppermute(block, axis, route)


def block_lists(window_blocks, global_blocks, random_blocks):
    listed = jnp.concatenate([window_blocks, global_blocks, random_blocks], axis=1)
    width = listed.shape[1]
    same = listed[:, :, None] == listed[:, None, :]
    earlier = jnp.arange(width)[None, :] < jnp.arange(width)[:, None]
    repeated = jnp.any(jnp.logical_and(same, earlier[None]), axis=2)
    return (listed, jnp.logical_not(repeated))


def grads_kernel(slots, steps, listed_ref, live_ref, q_ref, g_ref, kv_ref, dq_ref, dkv_ref, kc_ref, vc_ref):
    b = pl.program_id(0)
    scale = HD ** (-0.5)
    width = slots * BLOCK
    rows = q_ref.shape[0] // steps
    half = kv_ref.shape[2] // BLOCK

    @pl.when(b == 0)
    def _():
        dkv_ref[...] = jnp.zeros(dkv_ref.shape, dkv_ref.dtype)

    col = lax.broadcasted_iota(jnp.int32, (1, width), 1)
    nt = (((1,), (1,)), ((), ()))
    tn = (((0,), (0,)), ((), ()))
    for i in range(steps):
        base = (b * steps + i) * slots
        owners = []
        offsets = []
        lives = []
        for j in range(slots):
            n = listed_ref[base + j]
            owners.append(n // half)
            offsets.append(pl.multiple_of((n % half) * BLOCK, BLOCK))
            lives.append(live_ref[base + j])
            kc_ref[j * BLOCK:(j + 1) * BLOCK, :] = kv_ref[owners[j], 0, pl.ds(offsets[j], BLOCK), :]
            vc_ref[j * BLOCK:(j + 1) * BLOCK, :] = kv_ref[owners[j], 1, pl.ds(offsets[j], BLOCK), :]
        q = q_ref[i * rows:(i + 1) * rows, :]
        g = g_ref[i * rows:(i + 1) * rows, :]
        kc = kc_ref[...]
        vc = vc_ref[...]
        live_cols = jnp.zeros((1, width), jnp.int32)
        for j in range(slots):
            inside = jnp.logical_and(col >= j * BLOCK, col < (j + 1) * BLOCK)
            live_cols = jnp.where(inside, lives[j], live_cols)
        scores = lax.dot_general(q, kc, nt, preferred_element_type=jnp.float32) * scale
        scores = jnp.where(live_cols != 0, scores, -jnp.inf)
        top = jnp.max(scores, axis=-1, keepdims=True)
        expd = jnp.exp(scores - top)
        probs = expd / jnp.sum(expd, axis=-1, keepdims=True)
        probs_low = probs.astype(jnp.bfloat16)
        attn = jnp.dot(probs_low, vc, preferred_element_type=jnp.float32)
        attn = attn.astype(jnp.bfloat16).astype(jnp.float32)
        delta = jnp.sum(g.astype(jnp.float32) * attn, axis=-1, keepdims=True)
        dprobs = lax.dot_general(g, vc, nt, preferred_element_type=jnp.float32)
        ds_low = (probs * (dprobs - delta)).astype(jnp.bfloat16)
        dq = jnp.dot(ds_low, kc, preferred_element_type=jnp.float32) * scale
        dq_ref[i * rows:(i + 1) * rows, :] = dq.astype(jnp.bfloat16)
        dk_slots = lax.dot_general(ds_low, q, tn, preferred_element_type=jnp.float32) * scale
        dv_slots = lax.dot_general(probs_low, g, tn, preferred_element_type=jnp.float32)
        for j in range(slots):
            @pl.when(lives[j] != 0)
            def _():
                window = pl.ds(offsets[j], BLOCK)
                dkv_ref[owners[j], 0, window, :] += dk_slots[j * BLOCK:(j + 1) * BLOCK, :]
                dkv_ref[owners[j], 1, window, :] += dv_slots[j * BLOCK:(j + 1) * BLOCK, :]


def block_grads(q_rows, g_rows, kv_parts, listed, live, steps=2):
    nblocks, slots = listed.shape
    rows = q_rows.shape[0] // nblocks * steps
    width = slots * BLOCK
    kernel = functools.partial(grads_kernel, slots, steps)
    whole = lambda b, *_: (0, 0, 0, 0)
    grid_spec = pltpu.PrefetchScalarGridSpec(
        num_scalar_prefetch=2,
        grid=(nblocks // steps,),
        in_specs=[
            pl.BlockSpec((rows, HD), lambda b, *_: (b, 0)),
            pl.BlockSpec((rows, HD), lambda b, *_: (b, 0)),
            pl.BlockSpec(kv_parts.shape, whole),
        ],
        out_specs=[
            pl.BlockSpec((rows, HD), lambda b, *_: (b, 0)),
            pl.BlockSpec(kv_parts.shape, whole),
        ],
        scratch_shapes=[
            pltpu.VMEM((width, HD), jnp.bfloat16),
            pltpu.VMEM((width, HD), jnp.bfloat16),
        ],
    )
    return pl.pallas_call(
        kernel,
        grid_spec=grid_spec,
        out_shape=[
            jax.ShapeDtypeStruct(q_rows.shape, jnp.bfloat16),
            jax.ShapeDtypeStruct(kv_parts.shape, jnp.float32),
        ],
        compiler_params=pltpu.CompilerParams(dimension_semantics=("arbitrary",)),
        cost_estimate=pl.CostEstimate(
            flops=12 * nblocks * (rows // steps) * width * HD,
            transcendentals=nblocks * (rows // steps) * width,
            bytes_accessed=6 * q_rows.size + 6 * kv_parts.size,
        ),
        interpret=INTERPRET,
    )(listed.reshape(-1), live.reshape(-1).astype(jnp.int32), q_rows, g_rows, kv_parts)


def body(queries, keys, values, out_grad, window_blocks, global_blocks, random_blocks):
    lanes = lax.axis_size("seq")
    tok = queries.shape[1]
    repeat = lanes // KV
    q_local = queries[0].reshape(tok, HEADS, HD)
    g_local = out_grad[0].reshape(tok, HEADS, HD)
    q_heads, g_heads = (
        lax.all_to_all(q_local, "seq", split_axis=1, concat_axis=0, tiled=True),
        lax.all_to_all(g_local, "seq", split_axis=1, concat_axis=0, tiled=True),
    )
    k_lead = keys[0].reshape(tok, KV, HD).transpose(1, 0, 2)
    v_lead = values[0].reshape(tok, KV, HD).transpose(1, 0, 2)
    kv_send = jnp.repeat(jnp.stack([k_lead, v_lead], axis=1), repeat, axis=0)
    kv_parts = lax.all_to_all(kv_send, "seq", split_axis=0, concat_axis=0, tiled=True)
    seqlen = q_heads.shape[0]
    per_device = q_heads.shape[1]
    listed, live = block_lists(window_blocks, global_blocks, random_blocks)
    q_rows = q_heads.reshape(seqlen * per_device, HD)
    g_rows = g_heads.reshape(seqlen * per_device, HD)
    dq_rows, dkv = block_grads(q_rows, g_rows, kv_parts, listed, live)
    dq_heads = dq_rows.reshape(seqlen, per_device, HD)
    dq_tokens = lax.all_to_all(dq_heads, "seq", split_axis=0, concat_axis=1, tiled=True)
    dkv_parts = lax.all_to_all(dkv, "seq", split_axis=0, concat_axis=0, tiled=True)
    dkv_sum = jnp.sum(dkv_parts.reshape(KV, repeat, 2, tok, HD), axis=1).astype(jnp.bfloat16)
    dk_tokens = dkv_sum[:, 0].transpose(1, 0, 2)
    dv_tokens = dkv_sum[:, 1].transpose(1, 0, 2)
    dq_flat = dq_tokens.reshape(1, tok, HEADS * HD)
    dk_flat = dk_tokens.reshape(1, tok, KV * HD)
    dv_flat = dv_tokens.reshape(1, tok, KV * HD)
    return from_behind((dq_flat, dk_flat, dv_flat), "pipe", -1)


def solution(mesh):
    in_specs = (
        P("pipe", "seq", None),
        P("pipe", "seq", None),
        P("pipe", "seq", None),
        P("pipe", "seq", None),
        P(),
        P(),
        P(),
    )
    out_specs = (P("pipe", "seq", None), P("pipe", "seq", None), P("pipe", "seq", None))
    return jax.shard_map(body, mesh=mesh, in_specs=in_specs, out_specs=out_specs, check_vma=False)
```

time: 301 us -> 293 us (0.973)
  blocking collectives: 0 us -> 33.4 us
  waiting for transfers between devices: 137 us -> 121 us
  local copies, waits for them, and re-layouts: 48.1 us -> 33.2 us
  starting transfers between devices: 40.4 us -> 33.3 us
  other arithmetic: 6.65 us -> 2.86 us
    all_to_all x0 -> x1, blocking collectives: none -> 33.4 us  [body(): lax.all_to_all(dq_heads, 'seq', split_axis=0, concat_axis=1, tiled=True)]
    all_to_all x3 -> x2, waiting for transfers between devices: 84.2 us -> 57.8 us  [the longest x1 41.3 us: body(): lax.all_to_all(dkv, 'seq', split_axis=0, concat_axis=0, tiled=True)]
    all_to_all x1, waiting for transfers between devices: 17.1 us -> 27.8 us  [body(): lax.all_to_all(g_local, 'seq', split_axis=1, concat_axis=0, tiled=True)]
    pallas_call x1 -> x0, local copies, waits for them, and re-layouts: 8.79 us -> none  [block_grads(): pl.pallas_call(kernel, grid_spec=grid_spec, out_shape=[jax.ShapeDtypeStru...]
    all_to_all x3 -> x2, starting transfers between devices: 20.5 us -> 12.8 us  [the longest x1 6.89 us: body(): lax.all_to_all(kv_send, 'seq', split_axis=0, concat_axis=0, tiled=True)]
    unnamed x1 -> x0, other arithmetic: 5 us -> none
    unnamed x15 -> x17, local copies, waits for them, and re-layouts: 13.2 us -> 11.3 us
  transfers between devices with their start and end apart: 8 -> 7, of which waited for: 7 -> 7; matrix products, arithmetic and copies ran while one was open for 14% -> 10% of each run, Pallas kernels for 0% -> 0%
where the time goes in v3:
time: 293 us; the launch traced here: 292 us
  waiting for transfers between devices  121 us (41%)
  Pallas kernels  67.3 us (23%)
  blocking collectives  33.4 us (11%)
  starting transfers between devices  33.3 us (11%)
  local copies, waits for them, and re-layouts  33.2 us (11%)
    pallas_call x1, Pallas kernels, block_grads(): pl.pallas_call(kernel, grid_spec=grid_spec, out_shape=[jax.ShapeDtypeStru...  67.3 us
    all_to_all x1, waiting for transfers between devices, body(): lax.all_to_all(dkv, 'seq', split_axis=0, concat_axis=0, tiled=True)  41.3 us
    all_to_all x1, blocking collectives, body(): lax.all_to_all(dq_heads, 'seq', split_axis=0, concat_axis=1, tiled=True)  33.4 us
    all_to_all x1, waiting for transfers between devices, body(): lax.all_to_all(g_local, 'seq', split_axis=1, concat_axis=0, tiled=True)  27.8 us
    all_to_all x1, waiting for transfers between devices, body(): lax.all_to_all(q_local, 'seq', split_axis=1, concat_axis=0, tiled=True)  23.8 us
    all_to_all x1, waiting for transfers between devices, body(): lax.all_to_all(kv_send, 'seq', split_axis=0, concat_axis=0, tiled=True)  16.5 us
    ppermute x3, waiting for transfers between devices, from_behind(): return lax.ppermute(block, axis, route)  11.8 us
    unnamed x17, local copies, waits for them, and re-layouts  11.3 us
  transfers between devices with their start and end apart: 7, of which 7 were waited for; matrix products, arithmetic and copies ran while one was open for 10% of the time, Pallas kernels for 0%

profile of v3, /device:TPU:98, one launch (start us, length us, event | category | flops | bytes accessed | tf_op | source)
XLA Modules:
  0.0 292.1 jit_solution(13720484588866529150)
XLA Ops:
  0.6 4.1 %copy.60 = bf16[1,128,8192]{1,2,0:T(8,128)(2,1)} copy(bf16[1,128,8192]{2,1,0:T(8,128)(2,1)} %param.7) | data formatting | bytes 4194304 | tf_op args[0]
  4.7 7.6 %all-to-all-start = ((bf16[128,64,128]{0,2,1:T(8,128)(2,1)}), bf16[128,64,128]{0,2,1:T(8,128)(2,1)S(1)}, u32[]{:S(2)}, u32[]{:S(2)}) async-start(bf16[128,64,128]{0,2,1:T(8,128)(2,1)} %bitcast.45), calls=%async_computation | async-start | bytes 4194304 | tf_op jit(solution)/shard_map/all_to_all | solution.py:136
  12.3 4.1 %copy.63 = bf16[1,128,8192]{1,2,0:T(8,128)(2,1)} copy(bf16[1,128,8192]{2,1,0:T(8,128)(2,1)} %param.10) | data formatting | bytes 4194304 | tf_op args[3]
  16.4 23.8 %all-to-all-done = bf16[128,64,128]{0,2,1:T(8,128)(2,1)S(1)} async-done(((bf16[128,64,128]{0,2,1:T(8,128)(2,1)}), bf16[128,64,128]{0,2,1:T(8,128)(2,1)S(1)}, u32[]{:S(2)}, u32[]{:S(2)}) %all-to-all-start) | async-done | bytes 2097184 | tf_op jit(solution)/shard_map/all_to_all | solution.py:136
  40.2 6.9 %all-to-all-start.1 = ((bf16[128,64,128]{0,2,1:T(8,128)(2,1)}), bf16[128,64,128]{0,2,1:T(8,128)(2,1)}, u32[]{:S(2)}, u32[]{:S(2)}) async-start(bf16[128,64,128]{0,2,1:T(8,128)(2,1)} %bitcast.43), calls=%async_computation.1 | async-start | bytes 4194304 | tf_op jit(solution)/shard_map/all_to_all | solution.py:137
  47.4 27.8 %all-to-all-done.1 = bf16[128,64,128]{0,2,1:T(8,128)(2,1)} async-done(((bf16[128,64,128]{0,2,1:T(8,128)(2,1)}), bf16[128,64,128]{0,2,1:T(8,128)(2,1)}, u32[]{:S(2)}, u32[]{:S(2)}) %all-to-all-start.1) | async-done | bytes 2097184 | tf_op jit(solution)/shard_map/all_to_all | solution.py:137
  75.2 1.8 broadcast_in_dim.2
  77.0 6.9 %all-to-all-start.2 = ((bf16[32,2,128,128]{3,2,1,0:T(8,128)(2,1)}), bf16[32,2,128,128]{3,2,1,0:T(8,128)(2,1)}, u32[]{:S(2)}, u32[]{:S(2)}) async-start(bf16[32,2,128,128]{3,2,1,0:T(8,128)(2,1)} %bitcast.14), calls=%async_computation.2 | async-start | bytes 4194304 | tf_op jit(solution)/shard_map/all_to_all | solution.py:142
  85.6 3.8 %copy.62 = bf16[32,128,2,128]{3,2,1,0:T(2,128)(2,1)} copy(bf16[32,128,2,128]{1,3,2,0:T(8,128)(2,1)S(1)} %bitcast.42) | data formatting | bytes 4194304 | tf_op jit(solution)/shard_map/all_to_all | solution.py:136
  89.4 6.2 %copy.65 = bf16[32,128,2,128]{3,2,1,0:T(2,128)(2,1)} copy(bf16[32,128,2,128]{1,3,2,0:T(8,128)(2,1)} %bitcast.8) | data formatting | bytes 4194304 | tf_op jit(solution)/shard_map/all_to_all | solution.py:137
  95.5 16.5 %all-to-all-done.2.kv_ref = bf16[32,2,128,128]{3,2,1,0:T(8,128)(2,1)} async-done(((bf16[32,2,128,128]{3,2,1,0:T(8,128)(2,1)}), bf16[32,2,128,128]{3,2,1,0:T(8,128)(2,1)}, u32[]{:S(2)}, u32[]{:S(2)}) %all-to-all-start.2) | async-done | bytes 2097184 | tf_op jit(solution)/shard_map/all_to_all | solution.py:142
  112.0 67.3 %shard_map.94 = (bf16[8192,128]{1,0:T(8,128)(2,1)}, f32[32,2,128,128]{3,2,1,0:T(8,128)}) custom-call(s32[512]{0:T(512)} %reshape.55.listed_ref, s32[512]{0:T(512)} %reshape.64.live_ref, bf16[8192,128]{1,0:T(8,128)(2,1)} %bitcast.47, bf16[8192,128]{1,0:T(8,128)(2,1)} %bitcast.48, bf16[32,2,128,128]{3,2,1,0:T(8,128)(2,1)} %all-to-all-done.2.kv_ref), custom_call_target="tpu_custom_call" | custom-call | flops 6442450944 | bytes 12582912 | tf_op jit(solution)/shard_map/pallas_call | solution.py:112
  179.3 33.4 %all_to_all.55 = bf16[4096,2,128]{2,1,0:T(2,128)(2,1)S(1)} all-to-all(bf16[4096,2,128]{2,1,0:T(2,128)(2,1)} %bitcast.49), channel_id=1, replica_groups=mesh['pipe'=8,'seq'=32] {'seq'}, dimensions={0} | all-to-all | bytes 4194304 | tf_op jit(solution)/shard_map/all_to_all | solution.py:150
  212.7 5.9 %all-to-all-start.4 = ((f32[32,2,128,128]{3,2,1,0:T(8,128)}), f32[32,2,128,128]{3,2,1,0:T(8,128)}, u32[]{:S(2)}, u32[]{:S(2)}) async-start(f32[32,2,128,128]{3,2,1,0:T(8,128)} %get-tuple-element.6), calls=%async_computation.4 | async-start | bytes 8388608 | tf_op jit(solution)/shard_map/all_to_all | solution.py:151
  218.6 3.7 %copy.77 = bf16[32,128,2,128]{3,2,0,1:T(2,128)(2,1)} copy(bf16[32,128,2,128]{3,2,1,0:T(2,128)(2,1)S(1)} %bitcast.44) | data formatting | bytes 4194304 | tf_op jit(solution)/shard_map/all_to_all | solution.py:150
  222.3 4.5 %reshape.60 = bf16[1,128,8192]{2,1,0:T(8,128)(2,1)} reshape(bf16[128,32,2,128]{3,2,1,0:T(2,128)(2,1)} %bitcast.46) | data formatting | bytes 4194304 | tf_op jit(solution)/shard_map/reshape | solution.py:155
  226.8 2.0 collective-permute-start
  228.8 41.3 %all-to-all-done.4 = f32[32,2,128,128]{3,2,1,0:T(8,128)} async-done(((f32[32,2,128,128]{3,2,1,0:T(8,128)}), f32[32,2,128,128]{3,2,1,0:T(8,128)}, u32[]{:S(2)}, u32[]{:S(2)}) %all-to-all-start.4) | async-done | bytes 4194336 | tf_op jit(solution)/shard_map/all_to_all | solution.py:151
  270.1 2.7 bitcast_reduce_fusion
  273.2 2.0 collective-permute-start.1
  275.3 2.0 collective-permute-start.2
  278.0 7.6 %collective-permute-done.1 = bf16[1,128,1024]{1,2,0:T(8,128)(2,1)S(1)} collective-permute-done((bf16[1,128,1024]{1,2,0:T(8,128)(2,1)S(1)}, bf16[1,128,1024]{1,2,0:T(8,128)(2,1)S(1)}, u32[]{:S(2)}, u32[]{:S(2)}) %collective-permute-start.1) | collective-permute-done | bytes 262176 | tf_op jit(solution)/shard_map/ppermute | solution.py:20
  286.4 3.6 %collective-permute-done.2 = bf16[1,128,1024]{1,2,0:T(8,128)(2,1)S(1)} collective-permute-done((bf16[1,128,1024]{1,2,0:T(8,128)(2,1)S(1)}, bf16[1,128,1024]{1,2,0:T(8,128)(2,1)S(1)}, u32[]{:S(2)}, u32[]{:S(2)}) %collective-permute-start.2) | collective-permute-done | bytes 262176 | tf_op jit(solution)/shard_map/ppermute | solution.py:20
  290.8 1.3 copy.79
  (28 shorter events, 4.6 us)
Async XLA Ops:
  4.7 35.5 %all-to-all-start = ((bf16[128,64,128]{0,2,1:T(8,128)(2,1)}), bf16[128,64,128]{0,2,1:T(8,128)(2,1)S(1)}, u32[]{:S(2)}, u32[]{:S(2)}) async-start(bf16[128,64,128]{0,2,1:T(8,128)(2,1)} %bitcast.45), calls=%async_computation | async-start | bytes 4194304 | tf_op jit(solution)/shard_map/all_to_all | solution.py:136
  40.2 6.9 %copy-start = (bf16[1,128,1024]{2,1,0:T(8,128)(2,1)S(1)}, bf16[1,128,1024]{2,1,0:T(8,128)(2,1)}, u32[]{:S(2)}) copy-start(bf16[1,128,1024]{2,1,0:T(8,128)(2,1)} %param.8) | copy-start | bytes 786436
  40.2 6.9 %copy-start.1 = (bf16[1,128,1024]{2,1,0:T(8,128)(2,1)S(1)}, bf16[1,128,1024]{2,1,0:T(8,128)(2,1)}, u32[]{:S(2)}) copy-start(bf16[1,128,1024]{2,1,0:T(8,128)(2,1)} %param.9) | copy-start | bytes 786436
  40.2 35.0 %all-to-all-start.1 = ((bf16[128,64,128]{0,2,1:T(8,128)(2,1)}), bf16[128,64,128]{0,2,1:T(8,128)(2,1)}, u32[]{:S(2)}, u32[]{:S(2)}) async-start(bf16[128,64,128]{0,2,1:T(8,128)(2,1)} %bitcast.43), calls=%async_computation.1 | async-start | bytes 4194304 | tf_op jit(solution)/shard_map/all_to_all | solution.py:137
  77.0 6.9 %copy-start.2 = (s32[64,3]{0,1:T(4,128)S(1)}, s32[64,3]{0,1:T(4,128)}, u32[]{:S(2)}) copy-start(s32[64,3]{0,1:T(4,128)} %param.13) | copy-start | bytes 2308
  77.0 6.9 %copy-start.3 = (s32[64,3]{0,1:T(4,128)S(1)}, s32[64,3]{0,1:T(4,128)}, u32[]{:S(2)}) copy-start(s32[64,3]{0,1:T(4,128)} %param.11) | copy-start | bytes 2308
  77.0 6.9 %copy-start.4 = (s32[64,2]{0,1:T(2,128)S(1)}, s32[64,2]{0,1:T(2,128)}, u32[]{:S(2)}) copy-start(s32[64,2]{0,1:T(2,128)} %param.12) | copy-start | bytes 1540
  77.0 35.0 %all-to-all-start.2 = ((bf16[32,2,128,128]{3,2,1,0:T(8,128)(2,1)}), bf16[32,2,128,128]{3,2,1,0:T(8,128)(2,1)}, u32[]{:S(2)}, u32[]{:S(2)}) async-start(bf16[32,2,128,128]{3,2,1,0:T(8,128)(2,1)} %bitcast.14), calls=%async_computation.2 | async-start | bytes 4194304 | tf_op jit(solution)/shard_map/all_to_all | solution.py:142
  212.7 57.4 %all-to-all-start.4 = ((f32[32,2,128,128]{3,2,1,0:T(8,128)}), f32[32,2,128,128]{3,2,1,0:T(8,128)}, u32[]{:S(2)}, u32[]{:S(2)}) async-start(f32[32,2,128,128]{3,2,1,0:T(8,128)} %get-tuple-element.6), calls=%async_computation.4 | async-start | bytes 8388608 | tf_op jit(solution)/shard_map/all_to_all | solution.py:151
  226.8 51.1 %collective-permute-start = (bf16[1,128,8192]{2,1,0:T(8,128)(2,1)}, bf16[1,128,8192]{2,1,0:T(8,128)(2,1)S(1)}, u32[]{:S(2)}, u32[]{:S(2)}) collective-permute-start(bf16[1,128,8192]{2,1,0:T(8,128)(2,1)} %reshape.60), channel_id=1, source_target_pairs={{32,0},{64,32},{96,64},{128,96},{160,128},{192,160},{224,192},{33,... | collective-permute-start | bytes 6291464 | tf_op jit(solution)/shard_map/ppermute | solution.py:20
  273.2 12.3 %collective-permute-start.1 = (bf16[1,128,1024]{1,2,0:T(8,128)(2,1)S(1)}, bf16[1,128,1024]{1,2,0:T(8,128)(2,1)S(1)}, u32[]{:S(2)}, u32[]{:S(2)}) collective-permute-start(bf16[1,128,1024]{1,2,0:T(8,128)(2,1)S(1)} %bitcast.55), channel_id=1, source_target_pairs={{32,0},{64,32},{96,64},{128,96},{160,128},{192,160},{224,192},{33,... | collective-permute-start | bytes 786440 | tf_op jit(solution)/shard_map/ppermute | solution.py:20
  275.3 14.7 %collective-permute-start.2 = (bf16[1,128,1024]{1,2,0:T(8,128)(2,1)S(1)}, bf16[1,128,1024]{1,2,0:T(8,128)(2,1)S(1)}, u32[]{:S(2)}, u32[]{:S(2)}) collective-permute-start(bf16[1,128,1024]{1,2,0:T(8,128)(2,1)S(1)} %bitcast.54), channel_id=1, source_target_pairs={{32,0},{64,32},{96,64},{128,96},{160,128},{192,160},{224,192},{33,... | collective-permute-start | bytes 786440 | tf_op jit(solution)/shard_map/ppermute | solution.py:20

commit v4 on v3

--- a/solution.py
+++ b/solution.py
@@ -33,7 +33,6 @@
     b = pl.program_id(0)
     scale = HD ** (-0.5)
     width = slots * BLOCK
-    rows = q_ref.shape[0] // steps
     half = kv_ref.shape[2] // BLOCK
 
     @pl.when(b == 0)
@@ -55,8 +54,8 @@
             lives.append(live_ref[base + j])
             kc_ref[j * BLOCK:(j + 1) * BLOCK, :] = kv_ref[owners[j], 0, pl.ds(offsets[j], BLOCK), :]
             vc_ref[j * BLOCK:(j + 1) * BLOCK, :] = kv_ref[owners[j], 1, pl.ds(offsets[j], BLOCK), :]
-        q = q_ref[i * rows:(i + 1) * rows, :]
-        g = g_ref[i * rows:(i + 1) * rows, :]
+        q = q_ref[:, i * BLOCK:(i + 1) * BLOCK, :].reshape(-1, HD)
+        g = g_ref[:, i * BLOCK:(i + 1) * BLOCK, :].reshape(-1, HD)
         kc = kc_ref[...]
         vc = vc_ref[...]
         live_cols = jnp.zeros((1, width), jnp.int32)
@@ -75,7 +74,7 @@
         dprobs = lax.dot_general(g, vc, nt, preferred_element_type=jnp.float32)
         ds_low = (probs * (dprobs - delta)).astype(jnp.bfloat16)
         dq = jnp.dot(ds_low, kc, preferred_element_type=jnp.float32) * scale
-        dq_ref[i * rows:(i + 1) * rows, :] = dq.astype(jnp.bfloat16)
+        dq_ref[:, i * BLOCK:(i + 1) * BLOCK, :] = dq.astype(jnp.bfloat16).reshape(-1, BLOCK, HD)
         dk_slots = lax.dot_general(ds_low, q, tn, preferred_element_type=jnp.float32) * scale
         dv_slots = lax.dot_general(probs_low, g, tn, preferred_element_type=jnp.float32)
         for j in range(slots):
@@ -86,23 +85,25 @@
                 dkv_ref[owners[j], 1, window, :] += dv_slots[j * BLOCK:(j + 1) * BLOCK, :]
 
 
-def block_grads(q_rows, g_rows, kv_parts, listed, live, steps=2):
+def block_grads(packed, listed, live, steps=2):
     nblocks, slots = listed.shape
-    rows = q_rows.shape[0] // nblocks * steps
+    lanes, _, tok, _ = packed.shape
+    half = tok // BLOCK
+    per_device = 2
+    rows = BLOCK * steps
     width = slots * BLOCK
     kernel = functools.partial(grads_kernel, slots, steps)
-    whole = lambda b, *_: (0, 0, 0, 0)
     grid_spec = pltpu.PrefetchScalarGridSpec(
         num_scalar_prefetch=2,
         grid=(nblocks // steps,),
         in_specs=[
-            pl.BlockSpec((rows, HD), lambda b, *_: (b, 0)),
-            pl.BlockSpec((rows, HD), lambda b, *_: (b, 0)),
-            pl.BlockSpec(kv_parts.shape, whole),
+            pl.BlockSpec((None, per_device, rows, HD), lambda b, *_: (b * steps // half, 0, b % (half // steps), 0)),
+            pl.BlockSpec((None, per_device, rows, HD), lambda b, *_: (b * steps // half, 1, b % (half // steps), 0)),
+            pl.BlockSpec((lanes, 2, tok, HD), lambda b, *_: (0, 2, 0, 0)),
         ],
         out_specs=[
-            pl.BlockSpec((rows, HD), lambda b, *_: (b, 0)),
-            pl.BlockSpec(kv_parts.shape, whole),
+            pl.BlockSpec((None, per_device, rows, HD), lambda b, *_: (b * steps // half, 0, b % (half // steps), 0)),
+            pl.BlockSpec((lanes, 2, tok, HD), lambda b, *_: (0, 0, 0, 0)),
         ],
         scratch_shapes=[
             pltpu.VMEM((width, HD), jnp.bfloat16),
@@ -113,41 +114,34 @@
         kernel,
         grid_spec=grid_spec,
         out_shape=[
-            jax.ShapeDtypeStruct(q_rows.shape, jnp.bfloat16),
-            jax.ShapeDtypeStruct(kv_parts.shape, jnp.float32),
+            jax.ShapeDtypeStruct((lanes, per_device, tok, HD), jnp.bfloat16),
+            jax.ShapeDtypeStruct((lanes, 2, tok, HD), jnp.float32),
         ],
         compiler_params=pltpu.CompilerParams(dimension_semantics=("arbitrary",)),
         cost_estimate=pl.CostEstimate(
-            flops=12 * nblocks * (rows // steps) * width * HD,
-            transcendentals=nblocks * (rows // steps) * width,
-            bytes_accessed=6 * q_rows.size + 6 * kv_parts.size,
+            flops=12 * nblocks * BLOCK * per_device * width * HD,
+            transcendentals=nblocks * BLOCK * per_device * width,
+            bytes_accessed=6 * packed.size,
         ),
         interpret=INTERPRET,
-    )(listed.reshape(-1), live.reshape(-1).astype(jnp.int32), q_rows, g_rows, kv_parts)
+    )(listed.reshape(-1), live.reshape(-1).astype(jnp.int32), packed, packed, packed)
 
 
 def body(queries, keys, values, out_grad, window_blocks, global_blocks, random_blocks):
     lanes = lax.axis_size("seq")
     tok = queries.shape[1]
     repeat = lanes // KV
-    q_local = queries[0].reshape(tok, HEADS, HD)
-    g_local = out_grad[0].reshape(tok, HEADS, HD)
-    q_heads, g_heads = (
-        lax.all_to_all(q_local, "seq", split_axis=1, concat_axis=0, tiled=True),
-        lax.all_to_all(g_local, "seq", split_axis=1, concat_axis=0, tiled=True),
-    )
-    k_lead = keys[0].reshape(tok, KV, HD).transpose(1, 0, 2)
-    v_lead = values[0].reshape(tok, KV, HD).transpose(1, 0, 2)
-    kv_send = jnp.repeat(jnp.stack([k_lead, v_lead], axis=1), repeat, axis=0)
-    kv_parts = lax.all_to_all(kv_send, "seq", split_axis=0, concat_axis=0, tiled=True)
-    seqlen = q_heads.shape[0]
-    per_device = q_heads.shape[1]
+    per_device = HEADS // lanes
+    q_lead = queries[0].reshape(tok, lanes, per_device, HD).transpose(1, 2, 0, 3)
+    g_lead = out_grad[0].reshape(tok, lanes, per_device, HD).transpose(1, 2, 0, 3)
+    k_lead = jnp.repeat(keys[0].reshape(tok, KV, 1, HD).transpose(1, 2, 0, 3), repeat, axis=0)
+    v_lead = jnp.repeat(values[0].reshape(tok, KV, 1, HD).transpose(1, 2, 0, 3), repeat, axis=0)
+    send = jnp.concatenate([q_lead, g_lead, k_lead, v_lead], axis=1)
+    packed = lax.all_to_all(send, "seq", split_axis=0, concat_axis=0, tiled=True)
     listed, live = block_lists(window_blocks, global_blocks, random_blocks)
-    q_rows = q_heads.reshape(seqlen * per_device, HD)
-    g_rows = g_heads.reshape(seqlen * per_device, HD)
-    dq_rows, dkv = block_grads(q_rows, g_rows, kv_parts, listed, live)
-    dq_heads = dq_rows.reshape(seqlen, per_device, HD)
-    dq_tokens = lax.all_to_all(dq_heads, "seq", split_axis=0, concat_axis=1, tiled=True)
+    dq_heads, dkv = block_grads(packed, listed, live)
+    dq_parts = lax.all_to_all(dq_heads, "seq", split_axis=0, concat_axis=0, tiled=True)
+    dq_tokens = dq_parts.transpose(2, 0, 1, 3)
     dkv_parts = lax.all_to_all(dkv, "seq", split_axis=0, concat_axis=0, tiled=True)
     dkv_sum = jnp.sum(dkv_parts.reshape(KV, repeat, 2, tok, HD), axis=1).astype(jnp.bfloat16)
     dk_tokens = dkv_sum[:, 0].transpose(1, 0, 2)

time: 293 us -> 285 us (0.973)
  starting transfers between devices: 33.3 us -> 19.7 us
  waiting for transfers between devices: 121 us -> 129 us
  local copies, waits for them, and re-layouts: 33.2 us -> 25.3 us
  other arithmetic: 2.86 us -> 7.51 us
    all_to_all x3 -> x0, local copies, waits for them, and re-layouts: 13.6 us -> none  [the longest x1 6.18 us: body(): lax.all_to_all(g_local, 'seq', split_axis=1, concat_axis=0, tiled=True)]
    all_to_all x3 -> x1, starting transfers between devices: 21.4 us -> 7.81 us  [body(): lax.all_to_all(send, 'seq', split_axis=0, concat_axis=0, tiled=True)]
    another operation x1 -> x2, local copies, waits for them, and re-layouts: 0.1 us -> 5.8 us  [the longest x1 2.91 us: body(): queries[0].reshape(tok, lanes, per_device, HD).transpose(1, 2, 0, 3)]
    all_to_all x3 -> x1, waiting for transfers between devices: 68.1 us -> 73.5 us  [body(): lax.all_to_all(send, 'seq', split_axis=0, concat_axis=0, tiled=True)]
    all_to_all x1, waiting for transfers between devices: 41.3 us -> 46.6 us  [body(): lax.all_to_all(dkv, 'seq', split_axis=0, concat_axis=0, tiled=True)]
    concatenate x0 -> x1, other arithmetic: none -> 4.7 us  [body(): send = jnp.concatenate([q_lead, g_lead, k_lead, v_lead], axis=1)]
    reshape x1 -> x0, local copies, waits for them, and re-layouts: 4.51 us -> none  [body(): dq_flat = dq_tokens.reshape(1, tok, HEADS * HD)]
    transpose x0 -> x3, local copies, waits for them, and re-layouts: none -> 2.97 us  [the longest x1 2.89 us: body(): dq_tokens = dq_parts.transpose(2, 0, 1, 3)]
  transfers between devices with their start and end apart: 7 -> 5, of which waited for: 7 -> 4; matrix products, arithmetic and copies ran while one was open for 10% -> 4% of each run, Pallas kernels for 0% -> 0%
where the time goes in v4:
time: 285 us; the launch traced here: 284 us
  waiting for transfers between devices  129 us (45%)
  Pallas kernels  68 us (24%)
  blocking collectives  34 us (12%)
  local copies, waits for them, and re-layouts  25.3 us (9%)
  starting transfers between devices  19.7 us (7%)
  other arithmetic  7.51 us (3%)
    all_to_all x1, waiting for transfers between devices, body(): lax.all_to_all(send, 'seq', split_axis=0, concat_axis=0, tiled=True)  73.5 us
    pallas_call x1, Pallas kernels, block_grads(): pl.pallas_call(kernel, grid_spec=grid_spec, out_shape=[jax.ShapeDtypeStru...  68 us
    all_to_all x1, waiting for transfers between devices, body(): lax.all_to_all(dkv, 'seq', split_axis=0, concat_axis=0, tiled=True)  46.6 us
    all_to_all x1, blocking collectives, body(): lax.all_to_all(dq_heads, 'seq', split_axis=0, concat_axis=0, tiled=True)  34 us
    unnamed x15, local copies, waits for them, and re-layouts  14.1 us
    ppermute x3, waiting for transfers between devices, from_behind(): return lax.ppermute(block, axis, route)  8.93 us
    all_to_all x1, starting transfers between devices, body(): lax.all_to_all(send, 'seq', split_axis=0, concat_axis=0, tiled=True)  7.81 us
    ppermute x3, starting transfers between devices, from_behind(): return lax.ppermute(block, axis, route)  6.03 us
  transfers between devices with their start and end apart: 5, of which 4 were waited for; matrix products, arithmetic and copies ran while one was open for 4% of the time, Pallas kernels for 0%

profile of v4, /device:TPU:98, one launch (start us, length us, event | category | flops | bytes accessed | tf_op | source)
XLA Modules:
  0.0 284.4 jit_solution(10923107821360872694)
XLA Ops:
  0.6 1.0 copy.65
  1.7 1.0 copy.66
  2.7 3.2 %copy.53 = bf16[1,128,8192]{1,2,0:T(8,128)(2,1)S(1)} copy(bf16[1,128,8192]{2,1,0:T(8,128)(2,1)} %param.7) | data formatting | bytes 4194304 | tf_op args[0]
  6.0 2.9 %copy.54 = bf16[128,32,2,128]{3,0,2,1:T(8,128)(2,1)} copy(bf16[128,32,2,128]{0,3,2,1:T(8,128)(2,1)S(1)} %bitcast.39) | data formatting | bytes 4194304 | tf_op jit(solution)/shard_map/reshape;squeeze | solution.py:135
  8.9 3.2 %copy.55 = bf16[1,128,8192]{1,2,0:T(8,128)(2,1)S(1)} copy(bf16[1,128,8192]{2,1,0:T(8,128)(2,1)} %param.10) | data formatting | bytes 4194304 | tf_op args[3]
  12.1 2.9 %copy.56 = bf16[128,32,2,128]{3,0,2,1:T(8,128)(2,1)} copy(bf16[128,32,2,128]{0,3,2,1:T(8,128)(2,1)S(1)} %bitcast.40) | data formatting | bytes 4194304 | tf_op jit(solution)/shard_map/reshape;squeeze | solution.py:136
  15.5 1.1 copy-done
  16.6 4.7 %pad_maximum_fusion = bf16[32,6,128,128]{3,2,1,0:T(8,128)(2,1)} fusion(bf16[32,1,128,128]{3,2,1,0:T(8,128)(2,1)S(1)} %bitcast.43, bf16[32,1,128,128]{3,2,1,0:T(8,128)(2,1)S(1)} %bitcast.44, bf16[32,2,128,128]{3,2,1,0:T(8,128)(2,1)} %bitcast.42, bf16[32,2,128,128]{3,2,1,0:T(8,128)(2,1)S(1)} %bitcast.41), kind=kLoop, calls=%fused_computation | loop fusion | flops 9437184 | bytes 12582912 | tf_op jit(solution)/shard_map/concatenate | solution.py:139
  21.3 7.8 %all-to-all-start = ((bf16[32,6,128,128]{3,2,1,0:T(8,128)(2,1)}), bf16[32,6,128,128]{3,2,1,0:T(8,128)(2,1)}, u32[]{:S(2)}, u32[]{:S(2)}) async-start(bf16[32,6,128,128]{3,2,1,0:T(8,128)(2,1)} %pad_maximum_fusion), calls=%async_computation | async-start | bytes 12582912 | tf_op jit(solution)/shard_map/all_to_all | solution.py:140
  30.8 73.5 %all-to-all-done.q_ref.g_ref.kv_ref = bf16[32,6,128,128]{3,2,1,0:T(8,128)(2,1)} async-done(((bf16[32,6,128,128]{3,2,1,0:T(8,128)(2,1)}), bf16[32,6,128,128]{3,2,1,0:T(8,128)(2,1)}, u32[]{:S(2)}, u32[]{:S(2)}) %all-to-all-start) | async-done | bytes 6291488 | tf_op jit(solution)/shard_map/all_to_all | solution.py:140
  104.3 68.0 %shard_map.94 = (bf16[32,2,128,128]{3,2,1,0:T(8,128)(2,1)}, f32[32,2,128,128]{3,2,1,0:T(8,128)}) custom-call(s32[512]{0:T(512)} %reshape.50.listed_ref, s32[512]{0:T(512)} %reshape.55.live_ref, bf16[32,6,128,128]{3,2,1,0:T(8,128)(2,1)} %all-to-all-done.q_ref.g_ref.kv_ref, bf16[32,6,128,128]{3,2,1,0:T(8,128)(2,1)} %all-to-all-done.q_ref.g_ref.kv_ref, ...), custom_call_target="tpu_custom_call" | custom-call | flops 6442450944 | bytes 18874368 | tf_op jit(solution)/shard_map/pallas_call | solution.py:113
  172.3 34.0 %all_to_all.15 = bf16[32,2,128,128]{3,2,1,0:T(8,128)(2,1)S(1)} all-to-all(bf16[32,2,128,128]{3,2,1,0:T(8,128)(2,1)} %get-tuple-element.5), channel_id=1, replica_groups=mesh['pipe'=8,'seq'=32] {'seq'}, dimensions={0} | all-to-all | bytes 4194304 | tf_op jit(solution)/shard_map/all_to_all | solution.py:143
  206.3 5.9 %all-to-all-start.2 = ((f32[32,2,128,128]{3,2,1,0:T(8,128)}), f32[32,2,128,128]{3,2,1,0:T(8,128)}, u32[]{:S(2)}, u32[]{:S(2)}) async-start(f32[32,2,128,128]{3,2,1,0:T(8,128)} %get-tuple-element.6), calls=%async_computation.2 | async-start | bytes 8388608 | tf_op jit(solution)/shard_map/all_to_all | solution.py:145
  212.2 2.9 %copy.59 = bf16[128,32,2,128]{0,3,2,1:T(8,128)(2,1)} copy(bf16[128,32,2,128]{3,0,2,1:T(8,128)(2,1)S(1)} %bitcast.38) | data formatting | bytes 4194304 | tf_op jit(solution)/shard_map/transpose | solution.py:144
  215.1 2.0 collective-permute-start
  217.1 46.6 %all-to-all-done.2 = f32[32,2,128,128]{3,2,1,0:T(8,128)} async-done(((f32[32,2,128,128]{3,2,1,0:T(8,128)}), f32[32,2,128,128]{3,2,1,0:T(8,128)}, u32[]{:S(2)}, u32[]{:S(2)}) %all-to-all-start.2) | async-done | bytes 4194336 | tf_op jit(solution)/shard_map/all_to_all | solution.py:145
  263.7 2.7 bitcast_reduce_fusion
  266.8 2.0 collective-permute-start.1
  268.8 2.0 collective-permute-start.2
  270.9 2.9 %copy.62 = bf16[1,128,8192]{2,1,0:T(8,128)(2,1)} copy(bf16[1,128,8192]{1,2,0:T(8,128)(2,1)S(1)} %collective-permute-done) | data formatting | bytes 4194304
  273.8 5.3 %collective-permute-done.1 = bf16[1,128,1024]{1,2,0:T(8,128)(2,1)S(1)} collective-permute-done((bf16[1,128,1024]{1,2,0:T(8,128)(2,1)S(1)}, bf16[1,128,1024]{1,2,0:T(8,128)(2,1)S(1)}, u32[]{:S(2)}, u32[]{:S(2)}) %collective-permute-start.1) | collective-permute-done | bytes 262176 | tf_op jit(solution)/shard_map/ppermute | solution.py:20
  279.1 0.8 copy.63
  280.0 3.6 %collective-permute-done.2 = bf16[1,128,1024]{1,2,0:T(8,128)(2,1)S(1)} collective-permute-done((bf16[1,128,1024]{1,2,0:T(8,128)(2,1)S(1)}, bf16[1,128,1024]{1,2,0:T(8,128)(2,1)S(1)}, u32[]{:S(2)}, u32[]{:S(2)}) %collective-permute-start.2) | collective-permute-done | bytes 262176 | tf_op jit(solution)/shard_map/ppermute | solution.py:20
  283.5 0.8 copy.64
  (23 shorter events, 2.6 us)
Async XLA Ops:
  15.0 1.6 copy-start
  21.3 7.8 %copy-start.1 = (s32[64,3]{0,1:T(4,128)S(1)}, s32[64,3]{0,1:T(4,128)}, u32[]{:S(2)}) copy-start(s32[64,3]{0,1:T(4,128)} %param.13) | copy-start | bytes 2308
  21.3 7.8 %copy-start.2 = (s32[64,3]{0,1:T(4,128)S(1)}, s32[64,3]{0,1:T(4,128)}, u32[]{:S(2)}) copy-start(s32[64,3]{0,1:T(4,128)} %param.11) | copy-start | bytes 2308
  21.3 7.8 %copy-start.3 = (s32[64,2]{0,1:T(2,128)S(1)}, s32[64,2]{0,1:T(2,128)}, u32[]{:S(2)}) copy-start(s32[64,2]{0,1:T(2,128)} %param.12) | copy-start | bytes 1540
  21.3 83.0 %all-to-all-start = ((bf16[32,6,128,128]{3,2,1,0:T(8,128)(2,1)}), bf16[32,6,128,128]{3,2,1,0:T(8,128)(2,1)}, u32[]{:S(2)}, u32[]{:S(2)}) async-start(bf16[32,6,128,128]{3,2,1,0:T(8,128)(2,1)} %pad_maximum_fusion), calls=%async_computation | async-start | bytes 12582912 | tf_op jit(solution)/shard_map/all_to_all | solution.py:140
  206.3 57.4 %all-to-all-start.2 = ((f32[32,2,128,128]{3,2,1,0:T(8,128)}), f32[32,2,128,128]{3,2,1,0:T(8,128)}, u32[]{:S(2)}, u32[]{:S(2)}) async-start(f32[32,2,128,128]{3,2,1,0:T(8,128)} %get-tuple-element.6), calls=%async_computation.2 | async-start | bytes 8388608 | tf_op jit(solution)/shard_map/all_to_all | solution.py:145
  215.1 55.8 %collective-permute-start = (bf16[1,128,8192]{1,2,0:T(8,128)(2,1)}, bf16[1,128,8192]{1,2,0:T(8,128)(2,1)S(1)}, u32[]{:S(2)}, u32[]{:S(2)}) collective-permute-start(bf16[1,128,8192]{1,2,0:T(8,128)(2,1)} %bitcast.45), channel_id=1, source_target_pairs={{32,0},{64,32},{96,64},{128,96},{160,128},{192,160},{224,192},{33,... | collective-permute-start | bytes 6291464 | tf_op jit(solution)/shard_map/ppermute | solution.py:20
  266.8 12.3 %collective-permute-start.1 = (bf16[1,128,1024]{1,2,0:T(8,128)(2,1)S(1)}, bf16[1,128,1024]{1,2,0:T(8,128)(2,1)S(1)}, u32[]{:S(2)}, u32[]{:S(2)}) collective-permute-start(bf16[1,128,1024]{1,2,0:T(8,128)(2,1)S(1)} %bitcast.51), channel_id=1, source_target_pairs={{32,0},{64,32},{96,64},{128,96},{160,128},{192,160},{224,192},{33,... | collective-permute-start | bytes 786440 | tf_op jit(solution)/shard_map/ppermute | solution.py:20
  268.8 14.7 %collective-permute-start.2 = (bf16[1,128,1024]{1,2,0:T(8,128)(2,1)S(1)}, bf16[1,128,1024]{1,2,0:T(8,128)(2,1)S(1)}, u32[]{:S(2)}, u32[]{:S(2)}) collective-permute-start(bf16[1,128,1024]{1,2,0:T(8,128)(2,1)S(1)} %bitcast.50), channel_id=1, source_target_pairs={{32,0},{64,32},{96,64},{128,96},{160,128},{192,160},{224,192},{33,... | collective-permute-start | bytes 786440 | tf_op jit(solution)/shard_map/ppermute | solution.py:20

commit v5 on v4

--- a/solution.py
+++ b/solution.py
@@ -54,8 +54,9 @@
             lives.append(live_ref[base + j])
             kc_ref[j * BLOCK:(j + 1) * BLOCK, :] = kv_ref[owners[j], 0, pl.ds(offsets[j], BLOCK), :]
             vc_ref[j * BLOCK:(j + 1) * BLOCK, :] = kv_ref[owners[j], 1, pl.ds(offsets[j], BLOCK), :]
-        q = q_ref[:, i * BLOCK:(i + 1) * BLOCK, :].reshape(-1, HD)
-        g = g_ref[:, i * BLOCK:(i + 1) * BLOCK, :].reshape(-1, HD)
+        owner, within = divmod(i, half)
+        q = q_ref[owner, :, within * BLOCK:(within + 1) * BLOCK, :].reshape(-1, HD)
+        g = g_ref[owner, :, within * BLOCK:(within + 1) * BLOCK, :].reshape(-1, HD)
         kc = kc_ref[...]
         vc = vc_ref[...]
         live_cols = jnp.zeros((1, width), jnp.int32)
@@ -74,7 +75,7 @@
         dprobs = lax.dot_general(g, vc, nt, preferred_element_type=jnp.float32)
         ds_low = (probs * (dprobs - delta)).astype(jnp.bfloat16)
         dq = jnp.dot(ds_low, kc, preferred_element_type=jnp.float32) * scale
-        dq_ref[:, i * BLOCK:(i + 1) * BLOCK, :] = dq.astype(jnp.bfloat16).reshape(-1, BLOCK, HD)
+        dq_ref[owner, :, within * BLOCK:(within + 1) * BLOCK, :] = dq.astype(jnp.bfloat16).reshape(-1, BLOCK, HD)
         dk_slots = lax.dot_general(ds_low, q, tn, preferred_element_type=jnp.float32) * scale
         dv_slots = lax.dot_general(probs_low, g, tn, preferred_element_type=jnp.float32)
         for j in range(slots):
@@ -85,24 +86,24 @@
                 dkv_ref[owners[j], 1, window, :] += dv_slots[j * BLOCK:(j + 1) * BLOCK, :]
 
 
-def block_grads(packed, listed, live, steps=2):
+def block_grads(packed, listed, live, steps=4):
     nblocks, slots = listed.shape
     lanes, _, tok, _ = packed.shape
     half = tok // BLOCK
     per_device = 2
-    rows = BLOCK * steps
+    group = steps // half
     width = slots * BLOCK
     kernel = functools.partial(grads_kernel, slots, steps)
     grid_spec = pltpu.PrefetchScalarGridSpec(
         num_scalar_prefetch=2,
         grid=(nblocks // steps,),
         in_specs=[
-            pl.BlockSpec((None, per_device, rows, HD), lambda b, *_: (b * steps // half, 0, b % (half // steps), 0)),
-            pl.BlockSpec((None, per_device, rows, HD), lambda b, *_: (b * steps // half, 1, b % (half // steps), 0)),
+            pl.BlockSpec((group, per_device, tok, HD), lambda b, *_: (b, 0, 0, 0)),
+            pl.BlockSpec((group, per_device, tok, HD), lambda b, *_: (b, 1, 0, 0)),
             pl.BlockSpec((lanes, 2, tok, HD), lambda b, *_: (0, 2, 0, 0)),
         ],
         out_specs=[
-            pl.BlockSpec((None, per_device, rows, HD), lambda b, *_: (b * steps // half, 0, b % (half // steps), 0)),
+            pl.BlockSpec((group, per_device, tok, HD), lambda b, *_: (b, 0, 0, 0)),
             pl.BlockSpec((lanes, 2, tok, HD), lambda b, *_: (0, 0, 0, 0)),
         ],
         scratch_shapes=[

time: 285 us -> 284 us (level)
  no operation moved by 1% of the time
where the time goes in v5:
time: 284 us
  waiting for transfers between devices  129 us (45%)
  Pallas kernels  67.1 us (24%)
  blocking collectives  34 us (12%)
  local copies, waits for them, and re-layouts  25.3 us (9%)
  starting transfers between devices  19.8 us (7%)
  other arithmetic  7.51 us (3%)
    all_to_all x1, waiting for transfers between devices, body(): lax.all_to_all(send, 'seq', split_axis=0, concat_axis=0, tiled=True)  73.5 us
    pallas_call x1, Pallas kernels, block_grads(): pl.pallas_call(kernel, grid_spec=grid_spec, out_shape=[jax.ShapeDtypeStru...  67.1 us
    all_to_all x1, waiting for transfers between devices, body(): lax.all_to_all(dkv, 'seq', split_axis=0, concat_axis=0, tiled=True)  46.6 us
    all_to_all x1, blocking collectives, body(): lax.all_to_all(dq_heads, 'seq', split_axis=0, concat_axis=0, tiled=True)  34 us
    unnamed x15, local copies, waits for them, and re-layouts  14.1 us
    ppermute x3, waiting for transfers between devices, from_behind(): return lax.ppermute(block, axis, route)  8.93 us
    all_to_all x1, starting transfers between devices, body(): lax.all_to_all(send, 'seq', split_axis=0, concat_axis=0, tiled=True)  7.81 us
    ppermute x3, starting transfers between devices, from_behind(): return lax.ppermute(block, axis, route)  6.06 us
  transfers between devices with their start and end apart: 5, of which 4 were waited for; matrix products, arithmetic and copies ran while one was open for 4% of the time, Pallas kernels for 0%

profile of v5, /device:TPU:98, one launch (start us, length us, event | category | flops | bytes accessed | tf_op | source)
XLA Modules:
  0.0 283.5 jit_solution(7273722146028510620)
XLA Ops:
  0.6 1.0 copy.65
  1.7 1.0 copy.66
  2.7 3.2 %copy.53 = bf16[1,128,8192]{1,2,0:T(8,128)(2,1)S(1)} copy(bf16[1,128,8192]{2,1,0:T(8,128)(2,1)} %param.7) | data formatting | bytes 4194304 | tf_op args[0]
  6.0 2.9 %copy.54 = bf16[128,32,2,128]{3,0,2,1:T(8,128)(2,1)} copy(bf16[128,32,2,128]{0,3,2,1:T(8,128)(2,1)S(1)} %bitcast.39) | data formatting | bytes 4194304 | tf_op jit(solution)/shard_map/reshape;squeeze | solution.py:136
  8.9 3.2 %copy.55 = bf16[1,128,8192]{1,2,0:T(8,128)(2,1)S(1)} copy(bf16[1,128,8192]{2,1,0:T(8,128)(2,1)} %param.10) | data formatting | bytes 4194304 | tf_op args[3]
  12.1 2.9 %copy.56 = bf16[128,32,2,128]{3,0,2,1:T(8,128)(2,1)} copy(bf16[128,32,2,128]{0,3,2,1:T(8,128)(2,1)S(1)} %bitcast.40) | data formatting | bytes 4194304 | tf_op jit(solution)/shard_map/reshape;squeeze | solution.py:137
  15.5 1.1 copy-done
  16.6 4.7 %pad_maximum_fusion = bf16[32,6,128,128]{3,2,1,0:T(8,128)(2,1)} fusion(bf16[32,1,128,128]{3,2,1,0:T(8,128)(2,1)S(1)} %bitcast.43, bf16[32,1,128,128]{3,2,1,0:T(8,128)(2,1)S(1)} %bitcast.44, bf16[32,2,128,128]{3,2,1,0:T(8,128)(2,1)} %bitcast.42, bf16[32,2,128,128]{3,2,1,0:T(8,128)(2,1)S(1)} %bitcast.41), kind=kLoop, calls=%fused_computation | loop fusion | flops 9437184 | bytes 12582912 | tf_op jit(solution)/shard_map/concatenate | solution.py:140
  21.3 7.8 %all-to-all-start = ((bf16[32,6,128,128]{3,2,1,0:T(8,128)(2,1)}), bf16[32,6,128,128]{3,2,1,0:T(8,128)(2,1)}, u32[]{:S(2)}, u32[]{:S(2)}) async-start(bf16[32,6,128,128]{3,2,1,0:T(8,128)(2,1)} %pad_maximum_fusion), calls=%async_computation | async-start | bytes 12582912 | tf_op jit(solution)/shard_map/all_to_all | solution.py:141
  30.8 73.5 %all-to-all-done.q_ref.g_ref.kv_ref = bf16[32,6,128,128]{3,2,1,0:T(8,128)(2,1)} async-done(((bf16[32,6,128,128]{3,2,1,0:T(8,128)(2,1)}), bf16[32,6,128,128]{3,2,1,0:T(8,128)(2,1)}, u32[]{:S(2)}, u32[]{:S(2)}) %all-to-all-start) | async-done | bytes 6291488 | tf_op jit(solution)/shard_map/all_to_all | solution.py:141
  104.3 67.1 %shard_map.94 = (bf16[32,2,128,128]{3,2,1,0:T(8,128)(2,1)}, f32[32,2,128,128]{3,2,1,0:T(8,128)}) custom-call(s32[512]{0:T(512)} %reshape.50.listed_ref, s32[512]{0:T(512)} %reshape.55.live_ref, bf16[32,6,128,128]{3,2,1,0:T(8,128)(2,1)} %all-to-all-done.q_ref.g_ref.kv_ref, bf16[32,6,128,128]{3,2,1,0:T(8,128)(2,1)} %all-to-all-done.q_ref.g_ref.kv_ref, ...), custom_call_target="tpu_custom_call" | custom-call | flops 6442450944 | bytes 18874368 | tf_op jit(solution)/shard_map/pallas_call | solution.py:114
  171.4 34.0 %all_to_all.15 = bf16[32,2,128,128]{3,2,1,0:T(8,128)(2,1)S(1)} all-to-all(bf16[32,2,128,128]{3,2,1,0:T(8,128)(2,1)} %get-tuple-element.5), channel_id=1, replica_groups=mesh['pipe'=8,'seq'=32] {'seq'}, dimensions={0} | all-to-all | bytes 4194304 | tf_op jit(solution)/shard_map/all_to_all | solution.py:144
  205.4 5.9 %all-to-all-start.2 = ((f32[32,2,128,128]{3,2,1,0:T(8,128)}), f32[32,2,128,128]{3,2,1,0:T(8,128)}, u32[]{:S(2)}, u32[]{:S(2)}) async-start(f32[32,2,128,128]{3,2,1,0:T(8,128)} %get-tuple-element.6), calls=%async_computation.2 | async-start | bytes 8388608 | tf_op jit(solution)/shard_map/all_to_all | solution.py:146
  211.3 2.9 %copy.59 = bf16[128,32,2,128]{0,3,2,1:T(8,128)(2,1)} copy(bf16[128,32,2,128]{3,0,2,1:T(8,128)(2,1)S(1)} %bitcast.38) | data formatting | bytes 4194304 | tf_op jit(solution)/shard_map/transpose | solution.py:145
  214.2 2.0 collective-permute-start
  216.2 46.6 %all-to-all-done.2 = f32[32,2,128,128]{3,2,1,0:T(8,128)} async-done(((f32[32,2,128,128]{3,2,1,0:T(8,128)}), f32[32,2,128,128]{3,2,1,0:T(8,128)}, u32[]{:S(2)}, u32[]{:S(2)}) %all-to-all-start.2) | async-done | bytes 4194336 | tf_op jit(solution)/shard_map/all_to_all | solution.py:146
  262.8 2.7 bitcast_reduce_fusion
  265.9 2.0 collective-permute-start.1
  267.9 2.0 collective-permute-start.2
  270.0 2.9 %copy.62 = bf16[1,128,8192]{2,1,0:T(8,128)(2,1)} copy(bf16[1,128,8192]{1,2,0:T(8,128)(2,1)S(1)} %collective-permute-done) | data formatting | bytes 4194304
  272.9 5.3 %collective-permute-done.1 = bf16[1,128,1024]{1,2,0:T(8,128)(2,1)S(1)} collective-permute-done((bf16[1,128,1024]{1,2,0:T(8,128)(2,1)S(1)}, bf16[1,128,1024]{1,2,0:T(8,128)(2,1)S(1)}, u32[]{:S(2)}, u32[]{:S(2)}) %collective-permute-start.1) | collective-permute-done | bytes 262176 | tf_op jit(solution)/shard_map/ppermute | solution.py:20
  278.2 0.8 copy.63
  279.0 3.6 %collective-permute-done.2 = bf16[1,128,1024]{1,2,0:T(8,128)(2,1)S(1)} collective-permute-done((bf16[1,128,1024]{1,2,0:T(8,128)(2,1)S(1)}, bf16[1,128,1024]{1,2,0:T(8,128)(2,1)S(1)}, u32[]{:S(2)}, u32[]{:S(2)}) %collective-permute-start.2) | collective-permute-done | bytes 262176 | tf_op jit(solution)/shard_map/ppermute | solution.py:20
  282.7 0.8 copy.64
  (23 shorter events, 2.6 us)
Async XLA Ops:
  15.0 1.6 copy-start
  21.3 7.8 %copy-start.1 = (s32[64,3]{0,1:T(4,128)S(1)}, s32[64,3]{0,1:T(4,128)}, u32[]{:S(2)}) copy-start(s32[64,3]{0,1:T(4,128)} %param.13) | copy-start | bytes 2308
  21.3 7.8 %copy-start.2 = (s32[64,3]{0,1:T(4,128)S(1)}, s32[64,3]{0,1:T(4,128)}, u32[]{:S(2)}) copy-start(s32[64,3]{0,1:T(4,128)} %param.11) | copy-start | bytes 2308
  21.3 7.8 %copy-start.3 = (s32[64,2]{0,1:T(2,128)S(1)}, s32[64,2]{0,1:T(2,128)}, u32[]{:S(2)}) copy-start(s32[64,2]{0,1:T(2,128)} %param.12) | copy-start | bytes 1540
  21.3 83.0 %all-to-all-start = ((bf16[32,6,128,128]{3,2,1,0:T(8,128)(2,1)}), bf16[32,6,128,128]{3,2,1,0:T(8,128)(2,1)}, u32[]{:S(2)}, u32[]{:S(2)}) async-start(bf16[32,6,128,128]{3,2,1,0:T(8,128)(2,1)} %pad_maximum_fusion), calls=%async_computation | async-start | bytes 12582912 | tf_op jit(solution)/shard_map/all_to_all | solution.py:141
  205.4 57.4 %all-to-all-start.2 = ((f32[32,2,128,128]{3,2,1,0:T(8,128)}), f32[32,2,128,128]{3,2,1,0:T(8,128)}, u32[]{:S(2)}, u32[]{:S(2)}) async-start(f32[32,2,128,128]{3,2,1,0:T(8,128)} %get-tuple-element.6), calls=%async_computation.2 | async-start | bytes 8388608 | tf_op jit(solution)/shard_map/all_to_all | solution.py:146
  214.2 55.8 %collective-permute-start = (bf16[1,128,8192]{1,2,0:T(8,128)(2,1)}, bf16[1,128,8192]{1,2,0:T(8,128)(2,1)S(1)}, u32[]{:S(2)}, u32[]{:S(2)}) collective-permute-start(bf16[1,128,8192]{1,2,0:T(8,128)(2,1)} %bitcast.45), channel_id=1, source_target_pairs={{32,0},{64,32},{96,64},{128,96},{160,128},{192,160},{224,192},{33,... | collective-permute-start | bytes 6291464 | tf_op jit(solution)/shard_map/ppermute | solution.py:20
  265.9 12.3 %collective-permute-start.1 = (bf16[1,128,1024]{1,2,0:T(8,128)(2,1)S(1)}, bf16[1,128,1024]{1,2,0:T(8,128)(2,1)S(1)}, u32[]{:S(2)}, u32[]{:S(2)}) collective-permute-start(bf16[1,128,1024]{1,2,0:T(8,128)(2,1)S(1)} %bitcast.51), channel_id=1, source_target_pairs={{32,0},{64,32},{96,64},{128,96},{160,128},{192,160},{224,192},{33,... | collective-permute-start | bytes 786440 | tf_op jit(solution)/shard_map/ppermute | solution.py:20
  267.9 14.7 %collective-permute-start.2 = (bf16[1,128,1024]{1,2,0:T(8,128)(2,1)S(1)}, bf16[1,128,1024]{1,2,0:T(8,128)(2,1)S(1)}, u32[]{:S(2)}, u32[]{:S(2)}) collective-permute-start(bf16[1,128,1024]{1,2,0:T(8,128)(2,1)S(1)} %bitcast.50), channel_id=1, source_target_pairs={{32,0},{64,32},{96,64},{128,96},{160,128},{192,160},{224,192},{33,... | collective-permute-start | bytes 786440 | tf_op jit(solution)/shard_map/ppermute | solution.py:20

commit v6 on v5

--- a/solution.py
+++ b/solution.py
@@ -29,7 +29,7 @@
     return (listed, jnp.logical_not(repeated))
 
 
-def grads_kernel(slots, steps, listed_ref, live_ref, q_ref, g_ref, kv_ref, dq_ref, dkv_ref, kc_ref, vc_ref):
+def grads_kernel(slots, steps, listed_ref, live_ref, q_ref, g_ref, kv_ref, dq_ref, out_ref, kc_ref, vc_ref, dkv_ref):
     b = pl.program_id(0)
     scale = HD ** (-0.5)
     width = slots * BLOCK
@@ -85,6 +85,10 @@
                 dkv_ref[owners[j], 0, window, :] += dk_slots[j * BLOCK:(j + 1) * BLOCK, :]
                 dkv_ref[owners[j], 1, window, :] += dv_slots[j * BLOCK:(j + 1) * BLOCK, :]
 
+    @pl.when(b == pl.num_programs(0) - 1)
+    def _():
+        out_ref[...] = dkv_ref[...].astype(out_ref.dtype)
+
 
 def block_grads(packed, listed, live, steps=4):
     nblocks, slots = listed.shape
@@ -109,6 +113,7 @@
         scratch_shapes=[
             pltpu.VMEM((width, HD), jnp.bfloat16),
             pltpu.VMEM((width, HD), jnp.bfloat16),
+            pltpu.VMEM((lanes, 2, tok, HD), jnp.float32),
         ],
     )
     return pl.pallas_call(
@@ -116,7 +121,7 @@
         grid_spec=grid_spec,
         out_shape=[
             jax.ShapeDtypeStruct((lanes, per_device, tok, HD), jnp.bfloat16),
-            jax.ShapeDtypeStruct((lanes, 2, tok, HD), jnp.float32),
+            jax.ShapeDtypeStruct((lanes, 2, tok, HD), jnp.bfloat16),
         ],
         compiler_params=pltpu.CompilerParams(dimension_semantics=("arbitrary",)),
         cost_estimate=pl.CostEstimate(
@@ -144,7 +149,8 @@
     dq_parts = lax.all_to_all(dq_heads, "seq", split_axis=0, concat_axis=0, tiled=True)
     dq_tokens = dq_parts.transpose(2, 0, 1, 3)
     dkv_parts = lax.all_to_all(dkv, "seq", split_axis=0, concat_axis=0, tiled=True)
-    dkv_sum = jnp.sum(dkv_parts.reshape(KV, repeat, 2, tok, HD), axis=1).astype(jnp.bfloat16)
+    dkv_wide = dkv_parts.reshape(KV, repeat, 2, tok, HD).astype(jnp.float32)
+    dkv_sum = jnp.sum(dkv_wide, axis=1).astype(jnp.bfloat16)
     dk_tokens = dkv_sum[:, 0].transpose(1, 0, 2)
     dv_tokens = dkv_sum[:, 1].transpose(1, 0, 2)
     dq_flat = dq_tokens.reshape(1, tok, HEADS * HD)

time: 284 us -> 283 us (level)
    all_to_all x1, waiting for transfers between devices: 46.6 us -> 21.9 us  [body(): lax.all_to_all(dkv, 'seq', split_axis=0, concat_axis=0, tiled=True)]
    ppermute x3, waiting for transfers between devices: 8.93 us -> 32.7 us  [from_behind(): return lax.ppermute(block, axis, route)]
  transfers between devices with their start and end apart: 5 -> 5, of which waited for: 4 -> 4; matrix products, arithmetic and copies ran while one was open for 4% -> 3% of each run, Pallas kernels for 0% -> 0%
where the time goes in v6:
time: 283 us; the launch traced here: 282 us
  waiting for transfers between devices  128 us (45%)
  Pallas kernels  66.7 us (24%)
  blocking collectives  34.7 us (12%)
  local copies, waits for them, and re-layouts  27.6 us (10%)
  starting transfers between devices  18.9 us (7%)
  other arithmetic  5.19 us (2%)
    all_to_all x1, waiting for transfers between devices, body(): lax.all_to_all(send, 'seq', split_axis=0, concat_axis=0, tiled=True)  73.5 us
    pallas_call x1, Pallas kernels, block_grads(): pl.pallas_call(kernel, grid_spec=grid_spec, out_shape=[jax.ShapeDtypeStru...  66.7 us
    all_to_all x1, blocking collectives, body(): lax.all_to_all(dq_heads, 'seq', split_axis=0, concat_axis=0, tiled=True)  34.7 us
    ppermute x3, waiting for transfers between devices, from_behind(): return lax.ppermute(block, axis, route)  32.7 us
    all_to_all x1, waiting for transfers between devices, body(): lax.all_to_all(dkv, 'seq', split_axis=0, concat_axis=0, tiled=True)  21.9 us
    unnamed x15, local copies, waits for them, and re-layouts  15.3 us
    all_to_all x1, starting transfers between devices, body(): lax.all_to_all(send, 'seq', split_axis=0, concat_axis=0, tiled=True)  7.81 us
    ppermute x3, starting transfers between devices, from_behind(): return lax.ppermute(block, axis, route)  6.01 us
  transfers between devices with their start and end apart: 5, of which 4 were waited for; matrix products, arithmetic and copies ran while one was open for 3% of the time, Pallas kernels for 0%

profile of v6, /device:TPU:98, one launch (start us, length us, event | category | flops | bytes accessed | tf_op | source)
XLA Modules:
  0.0 282.3 jit_solution(11154174575448656014)
XLA Ops:
  0.6 1.0 copy.65
  1.7 1.0 copy.66
  2.7 3.2 %copy.53 = bf16[1,128,8192]{1,2,0:T(8,128)(2,1)S(1)} copy(bf16[1,128,8192]{2,1,0:T(8,128)(2,1)} %param.7) | data formatting | bytes 4194304 | tf_op args[0]
  6.0 2.9 %copy.54 = bf16[128,32,2,128]{3,0,2,1:T(8,128)(2,1)} copy(bf16[128,32,2,128]{0,3,2,1:T(8,128)(2,1)S(1)} %bitcast.39) | data formatting | bytes 4194304 | tf_op jit(solution)/shard_map/reshape;squeeze | solution.py:141
  8.9 3.2 %copy.55 = bf16[1,128,8192]{1,2,0:T(8,128)(2,1)S(1)} copy(bf16[1,128,8192]{2,1,0:T(8,128)(2,1)} %param.10) | data formatting | bytes 4194304 | tf_op args[3]
  12.1 2.9 %copy.56 = bf16[128,32,2,128]{3,0,2,1:T(8,128)(2,1)} copy(bf16[128,32,2,128]{0,3,2,1:T(8,128)(2,1)S(1)} %bitcast.40) | data formatting | bytes 4194304 | tf_op jit(solution)/shard_map/reshape;squeeze | solution.py:142
  15.5 1.1 copy-done
  16.6 4.7 %pad_maximum_fusion = bf16[32,6,128,128]{3,2,1,0:T(8,128)(2,1)} fusion(bf16[32,1,128,128]{3,2,1,0:T(8,128)(2,1)S(1)} %bitcast.43, bf16[32,1,128,128]{3,2,1,0:T(8,128)(2,1)S(1)} %bitcast.44, bf16[32,2,128,128]{3,2,1,0:T(8,128)(2,1)} %bitcast.42, bf16[32,2,128,128]{3,2,1,0:T(8,128)(2,1)S(1)} %bitcast.41), kind=kLoop, calls=%fused_computation | loop fusion | flops 9437184 | bytes 12582912 | tf_op jit(solution)/shard_map/concatenate | solution.py:145
  21.3 7.8 %all-to-all-start = ((bf16[32,6,128,128]{3,2,1,0:T(8,128)(2,1)}), bf16[32,6,128,128]{3,2,1,0:T(8,128)(2,1)}, u32[]{:S(2)}, u32[]{:S(2)}) async-start(bf16[32,6,128,128]{3,2,1,0:T(8,128)(2,1)} %pad_maximum_fusion), calls=%async_computation | async-start | bytes 12582912 | tf_op jit(solution)/shard_map/all_to_all | solution.py:146
  29.4 0.7 reshape.55.live_ref
  30.8 73.5 %all-to-all-done.q_ref.g_ref.kv_ref = bf16[32,6,128,128]{3,2,1,0:T(8,128)(2,1)} async-done(((bf16[32,6,128,128]{3,2,1,0:T(8,128)(2,1)}), bf16[32,6,128,128]{3,2,1,0:T(8,128)(2,1)}, u32[]{:S(2)}, u32[]{:S(2)}) %all-to-all-start) | async-done | bytes 6291488 | tf_op jit(solution)/shard_map/all_to_all | solution.py:146
  104.3 66.7 %shard_map.94 = (bf16[32,2,128,128]{3,2,1,0:T(8,128)(2,1)}, bf16[32,2,128,128]{3,2,1,0:T(8,128)(2,1)}) custom-call(s32[512]{0:T(512)} %reshape.50.listed_ref, s32[512]{0:T(512)} %reshape.55.live_ref, bf16[32,6,128,128]{3,2,1,0:T(8,128)(2,1)} %all-to-all-done.q_ref.g_ref.kv_ref, bf16[32,6,128,128]{3,2,1,0:T(8,128)(2,1)} %all-to-all-done.q_ref.g_ref.kv_ref, ...), custom_call_target="tpu_custom_call" | custom-call | flops 6442450944 | bytes 18874368 | tf_op jit(solution)/shard_map/pallas_call | solution.py:119
  171.0 34.7 %all_to_all.15 = bf16[32,2,128,128]{3,2,1,0:T(8,128)(2,1)} all-to-all(bf16[32,2,128,128]{3,2,1,0:T(8,128)(2,1)} %get-tuple-element.5), channel_id=1, replica_groups=mesh['pipe'=8,'seq'=32] {'seq'}, dimensions={0} | all-to-all | bytes 4194304 | tf_op jit(solution)/shard_map/all_to_all | solution.py:149
  205.8 5.1 %all-to-all-start.2 = ((bf16[32,2,128,128]{3,2,1,0:T(8,128)(2,1)}), bf16[32,2,128,128]{3,2,1,0:T(8,128)(2,1)S(1)}, u32[]{:S(2)}, u32[]{:S(2)}) async-start(bf16[32,2,128,128]{3,2,1,0:T(8,128)(2,1)} %get-tuple-element.6), calls=%async_computation.2 | async-start | bytes 4194304 | tf_op jit(solution)/shard_map/all_to_all | solution.py:151
  210.9 4.1 %copy.59 = bf16[128,32,2,128]{0,3,2,1:T(8,128)(2,1)} copy(bf16[128,32,2,128]{3,0,2,1:T(8,128)(2,1)} %bitcast.38) | data formatting | bytes 4194304 | tf_op jit(solution)/shard_map/transpose | solution.py:150
  215.0 2.0 collective-permute-start
  217.0 21.9 %all-to-all-done.2 = bf16[32,2,128,128]{3,2,1,0:T(8,128)(2,1)S(1)} async-done(((bf16[32,2,128,128]{3,2,1,0:T(8,128)(2,1)}), bf16[32,2,128,128]{3,2,1,0:T(8,128)(2,1)S(1)}, u32[]{:S(2)}, u32[]{:S(2)}) %all-to-all-start.2) | async-done | bytes 2097184 | tf_op jit(solution)/shard_map/all_to_all | solution.py:151
  239.7 2.0 collective-permute-start.1
  241.8 2.0 collective-permute-start.2
  243.8 28.7 %collective-permute-done.1 = bf16[1,128,1024]{1,2,0:T(8,128)(2,1)S(1)} collective-permute-done((bf16[1,128,1024]{1,2,0:T(8,128)(2,1)S(1)}, bf16[1,128,1024]{1,2,0:T(8,128)(2,1)S(1)}, u32[]{:S(2)}, u32[]{:S(2)}) %collective-permute-start.1) | collective-permute-done | bytes 262176 | tf_op jit(solution)/shard_map/ppermute | solution.py:20
  272.4 0.8 copy.63
  273.3 4.1 %collective-permute-done.2 = bf16[1,128,1024]{1,2,0:T(8,128)(2,1)S(1)} collective-permute-done((bf16[1,128,1024]{1,2,0:T(8,128)(2,1)S(1)}, bf16[1,128,1024]{1,2,0:T(8,128)(2,1)S(1)}, u32[]{:S(2)}, u32[]{:S(2)}) %collective-permute-start.2) | collective-permute-done | bytes 262176 | tf_op jit(solution)/shard_map/ppermute | solution.py:20
  277.3 0.8 copy.64
  278.2 4.1 %copy.62 = bf16[1,128,8192]{2,1,0:T(8,128)(2,1)} copy(bf16[1,128,8192]{1,2,0:T(8,128)(2,1)} %collective-permute-done) | data formatting | bytes 4194304
  (23 shorter events, 2.3 us)
Async XLA Ops:
  15.0 1.6 copy-start
  21.3 7.8 %copy-start.1 = (s32[64,3]{0,1:T(4,128)S(1)}, s32[64,3]{0,1:T(4,128)}, u32[]{:S(2)}) copy-start(s32[64,3]{0,1:T(4,128)} %param.13) | copy-start | bytes 2308
  21.3 7.8 %copy-start.2 = (s32[64,3]{0,1:T(4,128)S(1)}, s32[64,3]{0,1:T(4,128)}, u32[]{:S(2)}) copy-start(s32[64,3]{0,1:T(4,128)} %param.11) | copy-start | bytes 2308
  21.3 7.8 %copy-start.3 = (s32[64,2]{0,1:T(2,128)S(1)}, s32[64,2]{0,1:T(2,128)}, u32[]{:S(2)}) copy-start(s32[64,2]{0,1:T(2,128)} %param.12) | copy-start | bytes 1540
  21.3 83.0 %all-to-all-start = ((bf16[32,6,128,128]{3,2,1,0:T(8,128)(2,1)}), bf16[32,6,128,128]{3,2,1,0:T(8,128)(2,1)}, u32[]{:S(2)}, u32[]{:S(2)}) async-start(bf16[32,6,128,128]{3,2,1,0:T(8,128)(2,1)} %pad_maximum_fusion), calls=%async_computation | async-start | bytes 12582912 | tf_op jit(solution)/shard_map/all_to_all | solution.py:146
  205.8 33.2 %all-to-all-start.2 = ((bf16[32,2,128,128]{3,2,1,0:T(8,128)(2,1)}), bf16[32,2,128,128]{3,2,1,0:T(8,128)(2,1)S(1)}, u32[]{:S(2)}, u32[]{:S(2)}) async-start(bf16[32,2,128,128]{3,2,1,0:T(8,128)(2,1)} %get-tuple-element.6), calls=%async_computation.2 | async-start | bytes 4194304 | tf_op jit(solution)/shard_map/all_to_all | solution.py:151
  215.0 63.2 %collective-permute-start = (bf16[1,128,8192]{1,2,0:T(8,128)(2,1)}, bf16[1,128,8192]{1,2,0:T(8,128)(2,1)}, u32[]{:S(2)}, u32[]{:S(2)}) collective-permute-start(bf16[1,128,8192]{1,2,0:T(8,128)(2,1)} %bitcast.45), channel_id=1, source_target_pairs={{32,0},{64,32},{96,64},{128,96},{160,128},{192,160},{224,192},{33,... | collective-permute-start | bytes 6291464 | tf_op jit(solution)/shard_map/ppermute | solution.py:20
  239.7 32.7 %collective-permute-start.1 = (bf16[1,128,1024]{1,2,0:T(8,128)(2,1)S(1)}, bf16[1,128,1024]{1,2,0:T(8,128)(2,1)S(1)}, u32[]{:S(2)}, u32[]{:S(2)}) collective-permute-start(bf16[1,128,1024]{1,2,0:T(8,128)(2,1)S(1)} %bitcast.51), channel_id=1, source_target_pairs={{32,0},{64,32},{96,64},{128,96},{160,128},{192,160},{224,192},{33,... | collective-permute-start | bytes 786440 | tf_op jit(solution)/shard_map/ppermute | solution.py:20
  241.8 35.6 %collective-permute-start.2 = (bf16[1,128,1024]{1,2,0:T(8,128)(2,1)S(1)}, bf16[1,128,1024]{1,2,0:T(8,128)(2,1)S(1)}, u32[]{:S(2)}, u32[]{:S(2)}) collective-permute-start(bf16[1,128,1024]{1,2,0:T(8,128)(2,1)S(1)} %bitcast.50), channel_id=1, source_target_pairs={{32,0},{64,32},{96,64},{128,96},{160,128},{192,160},{224,192},{33,... | collective-permute-start | bytes 786440 | tf_op jit(solution)/shard_map/ppermute | solution.py:20

commit v7 on v6

--- a/solution.py
+++ b/solution.py
@@ -6,6 +6,7 @@
 from jax.experimental import pallas as pl
 from jax.experimental.pallas import tpu as pltpu
 from jax.sharding import PartitionSpec as P
+
 
 HEADS = 64
 KV = 8
@@ -29,7 +30,11 @@
     return (listed, jnp.logical_not(repeated))
 
 
-def grads_kernel(slots, steps, listed_ref, live_ref, q_ref, g_ref, kv_ref, dq_ref, out_ref, kc_ref, vc_ref, dkv_ref):
+def grads_kernel(slots, steps, part, chained, listed_ref, live_ref, q_ref, g_ref, kv_ref, *refs):
+    if chained:
+        acc_in_ref, dq_ref, out_ref, kc_ref, vc_ref, dkv_ref = refs
+    else:
+        dq_ref, out_ref, kc_ref, vc_ref, dkv_ref = refs
     b = pl.program_id(0)
     scale = HD ** (-0.5)
     width = slots * BLOCK
@@ -37,13 +42,16 @@
 
     @pl.when(b == 0)
     def _():
-        dkv_ref[...] = jnp.zeros(dkv_ref.shape, dkv_ref.dtype)
+        if chained:
+            dkv_ref[...] = acc_in_ref[...]
+        else:
+            dkv_ref[...] = jnp.zeros(dkv_ref.shape, dkv_ref.dtype)
 
     col = lax.broadcasted_iota(jnp.int32, (1, width), 1)
     nt = (((1,), (1,)), ((), ()))
     tn = (((0,), (0,)), ((), ()))
     for i in range(steps):
-        base = (b * steps + i) * slots
+        base = ((b * steps + i) * half + part) * slots
         owners = []
         offsets = []
         lives = []
@@ -54,9 +62,8 @@
             lives.append(live_ref[base + j])
             kc_ref[j * BLOCK:(j + 1) * BLOCK, :] = kv_ref[owners[j], 0, pl.ds(offsets[j], BLOCK), :]
             vc_ref[j * BLOCK:(j + 1) * BLOCK, :] = kv_ref[owners[j], 1, pl.ds(offsets[j], BLOCK), :]
-        owner, within = divmod(i, half)
-        q = q_ref[owner, :, within * BLOCK:(within + 1) * BLOCK, :].reshape(-1, HD)
-        g = g_ref[owner, :, within * BLOCK:(within + 1) * BLOCK, :].reshape(-1, HD)
+        q = q_ref[i].reshape(-1, HD)
+        g = g_ref[i].reshape(-1, HD)
         kc = kc_ref[...]
         vc = vc_ref[...]
         live_cols = jnp.zeros((1, width), jnp.int32)
@@ -75,7 +82,7 @@
         dprobs = lax.dot_general(g, vc, nt, preferred_element_type=jnp.float32)
         ds_low = (probs * (dprobs - delta)).astype(jnp.bfloat16)
         dq = jnp.dot(ds_low, kc, preferred_element_type=jnp.float32) * scale
-        dq_ref[owner, :, within * BLOCK:(within + 1) * BLOCK, :] = dq.astype(jnp.bfloat16).reshape(-1, BLOCK, HD)
+        dq_ref[i] = dq.astype(jnp.bfloat16).reshape(dq_ref.shape[1:])
         dk_slots = lax.dot_general(ds_low, q, tn, preferred_element_type=jnp.float32) * scale
         dv_slots = lax.dot_general(probs_low, g, tn, preferred_element_type=jnp.float32)
         for j in range(slots):
@@ -90,25 +97,30 @@
         out_ref[...] = dkv_ref[...].astype(out_ref.dtype)
 
 
-def block_grads(packed, listed, live, steps=4):
+def block_grads(packed, listed, live, part, acc_in=None, out_dtype=jnp.float32, steps=4):
     nblocks, slots = listed.shape
     lanes, _, tok, _ = packed.shape
-    half = tok // BLOCK
     per_device = 2
-    group = steps // half
     width = slots * BLOCK
-    kernel = functools.partial(grads_kernel, slots, steps)
+    chained = acc_in is not None
+    kernel = functools.partial(grads_kernel, slots, steps, part, chained)
+    whole = lambda b, *_: (0, 0, 0, 0)
+    in_specs = [
+        pl.BlockSpec((steps, per_device, BLOCK, HD), lambda b, *_: (b, 0, part, 0)),
+        pl.BlockSpec((steps, per_device, BLOCK, HD), lambda b, *_: (b, 1, part, 0)),
+        pl.BlockSpec((lanes, 2, tok, HD), lambda b, *_: (0, 2, 0, 0)),
+    ]
+    operands = [packed, packed, packed]
+    if chained:
+        in_specs.append(pl.BlockSpec((lanes, 2, tok, HD), whole))
+        operands.append(acc_in)
     grid_spec = pltpu.PrefetchScalarGridSpec(
         num_scalar_prefetch=2,
-        grid=(nblocks // steps,),
-        in_specs=[
-            pl.BlockSpec((group, per_device, tok, HD), lambda b, *_: (b, 0, 0, 0)),
-            pl.BlockSpec((group, per_device, tok, HD), lambda b, *_: (b, 1, 0, 0)),
-            pl.BlockSpec((lanes, 2, tok, HD), lambda b, *_: (0, 2, 0, 0)),
-        ],
+        grid=(lanes // steps,),
+        in_specs=in_specs,
         out_specs=[
-            pl.BlockSpec((group, per_device, tok, HD), lambda b, *_: (b, 0, 0, 0)),
-            pl.BlockSpec((lanes, 2, tok, HD), lambda b, *_: (0, 0, 0, 0)),
+            pl.BlockSpec((steps, per_device, BLOCK, HD), lambda b, *_: (b, 0, 0, 0)),
+            pl.BlockSpec((lanes, 2, tok, HD), whole),
         ],
         scratch_shapes=[
             pltpu.VMEM((width, HD), jnp.bfloat16),
@@ -120,17 +132,17 @@
         kernel,
         grid_spec=grid_spec,
         out_shape=[
-            jax.ShapeDtypeStruct((lanes, per_device, tok, HD), jnp.bfloat16),
-            jax.ShapeDtypeStruct((lanes, 2, tok, HD), jnp.bfloat16),
+            jax.ShapeDtypeStruct((lanes, per_device, BLOCK, HD), jnp.bfloat16),
+            jax.ShapeDtypeStruct((lanes, 2, tok, HD), out_dtype),
         ],
         compiler_params=pltpu.CompilerParams(dimension_semantics=("arbitrary",)),
         cost_estimate=pl.CostEstimate(
-            flops=12 * nblocks * BLOCK * per_device * width * HD,
-            transcendentals=nblocks * BLOCK * per_device * width,
-            bytes_accessed=6 * packed.size,
+            flops=6 * nblocks * BLOCK * per_device * width * HD,
+            transcendentals=nblocks * BLOCK * per_device * width // 2,
+            bytes_accessed=3 * packed.size,
         ),
         interpret=INTERPRET,
-    )(listed.reshape(-1), live.reshape(-1).astype(jnp.int32), packed, packed, packed)
+    )(listed.reshape(-1), live.reshape(-1).astype(jnp.int32), *operands)
 
 
 def body(queries, keys, values, out_grad, window_blocks, global_blocks, random_blocks):
@@ -145,18 +157,22 @@
     send = jnp.concatenate([q_lead, g_lead, k_lead, v_lead], axis=1)
     packed = lax.all_to_all(send, "seq", split_axis=0, concat_axis=0, tiled=True)
     listed, live = block_lists(window_blocks, global_blocks, random_blocks)
-    dq_heads, dkv = block_grads(packed, listed, live)
-    dq_parts = lax.all_to_all(dq_heads, "seq", split_axis=0, concat_axis=0, tiled=True)
-    dq_tokens = dq_parts.transpose(2, 0, 1, 3)
+    dq_first, acc = block_grads(packed, listed, live, 0)
+    dq_first_next = from_behind(dq_first, "pipe", -1)
+    dq_second, dkv = block_grads(packed, listed, live, 1, acc, jnp.bfloat16)
+    dq_second_next = from_behind(dq_second, "pipe", -1)
     dkv_parts = lax.all_to_all(dkv, "seq", split_axis=0, concat_axis=0, tiled=True)
     dkv_wide = dkv_parts.reshape(KV, repeat, 2, tok, HD).astype(jnp.float32)
     dkv_sum = jnp.sum(dkv_wide, axis=1).astype(jnp.bfloat16)
     dk_tokens = dkv_sum[:, 0].transpose(1, 0, 2)
     dv_tokens = dkv_sum[:, 1].transpose(1, 0, 2)
-    dq_flat = dq_tokens.reshape(1, tok, HEADS * HD)
     dk_flat = dk_tokens.reshape(1, tok, KV * HD)
     dv_flat = dv_tokens.reshape(1, tok, KV * HD)
-    return from_behind((dq_flat, dk_flat, dv_flat), "pipe", -1)
+    dk_next, dv_next = from_behind((dk_flat, dv_flat), "pipe", -1)
+    dq_heads = jnp.concatenate([dq_first_next, dq_second_next], axis=2)
+    dq_parts = lax.all_to_all(dq_heads, "seq", split_axis=0, concat_axis=0, tiled=True)
+    dq_next = dq_parts.transpose(2, 0, 1, 3).reshape(1, tok, HEADS * HD)
+    return dq_next, dk_next, dv_next
 
 
 def solution(mesh):
@@ -170,4 +186,5 @@
         P(),
     )
     out_specs = (P("pipe", "seq", None), P("pipe", "seq", None), P("pipe", "seq", None))
+
     return jax.shard_map(body, mesh=mesh, in_specs=in_specs, out_specs=out_specs, check_vma=False)

time: 283 us -> 281 us (level)
  blocking collectives: 34.7 us -> 0 us
  waiting for transfers between devices: 128 us -> 142 us
  starting transfers between devices: 18.9 us -> 30 us
  Pallas kernels: 66.7 us -> 73.1 us
    all_to_all x1 -> x0, blocking collectives: 34.7 us -> none  [body(): lax.all_to_all(dq_heads, 'seq', split_axis=0, concat_axis=0, tiled=True)]
    ppermute x3 -> x4, waiting for transfers between devices: 32.7 us -> 59.4 us  [from_behind(): return lax.ppermute(block, axis, route)]
    all_to_all x1, waiting for transfers between devices: 21.9 us -> 0.01 us  [body(): lax.all_to_all(dkv, 'seq', split_axis=0, concat_axis=0, tiled=True)]
    all_to_all x0 -> x1, waiting for transfers between devices: none -> 9.27 us  [body(): lax.all_to_all(dq_heads, 'seq', split_axis=0, concat_axis=0, tiled=True)]
    all_to_all x0 -> x1, starting transfers between devices: none -> 7.54 us  [body(): lax.all_to_all(dq_heads, 'seq', split_axis=0, concat_axis=0, tiled=True)]
    pallas_call x1 -> x2, Pallas kernels: 66.7 us -> 73.1 us  [block_grads(): pl.pallas_call(kernel, grid_spec=grid_spec, out_shape=[jax.ShapeDtypeStru...]
    ppermute x3 -> x4, starting transfers between devices: 6.01 us -> 7.87 us  [from_behind(): return lax.ppermute(block, axis, route)]
    unnamed x15 -> x17, local copies, waits for them, and re-layouts: 15.3 us -> 14.2 us
  transfers between devices with their start and end apart: 5 -> 7, of which waited for: 4 -> 6; matrix products, arithmetic and copies ran while one was open for 3% -> 2% of each run, Pallas kernels for 0% -> 0%
where the time goes in v7:
time: 281 us; the launch traced here: 279 us
  waiting for transfers between devices  142 us (51%)
  Pallas kernels  73.1 us (26%)
  starting transfers between devices  30 us (11%)
  local copies, waits for them, and re-layouts  25.6 us (9%)
  other arithmetic  6.69 us (2%)
    all_to_all x1, waiting for transfers between devices, body(): lax.all_to_all(send, 'seq', split_axis=0, concat_axis=0, tiled=True)  73.5 us
    pallas_call x2, Pallas kernels, block_grads(): pl.pallas_call(kernel, grid_spec=grid_spec, out_shape=[jax.ShapeDtypeStru...  73.1 us
    ppermute x4, waiting for transfers between devices, from_behind(): return lax.ppermute(block, axis, route)  59.4 us
    unnamed x17, local copies, waits for them, and re-layouts  14.2 us
    all_to_all x1, waiting for transfers between devices, body(): lax.all_to_all(dq_heads, 'seq', split_axis=0, concat_axis=0, tiled=True)  9.27 us
    ppermute x4, starting transfers between devices, from_behind(): return lax.ppermute(block, axis, route)  7.87 us
    all_to_all x1, starting transfers between devices, body(): lax.all_to_all(send, 'seq', split_axis=0, concat_axis=0, tiled=True)  7.81 us
    all_to_all x1, starting transfers between devices, body(): lax.all_to_all(dq_heads, 'seq', split_axis=0, concat_axis=0, tiled=True)  7.54 us
  transfers between devices with their start and end apart: 7, of which 6 were waited for; matrix products, arithmetic and copies ran while one was open for 2% of the time, Pallas kernels for 0%

profile of v7, /device:TPU:98, one launch (start us, length us, event | category | flops | bytes accessed | tf_op | source)
XLA Modules:
  0.0 278.5 jit_solution(10030638242929860017)
XLA Ops:
  2.7 3.2 %copy.53 = bf16[1,128,8192]{1,2,0:T(8,128)(2,1)S(1)} copy(bf16[1,128,8192]{2,1,0:T(8,128)(2,1)} %param.7) | data formatting | bytes 4194304 | tf_op args[0]
  6.0 2.9 %copy.54 = bf16[128,32,2,128]{3,0,2,1:T(8,128)(2,1)} copy(bf16[128,32,2,128]{0,3,2,1:T(8,128)(2,1)S(1)} %bitcast.39) | data formatting | bytes 4194304 | tf_op jit(solution)/shard_map/reshape;squeeze | solution.py:153
  8.9 3.2 %copy.55 = bf16[1,128,8192]{1,2,0:T(8,128)(2,1)S(1)} copy(bf16[1,128,8192]{2,1,0:T(8,128)(2,1)} %param.10) | data formatting | bytes 4194304 | tf_op args[3]
  12.1 2.9 %copy.56 = bf16[128,32,2,128]{3,0,2,1:T(8,128)(2,1)} copy(bf16[128,32,2,128]{0,3,2,1:T(8,128)(2,1)S(1)} %bitcast.40) | data formatting | bytes 4194304 | tf_op jit(solution)/shard_map/reshape;squeeze | solution.py:154
  15.5 1.1 copy-done
  16.6 4.7 %pad_maximum_fusion = bf16[32,6,128,128]{3,2,1,0:T(8,128)(2,1)} fusion(bf16[32,1,128,128]{3,2,1,0:T(8,128)(2,1)S(1)} %bitcast.43, bf16[32,1,128,128]{3,2,1,0:T(8,128)(2,1)S(1)} %bitcast.44, bf16[32,2,128,128]{3,2,1,0:T(8,128)(2,1)} %bitcast.42, bf16[32,2,128,128]{3,2,1,0:T(8,128)(2,1)S(1)} %bitcast.41), kind=kLoop, calls=%fused_computation | loop fusion | flops 9437184 | bytes 12582912 | tf_op jit(solution)/shard_map/concatenate | solution.py:157
  21.3 7.8 %all-to-all-start = ((bf16[32,6,128,128]{3,2,1,0:T(8,128)(2,1)}), bf16[32,6,128,128]{3,2,1,0:T(8,128)(2,1)}, u32[]{:S(2)}, u32[]{:S(2)}) async-start(bf16[32,6,128,128]{3,2,1,0:T(8,128)(2,1)} %pad_maximum_fusion), calls=%async_computation | async-start | bytes 12582912 | tf_op jit(solution)/shard_map/all_to_all | solution.py:158
  30.8 73.5 %all-to-all-done.q_ref.g_ref.kv_ref = bf16[32,6,128,128]{3,2,1,0:T(8,128)(2,1)} async-done(((bf16[32,6,128,128]{3,2,1,0:T(8,128)(2,1)}), bf16[32,6,128,128]{3,2,1,0:T(8,128)(2,1)}, u32[]{:S(2)}, u32[]{:S(2)}) %all-to-all-start) | async-done | bytes 6291488 | tf_op jit(solution)/shard_map/all_to_all | solution.py:158
  104.3 36.3 %shard_map.94 = (bf16[32,2,64,128]{3,2,1,0:T(8,128)(2,1)}, f32[32,2,128,128]{3,2,1,0:T(8,128)}) custom-call(s32[512]{0:T(512)} %reshape.52.listed_ref, s32[512]{0:T(512)} %reshape.57.live_ref, bf16[32,6,128,128]{3,2,1,0:T(8,128)(2,1)} %all-to-all-done.q_ref.g_ref.kv_ref, bf16[32,6,128,128]{3,2,1,0:T(8,128)(2,1)} %all-to-all-done.q_ref.g_ref.kv_ref, ...), custom_call_target="tpu_custom_call" | custom-call | flops 3221225472 | bytes 9437184 | tf_op jit(solution)/shard_map/pallas_call | solution.py:131
  140.6 36.8 %shard_map.95 = (bf16[32,2,64,128]{3,2,1,0:T(8,128)(2,1)}, bf16[32,2,128,128]{3,2,1,0:T(8,128)(2,1)}) custom-call(s32[512]{0:T(512)} %reshape.52.listed_ref, s32[512]{0:T(512)} %reshape.57.live_ref, bf16[32,6,128,128]{3,2,1,0:T(8,128)(2,1)} %all-to-all-done.q_ref.g_ref.kv_ref, bf16[32,6,128,128]{3,2,1,0:T(8,128)(2,1)} %all-to-all-done.q_ref.g_ref.kv_ref, ...), custom_call_target="tpu_custom_call" | custom-call | flops 3221225472 | bytes 9437184 | tf_op jit(solution)/shard_map/pallas_call | solution.py:131
  177.4 6.8 %all-to-all-start.2 = ((bf16[32,2,128,128]{3,2,1,0:T(8,128)(2,1)}), bf16[32,2,128,128]{3,2,1,0:T(8,128)(2,1)S(1)}, u32[]{:S(2)}, u32[]{:S(2)}) async-start(bf16[32,2,128,128]{3,2,1,0:T(8,128)(2,1)} %get-tuple-element.10), calls=%async_computation.2 | async-start | bytes 4194304 | tf_op jit(solution)/shard_map/all_to_all | solution.py:164
  184.2 2.0 collective-permute-start.1
  186.2 2.0 collective-permute-start
  188.3 25.3 %collective-permute-done.1 = bf16[32,2,64,128]{3,2,1,0:T(8,128)(2,1)S(1)} collective-permute-done((bf16[32,2,64,128]{3,2,1,0:T(8,128)(2,1)}, bf16[32,2,64,128]{3,2,1,0:T(8,128)(2,1)S(1)}, u32[]{:S(2)}, u32[]{:S(2)}) %collective-permute-start.1) | collective-permute-done | bytes 1048608 | tf_op jit(solution)/shard_map/ppermute | solution.py:21
  213.6 21.8 %collective-permute-done = bf16[32,2,64,128]{3,2,1,0:T(8,128)(2,1)S(1)} collective-permute-done((bf16[32,2,64,128]{3,2,1,0:T(8,128)(2,1)S(1)}, bf16[32,2,64,128]{3,2,1,0:T(8,128)(2,1)S(1)}, u32[]{:S(2)}, u32[]{:S(2)}) %collective-permute-start) | collective-permute-done | bytes 1048608 | tf_op jit(solution)/shard_map/ppermute | solution.py:21
  235.4 1.5 pad_maximum_fusion.1
  236.9 7.5 %all-to-all-start.1 = ((bf16[32,2,128,128]{3,2,1,0:T(8,128)(2,1)}), bf16[32,2,128,128]{3,2,1,0:T(8,128)(2,1)}, u32[]{:S(2)}, u32[]{:S(2)}) async-start(bf16[32,2,128,128]{3,2,1,0:T(8,128)(2,1)} %pad_maximum_fusion.1), calls=%async_computation.1 | async-start | bytes 4194304 | tf_op jit(solution)/shard_map/all_to_all | solution.py:173
  245.2 1.9 collective-permute-start.2
  247.2 1.9 collective-permute-start.3
  249.1 8.4 %collective-permute-done.2 = bf16[1,128,1024]{1,2,0:T(8,128)(2,1)S(1)} collective-permute-done((bf16[1,128,1024]{1,2,0:T(8,128)(2,1)S(1)}, bf16[1,128,1024]{1,2,0:T(8,128)(2,1)S(1)}, u32[]{:S(2)}, u32[]{:S(2)}) %collective-permute-start.2) | collective-permute-done | bytes 262176 | tf_op jit(solution)/shard_map/ppermute | solution.py:21
  258.4 3.9 %collective-permute-done.3 = bf16[1,128,1024]{1,2,0:T(8,128)(2,1)S(1)} collective-permute-done((bf16[1,128,1024]{1,2,0:T(8,128)(2,1)S(1)}, bf16[1,128,1024]{1,2,0:T(8,128)(2,1)S(1)}, u32[]{:S(2)}, u32[]{:S(2)}) %collective-permute-start.3) | collective-permute-done | bytes 262176 | tf_op jit(solution)/shard_map/ppermute | solution.py:21
  263.1 9.3 %all-to-all-done.1 = bf16[32,2,128,128]{3,2,1,0:T(8,128)(2,1)} async-done(((bf16[32,2,128,128]{3,2,1,0:T(8,128)(2,1)}), bf16[32,2,128,128]{3,2,1,0:T(8,128)(2,1)}, u32[]{:S(2)}, u32[]{:S(2)}) %all-to-all-start.1) | async-done | bytes 2097184 | tf_op jit(solution)/shard_map/all_to_all | solution.py:173
  272.4 3.2 %copy.59 = bf16[128,32,2,128]{0,3,2,1:T(8,128)(2,1)S(1)} copy(bf16[128,32,2,128]{3,0,2,1:T(8,128)(2,1)} %bitcast.10) | data formatting | bytes 4194304 | tf_op jit(solution)/shard_map/transpose | solution.py:174
  275.6 2.9 %copy.62 = bf16[1,128,8192]{2,1,0:T(8,128)(2,1)} copy(bf16[1,128,8192]{1,2,0:T(8,128)(2,1)S(1)} %bitcast.38) | data formatting | bytes 4194304
  (30 shorter events, 6.6 us)
Async XLA Ops:
  15.0 1.6 copy-start
  21.3 7.8 %copy-start.1 = (s32[64,3]{0,1:T(4,128)S(1)}, s32[64,3]{0,1:T(4,128)}, u32[]{:S(2)}) copy-start(s32[64,3]{0,1:T(4,128)} %param.13) | copy-start | bytes 2308
  21.3 7.8 %copy-start.2 = (s32[64,3]{0,1:T(4,128)S(1)}, s32[64,3]{0,1:T(4,128)}, u32[]{:S(2)}) copy-start(s32[64,3]{0,1:T(4,128)} %param.11) | copy-start | bytes 2308
  21.3 7.8 %copy-start.3 = (s32[64,2]{0,1:T(2,128)S(1)}, s32[64,2]{0,1:T(2,128)}, u32[]{:S(2)}) copy-start(s32[64,2]{0,1:T(2,128)} %param.12) | copy-start | bytes 1540
  21.3 83.0 %all-to-all-start = ((bf16[32,6,128,128]{3,2,1,0:T(8,128)(2,1)}), bf16[32,6,128,128]{3,2,1,0:T(8,128)(2,1)}, u32[]{:S(2)}, u32[]{:S(2)}) async-start(bf16[32,6,128,128]{3,2,1,0:T(8,128)(2,1)} %pad_maximum_fusion), calls=%async_computation | async-start | bytes 12582912 | tf_op jit(solution)/shard_map/all_to_all | solution.py:158
  177.4 8.8 %copy-start.4 = (bf16[32,2,64,128]{3,2,1,0:T(8,128)(2,1)S(1)}, bf16[32,2,64,128]{3,2,1,0:T(8,128)(2,1)}, u32[]{:S(2)}) copy-start(bf16[32,2,64,128]{3,2,1,0:T(8,128)(2,1)} %get-tuple-element.7) | copy-start | bytes 3145732
  177.4 59.5 %all-to-all-start.2 = ((bf16[32,2,128,128]{3,2,1,0:T(8,128)(2,1)}), bf16[32,2,128,128]{3,2,1,0:T(8,128)(2,1)S(1)}, u32[]{:S(2)}, u32[]{:S(2)}) async-start(bf16[32,2,128,128]{3,2,1,0:T(8,128)(2,1)} %get-tuple-element.10), calls=%async_computation.2 | async-start | bytes 4194304 | tf_op jit(solution)/shard_map/all_to_all | solution.py:164
  184.2 29.3 %collective-permute-start.1 = (bf16[32,2,64,128]{3,2,1,0:T(8,128)(2,1)}, bf16[32,2,64,128]{3,2,1,0:T(8,128)(2,1)S(1)}, u32[]{:S(2)}, u32[]{:S(2)}) collective-permute-start(bf16[32,2,64,128]{3,2,1,0:T(8,128)(2,1)} %get-tuple-element.9), channel_id=1, source_target_pairs={{32,0},{64,32},{96,64},{128,96},{160,128},{192,160},{224,192},{33,... | collective-permute-start | bytes 3145736 | tf_op jit(solution)/shard_map/ppermute | solution.py:21
  186.2 49.1 %collective-permute-start = (bf16[32,2,64,128]{3,2,1,0:T(8,128)(2,1)S(1)}, bf16[32,2,64,128]{3,2,1,0:T(8,128)(2,1)S(1)}, u32[]{:S(2)}, u32[]{:S(2)}) collective-permute-start(bf16[32,2,64,128]{3,2,1,0:T(8,128)(2,1)S(1)} %copy-done.4), channel_id=1, source_target_pairs={{32,0},{64,32},{96,64},{128,96},{160,128},{192,160},{224,192},{33,... | collective-permute-start | bytes 3145736 | tf_op jit(solution)/shard_map/ppermute | solution.py:21
  236.9 35.5 %all-to-all-start.1 = ((bf16[32,2,128,128]{3,2,1,0:T(8,128)(2,1)}), bf16[32,2,128,128]{3,2,1,0:T(8,128)(2,1)}, u32[]{:S(2)}, u32[]{:S(2)}) async-start(bf16[32,2,128,128]{3,2,1,0:T(8,128)(2,1)} %pad_maximum_fusion.1), calls=%async_computation.1 | async-start | bytes 4194304 | tf_op jit(solution)/shard_map/all_to_all | solution.py:173
  245.2 12.3 %collective-permute-start.2 = (bf16[1,128,1024]{1,2,0:T(8,128)(2,1)S(1)}, bf16[1,128,1024]{1,2,0:T(8,128)(2,1)S(1)}, u32[]{:S(2)}, u32[]{:S(2)}) collective-permute-start(bf16[1,128,1024]{1,2,0:T(8,128)(2,1)S(1)} %bitcast.50), channel_id=1, source_target_pairs={{32,0},{64,32},{96,64},{128,96},{160,128},{192,160},{224,192},{33,... | collective-permute-start | bytes 786440 | tf_op jit(solution)/shard_map/ppermute | solution.py:21
  247.2 15.1 %collective-permute-start.3 = (bf16[1,128,1024]{1,2,0:T(8,128)(2,1)S(1)}, bf16[1,128,1024]{1,2,0:T(8,128)(2,1)S(1)}, u32[]{:S(2)}, u32[]{:S(2)}) collective-permute-start(bf16[1,128,1024]{1,2,0:T(8,128)(2,1)S(1)} %bitcast.49), channel_id=1, source_target_pairs={{32,0},{64,32},{96,64},{128,96},{160,128},{192,160},{224,192},{33,... | collective-permute-start | bytes 786440 | tf_op jit(solution)/shard_map/ppermute | solution.py:21

commit v8 on v7

--- a/solution.py
+++ b/solution.py
@@ -145,16 +145,36 @@
     )(listed.reshape(-1), live.reshape(-1).astype(jnp.int32), *operands)
 
 
+def pack_kernel(q_ref, g_ref, k_ref, v_ref, out_ref):
+    out_ref[0] = q_ref[:, :HD]
+    out_ref[1] = q_ref[:, HD:]
+    out_ref[2] = g_ref[:, :HD]
+    out_ref[3] = g_ref[:, HD:]
+    out_ref[4] = k_ref[...]
+    out_ref[5] = v_ref[...]
+
+
+def pack(queries, out_grad, keys, values, lanes):
+    tok = queries.shape[1]
+    repeat = lanes // KV
+    wide = pl.BlockSpec((None, tok, 2 * HD), lambda d: (0, 0, d))
+    narrow = pl.BlockSpec((None, tok, HD), lambda d: (0, 0, d // repeat))
+    return pl.pallas_call(
+        pack_kernel,
+        grid=(lanes,),
+        in_specs=[wide, wide, narrow, narrow],
+        out_specs=pl.BlockSpec((None, 6, tok, HD), lambda d: (d, 0, 0, 0)),
+        out_shape=jax.ShapeDtypeStruct((lanes, 6, tok, HD), queries.dtype),
+        compiler_params=pltpu.CompilerParams(dimension_semantics=("arbitrary",)),
+        interpret=INTERPRET,
+    )(queries, out_grad, keys, values)
+
+
 def body(queries, keys, values, out_grad, window_blocks, global_blocks, random_blocks):
     lanes = lax.axis_size("seq")
     tok = queries.shape[1]
     repeat = lanes // KV
-    per_device = HEADS // lanes
-    q_lead = queries[0].reshape(tok, lanes, per_device, HD).transpose(1, 2, 0, 3)
-    g_lead = out_grad[0].reshape(tok, lanes, per_device, HD).transpose(1, 2, 0, 3)
-    k_lead = jnp.repeat(keys[0].reshape(tok, KV, 1, HD).transpose(1, 2, 0, 3), repeat, axis=0)
-    v_lead = jnp.repeat(values[0].reshape(tok, KV, 1, HD).transpose(1, 2, 0, 3), repeat, axis=0)
-    send = jnp.concatenate([q_lead, g_lead, k_lead, v_lead], axis=1)
+    send = pack(queries, out_grad, keys, values, lanes)
     packed = lax.all_to_all(send, "seq", split_axis=0, concat_axis=0, tiled=True)
     listed, live = block_lists(window_blocks, global_blocks, random_blocks)
     dq_first, acc = block_grads(packed, listed, live, 0)

time: 281 us -> 280 us (level)
  Pallas kernels: 73.1 us -> 91.1 us
  local copies, waits for them, and re-layouts: 25.6 us -> 9.73 us
  other arithmetic: 6.69 us -> 2 us
    pallas_call x0 -> x1, Pallas kernels: none -> 18 us  [pack(): pl.pallas_call(pack_kernel, grid=(lanes,), in_specs=[wide, wide, narrow,...]
    unnamed x17 -> x11, local copies, waits for them, and re-layouts: 14.2 us -> 4.61 us
    another operation x2 -> x0, local copies, waits for them, and re-layouts: 5.81 us -> none  [the longest x1 2.91 us: body(): queries[0].reshape(tok, lanes, per_device, HD).transpose(1, 2, 0, 3)]
    concatenate x1 -> x0, other arithmetic: 4.69 us -> none  [body(): send = jnp.concatenate([q_lead, g_lead, k_lead, v_lead], axis=1)]
where the time goes in v8:
time: 280 us; the launch traced here: 276 us
  waiting for transfers between devices  142 us (51%)
  Pallas kernels  91.1 us (33%)
  starting transfers between devices  30 us (11%)
  local copies, waits for them, and re-layouts  9.73 us (3%)
    all_to_all x1, waiting for transfers between devices, body(): lax.all_to_all(send, 'seq', split_axis=0, concat_axis=0, tiled=True)  73.5 us
    pallas_call x2, Pallas kernels, block_grads(): pl.pallas_call(kernel, grid_spec=grid_spec, out_shape=[jax.ShapeDtypeStru...  73.1 us
    ppermute x4, waiting for transfers between devices, from_behind(): return lax.ppermute(block, axis, route)  59.4 us
    pallas_call x1, Pallas kernels, pack(): pl.pallas_call(pack_kernel, grid=(lanes,), in_specs=[wide, wide, narrow,...  18 us
    all_to_all x1, waiting for transfers between devices, body(): lax.all_to_all(dq_heads, 'seq', split_axis=0, concat_axis=0, tiled=True)  9.27 us
    ppermute x4, starting transfers between devices, from_behind(): return lax.ppermute(block, axis, route)  7.88 us
    all_to_all x1, starting transfers between devices, body(): lax.all_to_all(send, 'seq', split_axis=0, concat_axis=0, tiled=True)  7.81 us
    all_to_all x1, starting transfers between devices, body(): lax.all_to_all(dq_heads, 'seq', split_axis=0, concat_axis=0, tiled=True)  7.55 us
  transfers between devices with their start and end apart: 7, of which 6 were waited for; matrix products, arithmetic and copies ran while one was open for 2% of the time, Pallas kernels for 0%

profile of v8, /device:TPU:98, one launch (start us, length us, event | category | flops | bytes accessed | tf_op | source)
XLA Modules:
  0.0 275.9 jit_solution(3643697780778449457)
XLA Ops:
  0.6 18.0 %shard_map.94 = bf16[32,6,128,128]{3,2,1,0:T(8,128)(2,1)} custom-call(bf16[1,128,8192]{2,1,0:T(8,128)(2,1)} %q_ref.1, bf16[1,128,8192]{2,1,0:T(8,128)(2,1)} %g_ref.1, bf16[1,128,1024]{2,1,0:T(8,128)(2,1)} %k_ref.1, bf16[1,128,1024]{2,1,0:T(8,128)(2,1)} %v_ref.1), custom_call_target="tpu_custom_call" | custom-call | tf_op jit(solution)/shard_map/pallas_call | solution.py:162
  18.7 7.8 %all-to-all-start = ((bf16[32,6,128,128]{3,2,1,0:T(8,128)(2,1)}), bf16[32,6,128,128]{3,2,1,0:T(8,128)(2,1)}, u32[]{:S(2)}, u32[]{:S(2)}) async-start(bf16[32,6,128,128]{3,2,1,0:T(8,128)(2,1)} %shard_map.94), calls=%async_computation | async-start | bytes 12582912 | tf_op jit(solution)/shard_map/all_to_all | solution.py:178
  26.8 0.7 reshape.47.live_ref
  27.5 0.7 reshape.42.listed_ref
  28.2 73.5 %all-to-all-done.q_ref.g_ref.kv_ref = bf16[32,6,128,128]{3,2,1,0:T(8,128)(2,1)} async-done(((bf16[32,6,128,128]{3,2,1,0:T(8,128)(2,1)}), bf16[32,6,128,128]{3,2,1,0:T(8,128)(2,1)}, u32[]{:S(2)}, u32[]{:S(2)}) %all-to-all-start) | async-done | bytes 6291488 | tf_op jit(solution)/shard_map/all_to_all | solution.py:178
  101.7 36.3 %shard_map.95 = (bf16[32,2,64,128]{3,2,1,0:T(8,128)(2,1)}, f32[32,2,128,128]{3,2,1,0:T(8,128)}) custom-call(s32[512]{0:T(512)} %reshape.42.listed_ref, s32[512]{0:T(512)} %reshape.47.live_ref, bf16[32,6,128,128]{3,2,1,0:T(8,128)(2,1)} %all-to-all-done.q_ref.g_ref.kv_ref, bf16[32,6,128,128]{3,2,1,0:T(8,128)(2,1)} %all-to-all-done.q_ref.g_ref.kv_ref, ...), custom_call_target="tpu_custom_call" | custom-call | flops 3221225472 | bytes 9437184 | tf_op jit(solution)/shard_map/pallas_call | solution.py:131
  138.0 36.8 %shard_map.96 = (bf16[32,2,64,128]{3,2,1,0:T(8,128)(2,1)}, bf16[32,2,128,128]{3,2,1,0:T(8,128)(2,1)}) custom-call(s32[512]{0:T(512)} %reshape.42.listed_ref, s32[512]{0:T(512)} %reshape.47.live_ref, bf16[32,6,128,128]{3,2,1,0:T(8,128)(2,1)} %all-to-all-done.q_ref.g_ref.kv_ref, bf16[32,6,128,128]{3,2,1,0:T(8,128)(2,1)} %all-to-all-done.q_ref.g_ref.kv_ref, ...), custom_call_target="tpu_custom_call" | custom-call | flops 3221225472 | bytes 9437184 | tf_op jit(solution)/shard_map/pallas_call | solution.py:131
  174.8 6.8 %all-to-all-start.2 = ((bf16[32,2,128,128]{3,2,1,0:T(8,128)(2,1)}), bf16[32,2,128,128]{3,2,1,0:T(8,128)(2,1)S(1)}, u32[]{:S(2)}, u32[]{:S(2)}) async-start(bf16[32,2,128,128]{3,2,1,0:T(8,128)(2,1)} %get-tuple-element.10), calls=%async_computation.2 | async-start | bytes 4194304 | tf_op jit(solution)/shard_map/all_to_all | solution.py:184
  181.6 2.0 collective-permute-start.1
  183.7 2.0 collective-permute-start
  185.7 25.3 %collective-permute-done.1 = bf16[32,2,64,128]{3,2,1,0:T(8,128)(2,1)S(1)} collective-permute-done((bf16[32,2,64,128]{3,2,1,0:T(8,128)(2,1)}, bf16[32,2,64,128]{3,2,1,0:T(8,128)(2,1)S(1)}, u32[]{:S(2)}, u32[]{:S(2)}) %collective-permute-start.1) | collective-permute-done | bytes 1048608 | tf_op jit(solution)/shard_map/ppermute | solution.py:21
  211.0 21.8 %collective-permute-done = bf16[32,2,64,128]{3,2,1,0:T(8,128)(2,1)S(1)} collective-permute-done((bf16[32,2,64,128]{3,2,1,0:T(8,128)(2,1)S(1)}, bf16[32,2,64,128]{3,2,1,0:T(8,128)(2,1)S(1)}, u32[]{:S(2)}, u32[]{:S(2)}) %collective-permute-start) | collective-permute-done | bytes 1048608 | tf_op jit(solution)/shard_map/ppermute | solution.py:21
  232.8 1.5 pad_maximum_fusion
  234.3 7.5 %all-to-all-start.1 = ((bf16[32,2,128,128]{3,2,1,0:T(8,128)(2,1)}), bf16[32,2,128,128]{3,2,1,0:T(8,128)(2,1)}, u32[]{:S(2)}, u32[]{:S(2)}) async-start(bf16[32,2,128,128]{3,2,1,0:T(8,128)(2,1)} %pad_maximum_fusion), calls=%async_computation.1 | async-start | bytes 4194304 | tf_op jit(solution)/shard_map/all_to_all | solution.py:193
  241.9 0.4 bitcast_reduce_fusion
  242.7 1.9 collective-permute-start.2
  244.6 1.9 collective-permute-start.3
  246.5 8.4 %collective-permute-done.2 = bf16[1,128,1024]{1,2,0:T(8,128)(2,1)S(1)} collective-permute-done((bf16[1,128,1024]{1,2,0:T(8,128)(2,1)S(1)}, bf16[1,128,1024]{1,2,0:T(8,128)(2,1)S(1)}, u32[]{:S(2)}, u32[]{:S(2)}) %collective-permute-start.2) | collective-permute-done | bytes 262176 | tf_op jit(solution)/shard_map/ppermute | solution.py:21
  254.9 0.8 copy.37
  255.8 3.9 %collective-permute-done.3 = bf16[1,128,1024]{1,2,0:T(8,128)(2,1)S(1)} collective-permute-done((bf16[1,128,1024]{1,2,0:T(8,128)(2,1)S(1)}, bf16[1,128,1024]{1,2,0:T(8,128)(2,1)S(1)}, u32[]{:S(2)}, u32[]{:S(2)}) %collective-permute-start.3) | collective-permute-done | bytes 262176 | tf_op jit(solution)/shard_map/ppermute | solution.py:21
  259.7 0.8 copy.38
  260.6 9.3 %all-to-all-done.1 = bf16[32,2,128,128]{3,2,1,0:T(8,128)(2,1)} async-done(((bf16[32,2,128,128]{3,2,1,0:T(8,128)(2,1)}), bf16[32,2,128,128]{3,2,1,0:T(8,128)(2,1)}, u32[]{:S(2)}, u32[]{:S(2)}) %all-to-all-start.1) | async-done | bytes 2097184 | tf_op jit(solution)/shard_map/all_to_all | solution.py:193
  269.8 3.2 %copy.33 = bf16[128,32,2,128]{0,3,2,1:T(8,128)(2,1)S(1)} copy(bf16[128,32,2,128]{3,0,2,1:T(8,128)(2,1)} %bitcast) | data formatting | bytes 4194304 | tf_op jit(solution)/shard_map/transpose | solution.py:194
  273.1 2.9 %copy.36 = bf16[1,128,8192]{2,1,0:T(8,128)(2,1)} copy(bf16[1,128,8192]{1,2,0:T(8,128)(2,1)S(1)} %bitcast.14) | data formatting | bytes 4194304
  (18 shorter events, 0.7 us)
Async XLA Ops:
  18.7 7.8 %copy-start = (s32[64,3]{0,1:T(4,128)S(1)}, s32[64,3]{0,1:T(4,128)}, u32[]{:S(2)}) copy-start(s32[64,3]{0,1:T(4,128)} %param.13) | copy-start | bytes 2308
  18.7 7.8 %copy-start.1 = (s32[64,3]{0,1:T(4,128)S(1)}, s32[64,3]{0,1:T(4,128)}, u32[]{:S(2)}) copy-start(s32[64,3]{0,1:T(4,128)} %param.11) | copy-start | bytes 2308
  18.7 7.8 %copy-start.2 = (s32[64,2]{0,1:T(2,128)S(1)}, s32[64,2]{0,1:T(2,128)}, u32[]{:S(2)}) copy-start(s32[64,2]{0,1:T(2,128)} %param.12) | copy-start | bytes 1540
  18.7 83.0 %all-to-all-start = ((bf16[32,6,128,128]{3,2,1,0:T(8,128)(2,1)}), bf16[32,6,128,128]{3,2,1,0:T(8,128)(2,1)}, u32[]{:S(2)}, u32[]{:S(2)}) async-start(bf16[32,6,128,128]{3,2,1,0:T(8,128)(2,1)} %shard_map.94), calls=%async_computation | async-start | bytes 12582912 | tf_op jit(solution)/shard_map/all_to_all | solution.py:178
  174.8 8.8 %copy-start.3 = (bf16[32,2,64,128]{3,2,1,0:T(8,128)(2,1)S(1)}, bf16[32,2,64,128]{3,2,1,0:T(8,128)(2,1)}, u32[]{:S(2)}) copy-start(bf16[32,2,64,128]{3,2,1,0:T(8,128)(2,1)} %get-tuple-element.7) | copy-start | bytes 3145732
  174.8 59.5 %all-to-all-start.2 = ((bf16[32,2,128,128]{3,2,1,0:T(8,128)(2,1)}), bf16[32,2,128,128]{3,2,1,0:T(8,128)(2,1)S(1)}, u32[]{:S(2)}, u32[]{:S(2)}) async-start(bf16[32,2,128,128]{3,2,1,0:T(8,128)(2,1)} %get-tuple-element.10), calls=%async_computation.2 | async-start | bytes 4194304 | tf_op jit(solution)/shard_map/all_to_all | solution.py:184
  181.6 29.3 %collective-permute-start.1 = (bf16[32,2,64,128]{3,2,1,0:T(8,128)(2,1)}, bf16[32,2,64,128]{3,2,1,0:T(8,128)(2,1)S(1)}, u32[]{:S(2)}, u32[]{:S(2)}) collective-permute-start(bf16[32,2,64,128]{3,2,1,0:T(8,128)(2,1)} %get-tuple-element.9), channel_id=1, source_target_pairs={{32,0},{64,32},{96,64},{128,96},{160,128},{192,160},{224,192},{33,... | collective-permute-start | bytes 3145736 | tf_op jit(solution)/shard_map/ppermute | solution.py:21
  183.7 49.1 %collective-permute-start = (bf16[32,2,64,128]{3,2,1,0:T(8,128)(2,1)S(1)}, bf16[32,2,64,128]{3,2,1,0:T(8,128)(2,1)S(1)}, u32[]{:S(2)}, u32[]{:S(2)}) collective-permute-start(bf16[32,2,64,128]{3,2,1,0:T(8,128)(2,1)S(1)} %copy-done.3), channel_id=1, source_target_pairs={{32,0},{64,32},{96,64},{128,96},{160,128},{192,160},{224,192},{33,... | collective-permute-start | bytes 3145736 | tf_op jit(solution)/shard_map/ppermute | solution.py:21
  234.3 35.5 %all-to-all-start.1 = ((bf16[32,2,128,128]{3,2,1,0:T(8,128)(2,1)}), bf16[32,2,128,128]{3,2,1,0:T(8,128)(2,1)}, u32[]{:S(2)}, u32[]{:S(2)}) async-start(bf16[32,2,128,128]{3,2,1,0:T(8,128)(2,1)} %pad_maximum_fusion), calls=%async_computation.1 | async-start | bytes 4194304 | tf_op jit(solution)/shard_map/all_to_all | solution.py:193
  242.7 12.3 %collective-permute-start.2 = (bf16[1,128,1024]{1,2,0:T(8,128)(2,1)S(1)}, bf16[1,128,1024]{1,2,0:T(8,128)(2,1)S(1)}, u32[]{:S(2)}, u32[]{:S(2)}) collective-permute-start(bf16[1,128,1024]{1,2,0:T(8,128)(2,1)S(1)} %bitcast.16), channel_id=1, source_target_pairs={{32,0},{64,32},{96,64},{128,96},{160,128},{192,160},{224,192},{33,... | collective-permute-start | bytes 786440 | tf_op jit(solution)/shard_map/ppermute | solution.py:21
  244.6 15.1 %collective-permute-start.3 = (bf16[1,128,1024]{1,2,0:T(8,128)(2,1)S(1)}, bf16[1,128,1024]{1,2,0:T(8,128)(2,1)S(1)}, u32[]{:S(2)}, u32[]{:S(2)}) collective-permute-start(bf16[1,128,1024]{1,2,0:T(8,128)(2,1)S(1)} %bitcast.15), channel_id=1, source_target_pairs={{32,0},{64,32},{96,64},{128,96},{160,128},{192,160},{224,192},{33,... | collective-permute-start | bytes 786440 | tf_op jit(solution)/shard_map/ppermute | solution.py:21

commit v9 on v8

--- a/solution.py
+++ b/solution.py
@@ -145,25 +145,29 @@
     )(listed.reshape(-1), live.reshape(-1).astype(jnp.int32), *operands)
 
 
-def pack_kernel(q_ref, g_ref, k_ref, v_ref, out_ref):
-    out_ref[0] = q_ref[:, :HD]
-    out_ref[1] = q_ref[:, HD:]
-    out_ref[2] = g_ref[:, :HD]
-    out_ref[3] = g_ref[:, HD:]
-    out_ref[4] = k_ref[...]
-    out_ref[5] = v_ref[...]
-
-
-def pack(queries, out_grad, keys, values, lanes):
+def pack_kernel(count, repeat, q_ref, g_ref, k_ref, v_ref, out_ref):
+    for d in range(count):
+        lead = slice(2 * d * HD, 2 * d * HD + HD)
+        rest = slice(2 * d * HD + HD, 2 * (d + 1) * HD)
+        head = slice(d // repeat * HD, (d // repeat + 1) * HD)
+        out_ref[d, 0] = q_ref[:, lead]
+        out_ref[d, 1] = q_ref[:, rest]
+        out_ref[d, 2] = g_ref[:, lead]
+        out_ref[d, 3] = g_ref[:, rest]
+        out_ref[d, 4] = k_ref[:, head]
+        out_ref[d, 5] = v_ref[:, head]
+
+
+def pack(queries, out_grad, keys, values, lanes, count=8):
     tok = queries.shape[1]
     repeat = lanes // KV
-    wide = pl.BlockSpec((None, tok, 2 * HD), lambda d: (0, 0, d))
-    narrow = pl.BlockSpec((None, tok, HD), lambda d: (0, 0, d // repeat))
+    wide = pl.BlockSpec((None, tok, 2 * HD * count), lambda d: (0, 0, d))
+    narrow = pl.BlockSpec((None, tok, HD * count // repeat), lambda d: (0, 0, d))
     return pl.pallas_call(
-        pack_kernel,
-        grid=(lanes,),
+        functools.partial(pack_kernel, count, repeat),
+        grid=(lanes // count,),
         in_specs=[wide, wide, narrow, narrow],
-        out_specs=pl.BlockSpec((None, 6, tok, HD), lambda d: (d, 0, 0, 0)),
+        out_specs=pl.BlockSpec((count, 6, tok, HD), lambda d: (d, 0, 0, 0)),
         out_shape=jax.ShapeDtypeStruct((lanes, 6, tok, HD), queries.dtype),
         compiler_params=pltpu.CompilerParams(dimension_semantics=("arbitrary",)),
         interpret=INTERPRET,

time: 280 us -> 266 us (0.950)
  Pallas kernels: 91.1 us -> 78.8 us
    pallas_call x1, Pallas kernels: 18 us -> 5.67 us  [pack(): pl.pallas_call(functools.partial(pack_kernel, count, repeat), grid=(lanes...]
where the time goes in v9:
time: 266 us; the launch traced here: 264 us
  waiting for transfers between devices  142 us (53%)
  Pallas kernels  78.8 us (30%)
  starting transfers between devices  30 us (11%)
  local copies, waits for them, and re-layouts  9.73 us (4%)
    all_to_all x1, waiting for transfers between devices, body(): lax.all_to_all(send, 'seq', split_axis=0, concat_axis=0, tiled=True)  73.5 us
    pallas_call x2, Pallas kernels, block_grads(): pl.pallas_call(kernel, grid_spec=grid_spec, out_shape=[jax.ShapeDtypeStru...  73.1 us
    ppermute x4, waiting for transfers between devices, from_behind(): return lax.ppermute(block, axis, route)  59.4 us
    all_to_all x1, waiting for transfers between devices, body(): lax.all_to_all(dq_heads, 'seq', split_axis=0, concat_axis=0, tiled=True)  9.27 us
    ppermute x4, starting transfers between devices, from_behind(): return lax.ppermute(block, axis, route)  7.88 us
    all_to_all x1, starting transfers between devices, body(): lax.all_to_all(send, 'seq', split_axis=0, concat_axis=0, tiled=True)  7.81 us
    all_to_all x1, starting transfers between devices, body(): lax.all_to_all(dq_heads, 'seq', split_axis=0, concat_axis=0, tiled=True)  7.55 us
    all_to_all x1, starting transfers between devices, body(): lax.all_to_all(dkv, 'seq', split_axis=0, concat_axis=0, tiled=True)  6.81 us
  transfers between devices with their start and end apart: 7, of which 6 were waited for; matrix products, arithmetic and copies ran while one was open for 2% of the time, Pallas kernels for 0%

profile of v9, /device:TPU:98, one launch (start us, length us, event | category | flops | bytes accessed | tf_op | source)
XLA Modules:
  0.0 263.6 jit_solution(5528085627847479593)
XLA Ops:
  0.6 5.7 %shard_map.94 = bf16[32,6,128,128]{3,2,1,0:T(8,128)(2,1)} custom-call(bf16[1,128,8192]{2,1,0:T(8,128)(2,1)} %q_ref.1, bf16[1,128,8192]{2,1,0:T(8,128)(2,1)} %g_ref.1, bf16[1,128,1024]{2,1,0:T(8,128)(2,1)} %k_ref.1, bf16[1,128,1024]{2,1,0:T(8,128)(2,1)} %v_ref.1), custom_call_target="tpu_custom_call" | custom-call | tf_op jit(solution)/shard_map/pallas_call | solution.py:166
  6.3 7.8 %all-to-all-start = ((bf16[32,6,128,128]{3,2,1,0:T(8,128)(2,1)}), bf16[32,6,128,128]{3,2,1,0:T(8,128)(2,1)}, u32[]{:S(2)}, u32[]{:S(2)}) async-start(bf16[32,6,128,128]{3,2,1,0:T(8,128)(2,1)} %shard_map.94), calls=%async_computation | async-start | bytes 12582912 | tf_op jit(solution)/shard_map/all_to_all | solution.py:182
  14.5 0.7 reshape.47.live_ref
  15.1 0.7 reshape.42.listed_ref
  15.8 73.5 %all-to-all-done.q_ref.g_ref.kv_ref = bf16[32,6,128,128]{3,2,1,0:T(8,128)(2,1)} async-done(((bf16[32,6,128,128]{3,2,1,0:T(8,128)(2,1)}), bf16[32,6,128,128]{3,2,1,0:T(8,128)(2,1)}, u32[]{:S(2)}, u32[]{:S(2)}) %all-to-all-start) | async-done | bytes 6291488 | tf_op jit(solution)/shard_map/all_to_all | solution.py:182
  89.3 36.3 %shard_map.95 = (bf16[32,2,64,128]{3,2,1,0:T(8,128)(2,1)}, f32[32,2,128,128]{3,2,1,0:T(8,128)}) custom-call(s32[512]{0:T(512)} %reshape.42.listed_ref, s32[512]{0:T(512)} %reshape.47.live_ref, bf16[32,6,128,128]{3,2,1,0:T(8,128)(2,1)} %all-to-all-done.q_ref.g_ref.kv_ref, bf16[32,6,128,128]{3,2,1,0:T(8,128)(2,1)} %all-to-all-done.q_ref.g_ref.kv_ref, ...), custom_call_target="tpu_custom_call" | custom-call | flops 3221225472 | bytes 9437184 | tf_op jit(solution)/shard_map/pallas_call | solution.py:131
  125.6 36.8 %shard_map.96 = (bf16[32,2,64,128]{3,2,1,0:T(8,128)(2,1)}, bf16[32,2,128,128]{3,2,1,0:T(8,128)(2,1)}) custom-call(s32[512]{0:T(512)} %reshape.42.listed_ref, s32[512]{0:T(512)} %reshape.47.live_ref, bf16[32,6,128,128]{3,2,1,0:T(8,128)(2,1)} %all-to-all-done.q_ref.g_ref.kv_ref, bf16[32,6,128,128]{3,2,1,0:T(8,128)(2,1)} %all-to-all-done.q_ref.g_ref.kv_ref, ...), custom_call_target="tpu_custom_call" | custom-call | flops 3221225472 | bytes 9437184 | tf_op jit(solution)/shard_map/pallas_call | solution.py:131
  162.4 6.8 %all-to-all-start.2 = ((bf16[32,2,128,128]{3,2,1,0:T(8,128)(2,1)}), bf16[32,2,128,128]{3,2,1,0:T(8,128)(2,1)S(1)}, u32[]{:S(2)}, u32[]{:S(2)}) async-start(bf16[32,2,128,128]{3,2,1,0:T(8,128)(2,1)} %get-tuple-element.10), calls=%async_computation.2 | async-start | bytes 4194304 | tf_op jit(solution)/shard_map/all_to_all | solution.py:188
  169.3 2.0 collective-permute-start.1
  171.3 2.0 collective-permute-start
  173.3 25.3 %collective-permute-done.1 = bf16[32,2,64,128]{3,2,1,0:T(8,128)(2,1)S(1)} collective-permute-done((bf16[32,2,64,128]{3,2,1,0:T(8,128)(2,1)}, bf16[32,2,64,128]{3,2,1,0:T(8,128)(2,1)S(1)}, u32[]{:S(2)}, u32[]{:S(2)}) %collective-permute-start.1) | collective-permute-done | bytes 1048608 | tf_op jit(solution)/shard_map/ppermute | solution.py:21
  198.6 21.8 %collective-permute-done = bf16[32,2,64,128]{3,2,1,0:T(8,128)(2,1)S(1)} collective-permute-done((bf16[32,2,64,128]{3,2,1,0:T(8,128)(2,1)S(1)}, bf16[32,2,64,128]{3,2,1,0:T(8,128)(2,1)S(1)}, u32[]{:S(2)}, u32[]{:S(2)}) %collective-permute-start) | collective-permute-done | bytes 1048608 | tf_op jit(solution)/shard_map/ppermute | solution.py:21
  220.4 1.5 pad_maximum_fusion
  221.9 7.5 %all-to-all-start.1 = ((bf16[32,2,128,128]{3,2,1,0:T(8,128)(2,1)}), bf16[32,2,128,128]{3,2,1,0:T(8,128)(2,1)}, u32[]{:S(2)}, u32[]{:S(2)}) async-start(bf16[32,2,128,128]{3,2,1,0:T(8,128)(2,1)} %pad_maximum_fusion), calls=%async_computation.1 | async-start | bytes 4194304 | tf_op jit(solution)/shard_map/all_to_all | solution.py:197
  229.5 0.4 bitcast_reduce_fusion
  230.3 1.9 collective-permute-start.2
  232.2 1.9 collective-permute-start.3
  234.1 8.4 %collective-permute-done.2 = bf16[1,128,1024]{1,2,0:T(8,128)(2,1)S(1)} collective-permute-done((bf16[1,128,1024]{1,2,0:T(8,128)(2,1)S(1)}, bf16[1,128,1024]{1,2,0:T(8,128)(2,1)S(1)}, u32[]{:S(2)}, u32[]{:S(2)}) %collective-permute-start.2) | collective-permute-done | bytes 262176 | tf_op jit(solution)/shard_map/ppermute | solution.py:21
  242.6 0.8 copy.37
  243.4 3.9 %collective-permute-done.3 = bf16[1,128,1024]{1,2,0:T(8,128)(2,1)S(1)} collective-permute-done((bf16[1,128,1024]{1,2,0:T(8,128)(2,1)S(1)}, bf16[1,128,1024]{1,2,0:T(8,128)(2,1)S(1)}, u32[]{:S(2)}, u32[]{:S(2)}) %collective-permute-start.3) | collective-permute-done | bytes 262176 | tf_op jit(solution)/shard_map/ppermute | solution.py:21
  247.3 0.8 copy.38
  248.2 9.3 %all-to-all-done.1 = bf16[32,2,128,128]{3,2,1,0:T(8,128)(2,1)} async-done(((bf16[32,2,128,128]{3,2,1,0:T(8,128)(2,1)}), bf16[32,2,128,128]{3,2,1,0:T(8,128)(2,1)}, u32[]{:S(2)}, u32[]{:S(2)}) %all-to-all-start.1) | async-done | bytes 2097184 | tf_op jit(solution)/shard_map/all_to_all | solution.py:197
  257.5 3.2 %copy.33 = bf16[128,32,2,128]{0,3,2,1:T(8,128)(2,1)S(1)} copy(bf16[128,32,2,128]{3,0,2,1:T(8,128)(2,1)} %bitcast) | data formatting | bytes 4194304 | tf_op jit(solution)/shard_map/transpose | solution.py:198
  260.7 2.9 %copy.36 = bf16[1,128,8192]{2,1,0:T(8,128)(2,1)} copy(bf16[1,128,8192]{1,2,0:T(8,128)(2,1)S(1)} %bitcast.14) | data formatting | bytes 4194304
  (18 shorter events, 0.7 us)
Async XLA Ops:
  6.3 7.8 %copy-start = (s32[64,3]{0,1:T(4,128)S(1)}, s32[64,3]{0,1:T(4,128)}, u32[]{:S(2)}) copy-start(s32[64,3]{0,1:T(4,128)} %param.13) | copy-start | bytes 2308
  6.3 7.8 %copy-start.1 = (s32[64,3]{0,1:T(4,128)S(1)}, s32[64,3]{0,1:T(4,128)}, u32[]{:S(2)}) copy-start(s32[64,3]{0,1:T(4,128)} %param.11) | copy-start | bytes 2308
  6.3 7.8 %copy-start.2 = (s32[64,2]{0,1:T(2,128)S(1)}, s32[64,2]{0,1:T(2,128)}, u32[]{:S(2)}) copy-start(s32[64,2]{0,1:T(2,128)} %param.12) | copy-start | bytes 1540
  6.3 83.0 %all-to-all-start = ((bf16[32,6,128,128]{3,2,1,0:T(8,128)(2,1)}), bf16[32,6,128,128]{3,2,1,0:T(8,128)(2,1)}, u32[]{:S(2)}, u32[]{:S(2)}) async-start(bf16[32,6,128,128]{3,2,1,0:T(8,128)(2,1)} %shard_map.94), calls=%async_computation | async-start | bytes 12582912 | tf_op jit(solution)/shard_map/all_to_all | solution.py:182
  162.4 8.8 %copy-start.3 = (bf16[32,2,64,128]{3,2,1,0:T(8,128)(2,1)S(1)}, bf16[32,2,64,128]{3,2,1,0:T(8,128)(2,1)}, u32[]{:S(2)}) copy-start(bf16[32,2,64,128]{3,2,1,0:T(8,128)(2,1)} %get-tuple-element.7) | copy-start | bytes 3145732
  162.4 59.5 %all-to-all-start.2 = ((bf16[32,2,128,128]{3,2,1,0:T(8,128)(2,1)}), bf16[32,2,128,128]{3,2,1,0:T(8,128)(2,1)S(1)}, u32[]{:S(2)}, u32[]{:S(2)}) async-start(bf16[32,2,128,128]{3,2,1,0:T(8,128)(2,1)} %get-tuple-element.10), calls=%async_computation.2 | async-start | bytes 4194304 | tf_op jit(solution)/shard_map/all_to_all | solution.py:188
  169.3 29.3 %collective-permute-start.1 = (bf16[32,2,64,128]{3,2,1,0:T(8,128)(2,1)}, bf16[32,2,64,128]{3,2,1,0:T(8,128)(2,1)S(1)}, u32[]{:S(2)}, u32[]{:S(2)}) collective-permute-start(bf16[32,2,64,128]{3,2,1,0:T(8,128)(2,1)} %get-tuple-element.9), channel_id=1, source_target_pairs={{32,0},{64,32},{96,64},{128,96},{160,128},{192,160},{224,192},{33,... | collective-permute-start | bytes 3145736 | tf_op jit(solution)/shard_map/ppermute | solution.py:21
  171.3 49.1 %collective-permute-start = (bf16[32,2,64,128]{3,2,1,0:T(8,128)(2,1)S(1)}, bf16[32,2,64,128]{3,2,1,0:T(8,128)(2,1)S(1)}, u32[]{:S(2)}, u32[]{:S(2)}) collective-permute-start(bf16[32,2,64,128]{3,2,1,0:T(8,128)(2,1)S(1)} %copy-done.3), channel_id=1, source_target_pairs={{32,0},{64,32},{96,64},{128,96},{160,128},{192,160},{224,192},{33,... | collective-permute-start | bytes 3145736 | tf_op jit(solution)/shard_map/ppermute | solution.py:21
  221.9 35.5 %all-to-all-start.1 = ((bf16[32,2,128,128]{3,2,1,0:T(8,128)(2,1)}), bf16[32,2,128,128]{3,2,1,0:T(8,128)(2,1)}, u32[]{:S(2)}, u32[]{:S(2)}) async-start(bf16[32,2,128,128]{3,2,1,0:T(8,128)(2,1)} %pad_maximum_fusion), calls=%async_computation.1 | async-start | bytes 4194304 | tf_op jit(solution)/shard_map/all_to_all | solution.py:197
  230.3 12.3 %collective-permute-start.2 = (bf16[1,128,1024]{1,2,0:T(8,128)(2,1)S(1)}, bf16[1,128,1024]{1,2,0:T(8,128)(2,1)S(1)}, u32[]{:S(2)}, u32[]{:S(2)}) collective-permute-start(bf16[1,128,1024]{1,2,0:T(8,128)(2,1)S(1)} %bitcast.16), channel_id=1, source_target_pairs={{32,0},{64,32},{96,64},{128,96},{160,128},{192,160},{224,192},{33,... | collective-permute-start | bytes 786440 | tf_op jit(solution)/shard_map/ppermute | solution.py:21
  232.2 15.1 %collective-permute-start.3 = (bf16[1,128,1024]{1,2,0:T(8,128)(2,1)S(1)}, bf16[1,128,1024]{1,2,0:T(8,128)(2,1)S(1)}, u32[]{:S(2)}, u32[]{:S(2)}) collective-permute-start(bf16[1,128,1024]{1,2,0:T(8,128)(2,1)S(1)} %bitcast.15), channel_id=1, source_target_pairs={{32,0},{64,32},{96,64},{128,96},{160,128},{192,160},{224,192},{33,... | collective-permute-start | bytes 786440 | tf_op jit(solution)/shard_map/ppermute | solution.py:21

commit v10 on v9

--- a/solution.py
+++ b/solution.py
@@ -8,7 +8,6 @@
 from jax.sharding import PartitionSpec as P
 
 
-HEADS = 64
 KV = 8
 HD = 128
 BLOCK = 64
@@ -174,6 +173,25 @@
     )(queries, out_grad, keys, values)
 
 
+def unpack_kernel(count, src_ref, out_ref):
+    for p in range(count):
+        out_ref[:, 2 * p * HD:2 * p * HD + HD] = src_ref[p, 0]
+        out_ref[:, 2 * p * HD + HD:2 * (p + 1) * HD] = src_ref[p, 1]
+
+
+def unpack(parts, count=8):
+    lanes, per_device, tok, _ = parts.shape
+    return pl.pallas_call(
+        functools.partial(unpack_kernel, count),
+        grid=(lanes // count,),
+        in_specs=[pl.BlockSpec((count, per_device, tok, HD), lambda d: (d, 0, 0, 0))],
+        out_specs=pl.BlockSpec((None, tok, per_device * HD * count), lambda d: (0, 0, d)),
+        out_shape=jax.ShapeDtypeStruct((1, tok, lanes * per_device * HD), parts.dtype),
+        compiler_params=pltpu.CompilerParams(dimension_semantics=("arbitrary",)),
+        interpret=INTERPRET,
+    )(parts)
+
+
 def body(queries, keys, values, out_grad, window_blocks, global_blocks, random_blocks):
     lanes = lax.axis_size("seq")
     tok = queries.shape[1]
@@ -195,7 +213,7 @@
     dk_next, dv_next = from_behind((dk_flat, dv_flat), "pipe", -1)
     dq_heads = jnp.concatenate([dq_first_next, dq_second_next], axis=2)
     dq_parts = lax.all_to_all(dq_heads, "seq", split_axis=0, concat_axis=0, tiled=True)
-    dq_next = dq_parts.transpose(2, 0, 1, 3).reshape(1, tok, HEADS * HD)
+    dq_next = unpack(dq_parts)
     return dq_next, dk_next, dv_next
 
 

time: 266 us -> 264 us (level)
  local copies, waits for them, and re-layouts: 9.73 us -> 3.62 us
  Pallas kernels: 78.8 us -> 82.8 us
    pallas_call x0 -> x1, Pallas kernels: none -> 3.98 us  [unpack(): pl.pallas_call(functools.partial(unpack_kernel, count), grid=(lanes // co...]
    transpose x1 -> x0, local copies, waits for them, and re-layouts: 3.22 us -> none  [body(): dq_next = dq_parts.transpose(2, 0, 1, 3).reshape(1, tok, HEADS * HD)]
    unnamed x11 -> x10, local copies, waits for them, and re-layouts: 4.61 us -> 1.71 us
where the time goes in v10:
time: 264 us; the launch traced here: 261 us
  waiting for transfers between devices  142 us (54%)
  Pallas kernels  82.8 us (31%)
  starting transfers between devices  30 us (11%)
  local copies, waits for them, and re-layouts  3.62 us (1%)
    all_to_all x1, waiting for transfers between devices, body(): lax.all_to_all(send, 'seq', split_axis=0, concat_axis=0, tiled=True)  73.5 us
    pallas_call x2, Pallas kernels, block_grads(): pl.pallas_call(kernel, grid_spec=grid_spec, out_shape=[jax.ShapeDtypeStru...  73.1 us
    ppermute x4, waiting for transfers between devices, from_behind(): return lax.ppermute(block, axis, route)  59.4 us
    all_to_all x1, waiting for transfers between devices, body(): lax.all_to_all(dq_heads, 'seq', split_axis=0, concat_axis=0, tiled=True)  9.27 us
    ppermute x4, starting transfers between devices, from_behind(): return lax.ppermute(block, axis, route)  7.88 us
    all_to_all x1, starting transfers between devices, body(): lax.all_to_all(send, 'seq', split_axis=0, concat_axis=0, tiled=True)  7.81 us
    all_to_all x1, starting transfers between devices, body(): lax.all_to_all(dq_heads, 'seq', split_axis=0, concat_axis=0, tiled=True)  7.55 us
    all_to_all x1, starting transfers between devices, body(): lax.all_to_all(dkv, 'seq', split_axis=0, concat_axis=0, tiled=True)  6.81 us
  transfers between devices with their start and end apart: 7, of which 6 were waited for; matrix products, arithmetic and copies ran while one was open for 2% of the time, Pallas kernels for 0%

profile of v10, /device:TPU:98, one launch (start us, length us, event | category | flops | bytes accessed | tf_op | source)
XLA Modules:
  0.0 261.4 jit_solution(14455633758681302960)
XLA Ops:
  0.6 5.7 %shard_map.94 = bf16[32,6,128,128]{3,2,1,0:T(8,128)(2,1)} custom-call(bf16[1,128,8192]{2,1,0:T(8,128)(2,1)} %q_ref.1, bf16[1,128,8192]{2,1,0:T(8,128)(2,1)} %g_ref.1, bf16[1,128,1024]{2,1,0:T(8,128)(2,1)} %k_ref.1, bf16[1,128,1024]{2,1,0:T(8,128)(2,1)} %v_ref.1), custom_call_target="tpu_custom_call" | custom-call | tf_op jit(solution)/shard_map/pallas_call | solution.py:165
  6.3 7.8 %all-to-all-start = ((bf16[32,6,128,128]{3,2,1,0:T(8,128)(2,1)}), bf16[32,6,128,128]{3,2,1,0:T(8,128)(2,1)}, u32[]{:S(2)}, u32[]{:S(2)}) async-start(bf16[32,6,128,128]{3,2,1,0:T(8,128)(2,1)} %shard_map.94), calls=%async_computation | async-start | bytes 12582912 | tf_op jit(solution)/shard_map/all_to_all | solution.py:200
  14.5 0.7 reshape.43.live_ref
  15.1 0.7 reshape.39.listed_ref
  15.8 73.5 %all-to-all-done.q_ref.g_ref.kv_ref = bf16[32,6,128,128]{3,2,1,0:T(8,128)(2,1)} async-done(((bf16[32,6,128,128]{3,2,1,0:T(8,128)(2,1)}), bf16[32,6,128,128]{3,2,1,0:T(8,128)(2,1)}, u32[]{:S(2)}, u32[]{:S(2)}) %all-to-all-start) | async-done | bytes 6291488 | tf_op jit(solution)/shard_map/all_to_all | solution.py:200
  89.3 36.3 %shard_map.95 = (bf16[32,2,64,128]{3,2,1,0:T(8,128)(2,1)}, f32[32,2,128,128]{3,2,1,0:T(8,128)}) custom-call(s32[512]{0:T(512)} %reshape.39.listed_ref, s32[512]{0:T(512)} %reshape.43.live_ref, bf16[32,6,128,128]{3,2,1,0:T(8,128)(2,1)} %all-to-all-done.q_ref.g_ref.kv_ref, bf16[32,6,128,128]{3,2,1,0:T(8,128)(2,1)} %all-to-all-done.q_ref.g_ref.kv_ref, ...), custom_call_target="tpu_custom_call" | custom-call | flops 3221225472 | bytes 9437184 | tf_op jit(solution)/shard_map/pallas_call | solution.py:130
  125.6 36.8 %shard_map.96 = (bf16[32,2,64,128]{3,2,1,0:T(8,128)(2,1)}, bf16[32,2,128,128]{3,2,1,0:T(8,128)(2,1)}) custom-call(s32[512]{0:T(512)} %reshape.39.listed_ref, s32[512]{0:T(512)} %reshape.43.live_ref, bf16[32,6,128,128]{3,2,1,0:T(8,128)(2,1)} %all-to-all-done.q_ref.g_ref.kv_ref, bf16[32,6,128,128]{3,2,1,0:T(8,128)(2,1)} %all-to-all-done.q_ref.g_ref.kv_ref, ...), custom_call_target="tpu_custom_call" | custom-call | flops 3221225472 | bytes 9437184 | tf_op jit(solution)/shard_map/pallas_call | solution.py:130
  162.4 6.8 %all-to-all-start.2 = ((bf16[32,2,128,128]{3,2,1,0:T(8,128)(2,1)}), bf16[32,2,128,128]{3,2,1,0:T(8,128)(2,1)S(1)}, u32[]{:S(2)}, u32[]{:S(2)}) async-start(bf16[32,2,128,128]{3,2,1,0:T(8,128)(2,1)} %get-tuple-element.10), calls=%async_computation.2 | async-start | bytes 4194304 | tf_op jit(solution)/shard_map/all_to_all | solution.py:206
  169.3 2.0 collective-permute-start.1
  171.3 2.0 collective-permute-start
  173.3 25.3 %collective-permute-done.1 = bf16[32,2,64,128]{3,2,1,0:T(8,128)(2,1)S(1)} collective-permute-done((bf16[32,2,64,128]{3,2,1,0:T(8,128)(2,1)}, bf16[32,2,64,128]{3,2,1,0:T(8,128)(2,1)S(1)}, u32[]{:S(2)}, u32[]{:S(2)}) %collective-permute-start.1) | collective-permute-done | bytes 1048608 | tf_op jit(solution)/shard_map/ppermute | solution.py:20
  198.6 21.8 %collective-permute-done = bf16[32,2,64,128]{3,2,1,0:T(8,128)(2,1)S(1)} collective-permute-done((bf16[32,2,64,128]{3,2,1,0:T(8,128)(2,1)S(1)}, bf16[32,2,64,128]{3,2,1,0:T(8,128)(2,1)S(1)}, u32[]{:S(2)}, u32[]{:S(2)}) %collective-permute-start) | collective-permute-done | bytes 1048608 | tf_op jit(solution)/shard_map/ppermute | solution.py:20
  220.4 1.5 pad_maximum_fusion
  221.9 7.5 %all-to-all-start.1 = ((bf16[32,2,128,128]{3,2,1,0:T(8,128)(2,1)}), bf16[32,2,128,128]{3,2,1,0:T(8,128)(2,1)}, u32[]{:S(2)}, u32[]{:S(2)}) async-start(bf16[32,2,128,128]{3,2,1,0:T(8,128)(2,1)} %pad_maximum_fusion), calls=%async_computation.1 | async-start | bytes 4194304 | tf_op jit(solution)/shard_map/all_to_all | solution.py:215
  229.5 0.4 bitcast_reduce_fusion
  230.1 0.2 copy.27
  230.3 1.9 collective-permute-start.2
  232.2 1.9 collective-permute-start.3
  234.1 8.4 %collective-permute-done.2 = bf16[1,128,1024]{1,2,0:T(8,128)(2,1)S(1)} collective-permute-done((bf16[1,128,1024]{1,2,0:T(8,128)(2,1)S(1)}, bf16[1,128,1024]{1,2,0:T(8,128)(2,1)S(1)}, u32[]{:S(2)}, u32[]{:S(2)}) %collective-permute-start.2) | collective-permute-done | bytes 262176 | tf_op jit(solution)/shard_map/ppermute | solution.py:20
  242.6 0.8 copy.29
  243.4 3.9 %collective-permute-done.3 = bf16[1,128,1024]{1,2,0:T(8,128)(2,1)S(1)} collective-permute-done((bf16[1,128,1024]{1,2,0:T(8,128)(2,1)S(1)}, bf16[1,128,1024]{1,2,0:T(8,128)(2,1)S(1)}, u32[]{:S(2)}, u32[]{:S(2)}) %collective-permute-start.3) | collective-permute-done | bytes 262176 | tf_op jit(solution)/shard_map/ppermute | solution.py:20
  247.3 0.8 copy.30
  248.2 9.3 %all-to-all-done.1.src_ref = bf16[32,2,128,128]{3,2,1,0:T(8,128)(2,1)} async-done(((bf16[32,2,128,128]{3,2,1,0:T(8,128)(2,1)}), bf16[32,2,128,128]{3,2,1,0:T(8,128)(2,1)}, u32[]{:S(2)}, u32[]{:S(2)}) %all-to-all-start.1) | async-done | bytes 2097184 | tf_op jit(solution)/shard_map/all_to_all | solution.py:215
  257.5 4.0 %shard_map.97 = bf16[1,128,8192]{2,1,0:T(8,128)(2,1)} custom-call(bf16[32,2,128,128]{3,2,1,0:T(8,128)(2,1)} %all-to-all-done.1.src_ref), custom_call_target="tpu_custom_call" | custom-call | tf_op jit(solution)/shard_map/pallas_call | solution.py:184
  (17 shorter events, 0.5 us)
Async XLA Ops:
  6.3 7.8 %copy-start = (s32[64,3]{0,1:T(4,128)S(1)}, s32[64,3]{0,1:T(4,128)}, u32[]{:S(2)}) copy-start(s32[64,3]{0,1:T(4,128)} %param.13) | copy-start | bytes 2308
  6.3 7.8 %copy-start.1 = (s32[64,3]{0,1:T(4,128)S(1)}, s32[64,3]{0,1:T(4,128)}, u32[]{:S(2)}) copy-start(s32[64,3]{0,1:T(4,128)} %param.11) | copy-start | bytes 2308
  6.3 7.8 %copy-start.2 = (s32[64,2]{0,1:T(2,128)S(1)}, s32[64,2]{0,1:T(2,128)}, u32[]{:S(2)}) copy-start(s32[64,2]{0,1:T(2,128)} %param.12) | copy-start | bytes 1540
  6.3 83.0 %all-to-all-start = ((bf16[32,6,128,128]{3,2,1,0:T(8,128)(2,1)}), bf16[32,6,128,128]{3,2,1,0:T(8,128)(2,1)}, u32[]{:S(2)}, u32[]{:S(2)}) async-start(bf16[32,6,128,128]{3,2,1,0:T(8,128)(2,1)} %shard_map.94), calls=%async_computation | async-start | bytes 12582912 | tf_op jit(solution)/shard_map/all_to_all | solution.py:200
  162.4 8.8 %copy-start.3 = (bf16[32,2,64,128]{3,2,1,0:T(8,128)(2,1)S(1)}, bf16[32,2,64,128]{3,2,1,0:T(8,128)(2,1)}, u32[]{:S(2)}) copy-start(bf16[32,2,64,128]{3,2,1,0:T(8,128)(2,1)} %get-tuple-element.7) | copy-start | bytes 3145732
  162.4 59.5 %all-to-all-start.2 = ((bf16[32,2,128,128]{3,2,1,0:T(8,128)(2,1)}), bf16[32,2,128,128]{3,2,1,0:T(8,128)(2,1)S(1)}, u32[]{:S(2)}, u32[]{:S(2)}) async-start(bf16[32,2,128,128]{3,2,1,0:T(8,128)(2,1)} %get-tuple-element.10), calls=%async_computation.2 | async-start | bytes 4194304 | tf_op jit(solution)/shard_map/all_to_all | solution.py:206
  169.3 29.3 %collective-permute-start.1 = (bf16[32,2,64,128]{3,2,1,0:T(8,128)(2,1)}, bf16[32,2,64,128]{3,2,1,0:T(8,128)(2,1)S(1)}, u32[]{:S(2)}, u32[]{:S(2)}) collective-permute-start(bf16[32,2,64,128]{3,2,1,0:T(8,128)(2,1)} %get-tuple-element.9), channel_id=1, source_target_pairs={{32,0},{64,32},{96,64},{128,96},{160,128},{192,160},{224,192},{33,... | collective-permute-start | bytes 3145736 | tf_op jit(solution)/shard_map/ppermute | solution.py:20
  171.3 49.1 %collective-permute-start = (bf16[32,2,64,128]{3,2,1,0:T(8,128)(2,1)S(1)}, bf16[32,2,64,128]{3,2,1,0:T(8,128)(2,1)S(1)}, u32[]{:S(2)}, u32[]{:S(2)}) collective-permute-start(bf16[32,2,64,128]{3,2,1,0:T(8,128)(2,1)S(1)} %copy-done.3), channel_id=1, source_target_pairs={{32,0},{64,32},{96,64},{128,96},{160,128},{192,160},{224,192},{33,... | collective-permute-start | bytes 3145736 | tf_op jit(solution)/shard_map/ppermute | solution.py:20
  221.9 35.5 %all-to-all-start.1 = ((bf16[32,2,128,128]{3,2,1,0:T(8,128)(2,1)}), bf16[32,2,128,128]{3,2,1,0:T(8,128)(2,1)}, u32[]{:S(2)}, u32[]{:S(2)}) async-start(bf16[32,2,128,128]{3,2,1,0:T(8,128)(2,1)} %pad_maximum_fusion), calls=%async_computation.1 | async-start | bytes 4194304 | tf_op jit(solution)/shard_map/all_to_all | solution.py:215
  230.3 12.3 %collective-permute-start.2 = (bf16[1,128,1024]{1,2,0:T(8,128)(2,1)S(1)}, bf16[1,128,1024]{1,2,0:T(8,128)(2,1)S(1)}, u32[]{:S(2)}, u32[]{:S(2)}) collective-permute-start(bf16[1,128,1024]{1,2,0:T(8,128)(2,1)S(1)} %bitcast.13), channel_id=1, source_target_pairs={{32,0},{64,32},{96,64},{128,96},{160,128},{192,160},{224,192},{33,... | collective-permute-start | bytes 786440 | tf_op jit(solution)/shard_map/ppermute | solution.py:20
  232.2 15.1 %collective-permute-start.3 = (bf16[1,128,1024]{1,2,0:T(8,128)(2,1)S(1)}, bf16[1,128,1024]{1,2,0:T(8,128)(2,1)S(1)}, u32[]{:S(2)}, u32[]{:S(2)}) collective-permute-start(bf16[1,128,1024]{1,2,0:T(8,128)(2,1)S(1)} %bitcast.12), channel_id=1, source_target_pairs={{32,0},{64,32},{96,64},{128,96},{160,128},{192,160},{224,192},{33,... | collective-permute-start | bytes 786440 | tf_op jit(solution)/shard_map/ppermute | solution.py:20

commit v11 on v10

--- a/solution.py
+++ b/solution.py
@@ -202,17 +202,17 @@
     dq_first, acc = block_grads(packed, listed, live, 0)
     dq_first_next = from_behind(dq_first, "pipe", -1)
     dq_second, dkv = block_grads(packed, listed, live, 1, acc, jnp.bfloat16)
-    dq_second_next = from_behind(dq_second, "pipe", -1)
+    dq_second_tok = lax.all_to_all(dq_second, "seq", split_axis=0, concat_axis=0, tiled=True)
+    dq_second_next = from_behind(dq_second_tok, "pipe", -1)
     dkv_parts = lax.all_to_all(dkv, "seq", split_axis=0, concat_axis=0, tiled=True)
     dkv_wide = dkv_parts.reshape(KV, repeat, 2, tok, HD).astype(jnp.float32)
     dkv_sum = jnp.sum(dkv_wide, axis=1).astype(jnp.bfloat16)
-    dk_tokens = dkv_sum[:, 0].transpose(1, 0, 2)
-    dv_tokens = dkv_sum[:, 1].transpose(1, 0, 2)
-    dk_flat = dk_tokens.reshape(1, tok, KV * HD)
-    dv_flat = dv_tokens.reshape(1, tok, KV * HD)
-    dk_next, dv_next = from_behind((dk_flat, dv_flat), "pipe", -1)
-    dq_heads = jnp.concatenate([dq_first_next, dq_second_next], axis=2)
-    dq_parts = lax.all_to_all(dq_heads, "seq", split_axis=0, concat_axis=0, tiled=True)
+    dkv_tokens = dkv_sum.transpose(1, 2, 0, 3).reshape(2, tok, KV * HD)
+    dkv_next = from_behind(dkv_tokens, "pipe", -1)
+    dk_next = dkv_next[0:1]
+    dv_next = dkv_next[1:2]
+    dq_first_tok = lax.all_to_all(dq_first_next, "seq", split_axis=0, concat_axis=0, tiled=True)
+    dq_parts = jnp.concatenate([dq_first_tok, dq_second_next], axis=2)
     dq_next = unpack(dq_parts)
     return dq_next, dk_next, dv_next
 

time: 264 us -> 256 us (0.970)
  waiting for transfers between devices: 142 us -> 112 us
  blocking collectives: 0 us -> 23.4 us
  starting transfers between devices: 30 us -> 26.4 us
    all_to_all x0 -> x1, blocking collectives: none -> 23.4 us  [body(): lax.all_to_all(dq_second, 'seq', split_axis=0, concat_axis=0, tiled=True)]
    ppermute x4 -> x3, waiting for transfers between devices: 59.4 us -> 36.6 us  [from_behind(): return lax.ppermute(block, axis, route)]
    all_to_all x1, waiting for transfers between devices: 9.27 us -> 1.94 us  [body(): lax.all_to_all(dq_first_next, 'seq', split_axis=0, concat_axis=0, tiled=T...]
    ppermute x4 -> x3, starting transfers between devices: 7.88 us -> 5.96 us  [from_behind(): return lax.ppermute(block, axis, route)]
  transfers between devices with their start and end apart: 7 -> 6, of which waited for: 6 -> 5; matrix products, arithmetic and copies ran while one was open for 2% -> 3% of each run, Pallas kernels for 0% -> 2%
where the time goes in v11:
time: 256 us; the launch traced here: 255 us
  waiting for transfers between devices  112 us (44%)
  Pallas kernels  82.7 us (32%)
  starting transfers between devices  26.4 us (10%)
  blocking collectives  23.4 us (9%)
  local copies, waits for them, and re-layouts  5.59 us (2%)
  other arithmetic  4.14 us (2%)
    all_to_all x1, waiting for transfers between devices, body(): lax.all_to_all(send, 'seq', split_axis=0, concat_axis=0, tiled=True)  73.5 us
    pallas_call x2, Pallas kernels, block_grads(): pl.pallas_call(kernel, grid_spec=grid_spec, out_shape=[jax.ShapeDtypeStru...  73.1 us
    ppermute x3, waiting for transfers between devices, from_behind(): return lax.ppermute(block, axis, route)  36.6 us
    all_to_all x1, blocking collectives, body(): lax.all_to_all(dq_second, 'seq', split_axis=0, concat_axis=0, tiled=True)  23.4 us
    all_to_all x1, starting transfers between devices, body(): lax.all_to_all(send, 'seq', split_axis=0, concat_axis=0, tiled=True)  7.81 us
    all_to_all x1, starting transfers between devices, body(): lax.all_to_all(dq_first_next, 'seq', split_axis=0, concat_axis=0, tiled=T...  7.49 us
    ppermute x3, starting transfers between devices, from_behind(): return lax.ppermute(block, axis, route)  5.96 us
    pallas_call x1, Pallas kernels, pack(): pl.pallas_call(functools.partial(pack_kernel, count, repeat), grid=(lanes...  5.68 us
  transfers between devices with their start and end apart: 6, of which 5 were waited for; matrix products, arithmetic and copies ran while one was open for 3% of the time, Pallas kernels for 2%

profile of v11, /device:TPU:98, one launch (start us, length us, event | category | flops | bytes accessed | tf_op | source)
XLA Modules:
  0.0 255.1 jit_solution(3789401786130722080)
XLA Ops:
  0.6 5.7 %shard_map.94 = bf16[32,6,128,128]{3,2,1,0:T(8,128)(2,1)} custom-call(bf16[1,128,8192]{2,1,0:T(8,128)(2,1)} %q_ref.1, bf16[1,128,8192]{2,1,0:T(8,128)(2,1)} %g_ref.1, bf16[1,128,1024]{2,1,0:T(8,128)(2,1)} %k_ref.1, bf16[1,128,1024]{2,1,0:T(8,128)(2,1)} %v_ref.1), custom_call_target="tpu_custom_call" | custom-call | tf_op jit(solution)/shard_map/pallas_call | solution.py:165
  6.3 7.8 %all-to-all-start = ((bf16[32,6,128,128]{3,2,1,0:T(8,128)(2,1)}), bf16[32,6,128,128]{3,2,1,0:T(8,128)(2,1)}, u32[]{:S(2)}, u32[]{:S(2)}) async-start(bf16[32,6,128,128]{3,2,1,0:T(8,128)(2,1)} %shard_map.94), calls=%async_computation | async-start | bytes 12582912 | tf_op jit(solution)/shard_map/all_to_all | solution.py:200
  14.5 0.7 reshape.39.live_ref
  15.1 0.7 reshape.36.listed_ref
  15.8 73.5 %all-to-all-done.q_ref.g_ref.kv_ref = bf16[32,6,128,128]{3,2,1,0:T(8,128)(2,1)} async-done(((bf16[32,6,128,128]{3,2,1,0:T(8,128)(2,1)}), bf16[32,6,128,128]{3,2,1,0:T(8,128)(2,1)}, u32[]{:S(2)}, u32[]{:S(2)}) %all-to-all-start) | async-done | bytes 6291488 | tf_op jit(solution)/shard_map/all_to_all | solution.py:200
  89.3 36.3 %shard_map.95 = (bf16[32,2,64,128]{3,2,1,0:T(8,128)(2,1)}, f32[32,2,128,128]{3,2,1,0:T(8,128)}) custom-call(s32[512]{0:T(512)} %reshape.36.listed_ref, s32[512]{0:T(512)} %reshape.39.live_ref, bf16[32,6,128,128]{3,2,1,0:T(8,128)(2,1)} %all-to-all-done.q_ref.g_ref.kv_ref, bf16[32,6,128,128]{3,2,1,0:T(8,128)(2,1)} %all-to-all-done.q_ref.g_ref.kv_ref, ...), custom_call_target="tpu_custom_call" | custom-call | flops 3221225472 | bytes 9437184 | tf_op jit(solution)/shard_map/pallas_call | solution.py:130
  125.6 36.8 %shard_map.96 = (bf16[32,2,64,128]{3,2,1,0:T(8,128)(2,1)}, bf16[32,2,128,128]{3,2,1,0:T(8,128)(2,1)}) custom-call(s32[512]{0:T(512)} %reshape.36.listed_ref, s32[512]{0:T(512)} %reshape.39.live_ref, bf16[32,6,128,128]{3,2,1,0:T(8,128)(2,1)} %all-to-all-done.q_ref.g_ref.kv_ref, bf16[32,6,128,128]{3,2,1,0:T(8,128)(2,1)} %all-to-all-done.q_ref.g_ref.kv_ref, ...), custom_call_target="tpu_custom_call" | custom-call | flops 3221225472 | bytes 9437184 | tf_op jit(solution)/shard_map/pallas_call | solution.py:130
  162.4 23.4 %all_to_all.20 = bf16[32,2,64,128]{3,2,1,0:T(8,128)(2,1)} all-to-all(bf16[32,2,64,128]{3,2,1,0:T(8,128)(2,1)} %get-tuple-element.9), channel_id=1, replica_groups=mesh['pipe'=8,'seq'=32] {'seq'}, dimensions={0} | all-to-all | bytes 2097152 | tf_op jit(solution)/shard_map/all_to_all | solution.py:205
  185.8 5.1 %all-to-all-start.3 = ((bf16[32,2,128,128]{3,2,1,0:T(8,128)(2,1)}), bf16[32,2,128,128]{3,2,1,0:T(8,128)(2,1)S(1)}, u32[]{:S(2)}, u32[]{:S(2)}) async-start(bf16[32,2,128,128]{3,2,1,0:T(8,128)(2,1)} %get-tuple-element.10), calls=%async_computation.3 | async-start | bytes 4194304 | tf_op jit(solution)/shard_map/all_to_all | solution.py:207
  191.0 2.0 collective-permute-start
  193.0 2.0 collective-permute-start.1
  195.0 25.3 %collective-permute-done = bf16[32,2,64,128]{3,2,1,0:T(8,128)(2,1)S(1)} collective-permute-done((bf16[32,2,64,128]{3,2,1,0:T(8,128)(2,1)}, bf16[32,2,64,128]{3,2,1,0:T(8,128)(2,1)S(1)}, u32[]{:S(2)}, u32[]{:S(2)}) %collective-permute-start) | collective-permute-done | bytes 1048608 | tf_op jit(solution)/shard_map/ppermute | solution.py:20
  220.3 1.0 copy-done
  221.3 7.5 %all-to-all-start.1 = ((bf16[32,2,64,128]{3,2,1,0:T(8,128)(2,1)}), bf16[32,2,64,128]{3,2,1,0:T(8,128)(2,1)S(1)}, u32[]{:S(2)}, u32[]{:S(2)}) async-start(bf16[32,2,64,128]{3,2,1,0:T(8,128)(2,1)} %copy-done), calls=%async_computation.1 | async-start | bytes 2097152 | tf_op jit(solution)/shard_map/all_to_all | solution.py:214
  228.8 1.2 bitcast_reduce_fusion
  230.1 1.3 copy.26
  231.4 1.9 collective-permute-start.2
  233.3 9.6 %collective-permute-done.1 = bf16[32,2,64,128]{3,2,1,0:T(8,128)(2,1)} collective-permute-done((bf16[32,2,64,128]{3,2,1,0:T(8,128)(2,1)}, bf16[32,2,64,128]{3,2,1,0:T(8,128)(2,1)}, u32[]{:S(2)}, u32[]{:S(2)}) %collective-permute-start.1) | collective-permute-done | bytes 1048608 | tf_op jit(solution)/shard_map/ppermute | solution.py:20
  242.9 1.9 all-to-all-done.1
  244.8 2.8 %pad_maximum_fusion.src_ref = bf16[32,2,128,128]{3,2,1,0:T(8,128)(2,1)} fusion(bf16[32,2,64,128]{3,2,1,0:T(8,128)(2,1)} %collective-permute-done.1, bf16[32,2,64,128]{3,2,1,0:T(8,128)(2,1)S(1)} %all-to-all-done.1), kind=kLoop, calls=%fused_computation | loop fusion | flops 4194304 | bytes 4194304 | tf_op jit(solution)/shard_map/concatenate | solution.py:215
  247.6 4.0 %shard_map.97 = bf16[1,128,8192]{2,1,0:T(8,128)(2,1)} custom-call(bf16[32,2,128,128]{3,2,1,0:T(8,128)(2,1)} %pad_maximum_fusion.src_ref), custom_call_target="tpu_custom_call" | custom-call | tf_op jit(solution)/shard_map/pallas_call | solution.py:184
  251.6 1.8 collective-permute-done.2
  253.4 0.9 copy.28
  254.2 0.8 copy.27
  (15 shorter events, 0.3 us)
Async XLA Ops:
  6.3 7.8 %copy-start.1 = (s32[64,3]{0,1:T(4,128)S(1)}, s32[64,3]{0,1:T(4,128)}, u32[]{:S(2)}) copy-start(s32[64,3]{0,1:T(4,128)} %param.13) | copy-start | bytes 2308
  6.3 7.8 %copy-start.2 = (s32[64,3]{0,1:T(4,128)S(1)}, s32[64,3]{0,1:T(4,128)}, u32[]{:S(2)}) copy-start(s32[64,3]{0,1:T(4,128)} %param.11) | copy-start | bytes 2308
  6.3 7.8 %copy-start.3 = (s32[64,2]{0,1:T(2,128)S(1)}, s32[64,2]{0,1:T(2,128)}, u32[]{:S(2)}) copy-start(s32[64,2]{0,1:T(2,128)} %param.12) | copy-start | bytes 1540
  6.3 83.0 %all-to-all-start = ((bf16[32,6,128,128]{3,2,1,0:T(8,128)(2,1)}), bf16[32,6,128,128]{3,2,1,0:T(8,128)(2,1)}, u32[]{:S(2)}, u32[]{:S(2)}) async-start(bf16[32,6,128,128]{3,2,1,0:T(8,128)(2,1)} %shard_map.94), calls=%async_computation | async-start | bytes 12582912 | tf_op jit(solution)/shard_map/all_to_all | solution.py:200
  185.8 35.5 %all-to-all-start.3 = ((bf16[32,2,128,128]{3,2,1,0:T(8,128)(2,1)}), bf16[32,2,128,128]{3,2,1,0:T(8,128)(2,1)S(1)}, u32[]{:S(2)}, u32[]{:S(2)}) async-start(bf16[32,2,128,128]{3,2,1,0:T(8,128)(2,1)} %get-tuple-element.10), calls=%async_computation.3 | async-start | bytes 4194304 | tf_op jit(solution)/shard_map/all_to_all | solution.py:207
  191.0 29.3 %collective-permute-start = (bf16[32,2,64,128]{3,2,1,0:T(8,128)(2,1)}, bf16[32,2,64,128]{3,2,1,0:T(8,128)(2,1)S(1)}, u32[]{:S(2)}, u32[]{:S(2)}) collective-permute-start(bf16[32,2,64,128]{3,2,1,0:T(8,128)(2,1)} %get-tuple-element.7), channel_id=1, source_target_pairs={{32,0},{64,32},{96,64},{128,96},{160,128},{192,160},{224,192},{33,... | collective-permute-start | bytes 3145736 | tf_op jit(solution)/shard_map/ppermute | solution.py:20
  193.0 49.9 %collective-permute-start.1 = (bf16[32,2,64,128]{3,2,1,0:T(8,128)(2,1)}, bf16[32,2,64,128]{3,2,1,0:T(8,128)(2,1)}, u32[]{:S(2)}, u32[]{:S(2)}) collective-permute-start(bf16[32,2,64,128]{3,2,1,0:T(8,128)(2,1)} %all_to_all.20), channel_id=1, source_target_pairs={{32,0},{64,32},{96,64},{128,96},{160,128},{192,160},{224,192},{33,... | collective-permute-start | bytes 3145736 | tf_op jit(solution)/shard_map/ppermute | solution.py:20
  220.3 1.0 copy-start
  221.3 23.5 %all-to-all-start.1 = ((bf16[32,2,64,128]{3,2,1,0:T(8,128)(2,1)}), bf16[32,2,64,128]{3,2,1,0:T(8,128)(2,1)S(1)}, u32[]{:S(2)}, u32[]{:S(2)}) async-start(bf16[32,2,64,128]{3,2,1,0:T(8,128)(2,1)} %copy-done), calls=%async_computation.1 | async-start | bytes 2097152 | tf_op jit(solution)/shard_map/all_to_all | solution.py:214
  231.4 22.0 %collective-permute-start.2 = (bf16[2,128,1024]{1,2,0:T(8,128)(2,1)S(1)}, bf16[2,128,1024]{1,2,0:T(8,128)(2,1)S(1)}, u32[]{:S(2)}, u32[]{:S(2)}) collective-permute-start(bf16[2,128,1024]{1,2,0:T(8,128)(2,1)S(1)} %bitcast.5), channel_id=1, source_target_pairs={{32,0},{64,32},{96,64},{128,96},{160,128},{192,160},{224,192},{33,... | collective-permute-start | bytes 1572872 | tf_op jit(solution)/shard_map/ppermute | solution.py:20

commit v12 on v11

--- a/solution.py
+++ b/solution.py
@@ -96,7 +96,7 @@
         out_ref[...] = dkv_ref[...].astype(out_ref.dtype)
 
 
-def block_grads(packed, listed, live, part, acc_in=None, out_dtype=jnp.float32, steps=4):
+def block_grads(packed, listed, live, part, acc_in=None, out_dtype=jnp.float32, steps=8):
     nblocks, slots = listed.shape
     lanes, _, tok, _ = packed.shape
     per_device = 2
@@ -202,8 +202,7 @@
     dq_first, acc = block_grads(packed, listed, live, 0)
     dq_first_next = from_behind(dq_first, "pipe", -1)
     dq_second, dkv = block_grads(packed, listed, live, 1, acc, jnp.bfloat16)
-    dq_second_tok = lax.all_to_all(dq_second, "seq", split_axis=0, concat_axis=0, tiled=True)
-    dq_second_next = from_behind(dq_second_tok, "pipe", -1)
+    dq_second_next = from_behind(dq_second, "pipe", -1)
     dkv_parts = lax.all_to_all(dkv, "seq", split_axis=0, concat_axis=0, tiled=True)
     dkv_wide = dkv_parts.reshape(KV, repeat, 2, tok, HD).astype(jnp.float32)
     dkv_sum = jnp.sum(dkv_wide, axis=1).astype(jnp.bfloat16)
@@ -211,8 +210,8 @@
     dkv_next = from_behind(dkv_tokens, "pipe", -1)
     dk_next = dkv_next[0:1]
     dv_next = dkv_next[1:2]
-    dq_first_tok = lax.all_to_all(dq_first_next, "seq", split_axis=0, concat_axis=0, tiled=True)
-    dq_parts = jnp.concatenate([dq_first_tok, dq_second_next], axis=2)
+    dq_heads = jnp.concatenate([dq_first_next, dq_second_next], axis=2)
+    dq_parts = lax.all_to_all(dq_heads, "seq", split_axis=0, concat_axis=0, tiled=True)
     dq_next = unpack(dq_parts)
     return dq_next, dk_next, dv_next
 

time: 256 us -> 264 us (1.031)
  waiting for transfers between devices: 112 us -> 144 us
  blocking collectives: 23.4 us -> 0 us
    ppermute x3, waiting for transfers between devices: 36.6 us -> 62.2 us  [from_behind(): return lax.ppermute(block, axis, route)]
    all_to_all x1 -> x0, blocking collectives: 23.4 us -> none  [body(): lax.all_to_all(dq_second, 'seq', split_axis=0, concat_axis=0, tiled=True)]
    all_to_all x1, waiting for transfers between devices: 1.94 us -> 8.51 us  [body(): lax.all_to_all(dq_heads, 'seq', split_axis=0, concat_axis=0, tiled=True)]
  transfers between devices with their start and end apart: 6 -> 6, of which waited for: 5 -> 5; matrix products, arithmetic and copies ran while one was open for 3% -> 2% of each run, Pallas kernels for 2% -> 0%
where the time goes in v12:
time: 264 us; the launch traced here: 261 us
  waiting for transfers between devices  144 us (55%)
  Pallas kernels  82.3 us (31%)
  starting transfers between devices  28.1 us (11%)
  local copies, waits for them, and re-layouts  3.54 us (1%)
    all_to_all x1, waiting for transfers between devices, body(): lax.all_to_all(send, 'seq', split_axis=0, concat_axis=0, tiled=True)  73.5 us
    pallas_call x2, Pallas kernels, block_grads(): pl.pallas_call(kernel, grid_spec=grid_spec, out_shape=[jax.ShapeDtypeStru...  72.7 us
    ppermute x3, waiting for transfers between devices, from_behind(): return lax.ppermute(block, axis, route)  62.2 us
    all_to_all x1, waiting for transfers between devices, body(): lax.all_to_all(dq_heads, 'seq', split_axis=0, concat_axis=0, tiled=True)  8.51 us
    all_to_all x1, starting transfers between devices, body(): lax.all_to_all(send, 'seq', split_axis=0, concat_axis=0, tiled=True)  7.81 us
    all_to_all x1, starting transfers between devices, body(): lax.all_to_all(dq_heads, 'seq', split_axis=0, concat_axis=0, tiled=True)  7.55 us
    all_to_all x1, starting transfers between devices, body(): lax.all_to_all(dkv, 'seq', split_axis=0, concat_axis=0, tiled=True)  6.81 us
    ppermute x3, starting transfers between devices, from_behind(): return lax.ppermute(block, axis, route)  5.96 us
  transfers between devices with their start and end apart: 6, of which 5 were waited for; matrix products, arithmetic and copies ran while one was open for 2% of the time, Pallas kernels for 0%

profile of v12, /device:TPU:98, one launch (start us, length us, event | category | flops | bytes accessed | tf_op | source)
XLA Modules:
  0.0 261.0 jit_solution(10441658527392666001)
XLA Ops:
  0.6 5.7 %shard_map.94 = bf16[32,6,128,128]{3,2,1,0:T(8,128)(2,1)} custom-call(bf16[1,128,8192]{2,1,0:T(8,128)(2,1)} %q_ref.1, bf16[1,128,8192]{2,1,0:T(8,128)(2,1)} %g_ref.1, bf16[1,128,1024]{2,1,0:T(8,128)(2,1)} %k_ref.1, bf16[1,128,1024]{2,1,0:T(8,128)(2,1)} %v_ref.1), custom_call_target="tpu_custom_call" | custom-call | tf_op jit(solution)/shard_map/pallas_call | solution.py:165
  6.3 7.8 %all-to-all-start = ((bf16[32,6,128,128]{3,2,1,0:T(8,128)(2,1)}), bf16[32,6,128,128]{3,2,1,0:T(8,128)(2,1)}, u32[]{:S(2)}, u32[]{:S(2)}) async-start(bf16[32,6,128,128]{3,2,1,0:T(8,128)(2,1)} %shard_map.94), calls=%async_computation | async-start | bytes 12582912 | tf_op jit(solution)/shard_map/all_to_all | solution.py:200
  14.3 0.1 and_reduce_fusion
  14.4 0.1 copy.25
  14.5 0.7 reshape.39.live_ref
  15.1 0.7 reshape.36.listed_ref
  15.8 73.5 %all-to-all-done.q_ref.g_ref.kv_ref = bf16[32,6,128,128]{3,2,1,0:T(8,128)(2,1)} async-done(((bf16[32,6,128,128]{3,2,1,0:T(8,128)(2,1)}), bf16[32,6,128,128]{3,2,1,0:T(8,128)(2,1)}, u32[]{:S(2)}, u32[]{:S(2)}) %all-to-all-start) | async-done | bytes 6291488 | tf_op jit(solution)/shard_map/all_to_all | solution.py:200
  89.3 36.1 %shard_map.95 = (bf16[32,2,64,128]{3,2,1,0:T(8,128)(2,1)}, f32[32,2,128,128]{3,2,1,0:T(8,128)}) custom-call(s32[512]{0:T(512)} %reshape.36.listed_ref, s32[512]{0:T(512)} %reshape.39.live_ref, bf16[32,6,128,128]{3,2,1,0:T(8,128)(2,1)} %all-to-all-done.q_ref.g_ref.kv_ref, bf16[32,6,128,128]{3,2,1,0:T(8,128)(2,1)} %all-to-all-done.q_ref.g_ref.kv_ref, ...), custom_call_target="tpu_custom_call" | custom-call | flops 3221225472 | bytes 9437184 | tf_op jit(solution)/shard_map/pallas_call | solution.py:130
  125.4 36.6 %shard_map.96 = (bf16[32,2,64,128]{3,2,1,0:T(8,128)(2,1)}, bf16[32,2,128,128]{3,2,1,0:T(8,128)(2,1)}) custom-call(s32[512]{0:T(512)} %reshape.36.listed_ref, s32[512]{0:T(512)} %reshape.39.live_ref, bf16[32,6,128,128]{3,2,1,0:T(8,128)(2,1)} %all-to-all-done.q_ref.g_ref.kv_ref, bf16[32,6,128,128]{3,2,1,0:T(8,128)(2,1)} %all-to-all-done.q_ref.g_ref.kv_ref, ...), custom_call_target="tpu_custom_call" | custom-call | flops 3221225472 | bytes 9437184 | tf_op jit(solution)/shard_map/pallas_call | solution.py:130
  162.0 6.8 %all-to-all-start.2 = ((bf16[32,2,128,128]{3,2,1,0:T(8,128)(2,1)}), bf16[32,2,128,128]{3,2,1,0:T(8,128)(2,1)S(1)}, u32[]{:S(2)}, u32[]{:S(2)}) async-start(bf16[32,2,128,128]{3,2,1,0:T(8,128)(2,1)} %get-tuple-element.10), calls=%async_computation.2 | async-start | bytes 4194304 | tf_op jit(solution)/shard_map/all_to_all | solution.py:206
  168.8 2.0 collective-permute-start.1
  170.9 2.0 collective-permute-start
  172.9 25.3 %collective-permute-done.1 = bf16[32,2,64,128]{3,2,1,0:T(8,128)(2,1)S(1)} collective-permute-done((bf16[32,2,64,128]{3,2,1,0:T(8,128)(2,1)}, bf16[32,2,64,128]{3,2,1,0:T(8,128)(2,1)S(1)}, u32[]{:S(2)}, u32[]{:S(2)}) %collective-permute-start.1) | collective-permute-done | bytes 1048608 | tf_op jit(solution)/shard_map/ppermute | solution.py:20
  198.2 21.8 %collective-permute-done = bf16[32,2,64,128]{3,2,1,0:T(8,128)(2,1)S(1)} collective-permute-done((bf16[32,2,64,128]{3,2,1,0:T(8,128)(2,1)S(1)}, bf16[32,2,64,128]{3,2,1,0:T(8,128)(2,1)S(1)}, u32[]{:S(2)}, u32[]{:S(2)}) %collective-permute-start) | collective-permute-done | bytes 1048608 | tf_op jit(solution)/shard_map/ppermute | solution.py:20
  220.0 1.5 pad_maximum_fusion
  221.5 7.5 %all-to-all-start.1 = ((bf16[32,2,128,128]{3,2,1,0:T(8,128)(2,1)}), bf16[32,2,128,128]{3,2,1,0:T(8,128)(2,1)}, u32[]{:S(2)}, u32[]{:S(2)}) async-start(bf16[32,2,128,128]{3,2,1,0:T(8,128)(2,1)} %pad_maximum_fusion), calls=%async_computation.1 | async-start | bytes 4194304 | tf_op jit(solution)/shard_map/all_to_all | solution.py:214
  229.1 0.4 bitcast_reduce_fusion
  229.5 0.3 copy.26
  229.7 1.9 collective-permute-start.2
  231.7 15.1 %collective-permute-done.2 = bf16[2,128,1024]{1,2,0:T(8,128)(2,1)S(1)} collective-permute-done((bf16[2,128,1024]{1,2,0:T(8,128)(2,1)S(1)}, bf16[2,128,1024]{1,2,0:T(8,128)(2,1)S(1)}, u32[]{:S(2)}, u32[]{:S(2)}) %collective-permute-start.2) | collective-permute-done | bytes 524320 | tf_op jit(solution)/shard_map/ppermute | solution.py:20
  246.8 0.9 copy.28
  247.7 0.8 copy.27
  248.5 8.5 %all-to-all-done.1.src_ref = bf16[32,2,128,128]{3,2,1,0:T(8,128)(2,1)} async-done(((bf16[32,2,128,128]{3,2,1,0:T(8,128)(2,1)}), bf16[32,2,128,128]{3,2,1,0:T(8,128)(2,1)}, u32[]{:S(2)}, u32[]{:S(2)}) %all-to-all-start.1) | async-done | bytes 2097184 | tf_op jit(solution)/shard_map/all_to_all | solution.py:214
  257.0 4.0 %shard_map.97 = bf16[1,128,8192]{2,1,0:T(8,128)(2,1)} custom-call(bf16[32,2,128,128]{3,2,1,0:T(8,128)(2,1)} %all-to-all-done.1.src_ref), custom_call_target="tpu_custom_call" | custom-call | tf_op jit(solution)/shard_map/pallas_call | solution.py:184
  (14 shorter events, 0.2 us)
Async XLA Ops:
  6.3 7.8 %copy-start = (s32[64,3]{0,1:T(4,128)S(1)}, s32[64,3]{0,1:T(4,128)}, u32[]{:S(2)}) copy-start(s32[64,3]{0,1:T(4,128)} %param.13) | copy-start | bytes 2308
  6.3 7.8 %copy-start.1 = (s32[64,3]{0,1:T(4,128)S(1)}, s32[64,3]{0,1:T(4,128)}, u32[]{:S(2)}) copy-start(s32[64,3]{0,1:T(4,128)} %param.11) | copy-start | bytes 2308
  6.3 7.8 %copy-start.2 = (s32[64,2]{0,1:T(2,128)S(1)}, s32[64,2]{0,1:T(2,128)}, u32[]{:S(2)}) copy-start(s32[64,2]{0,1:T(2,128)} %param.12) | copy-start | bytes 1540
  6.3 83.0 %all-to-all-start = ((bf16[32,6,128,128]{3,2,1,0:T(8,128)(2,1)}), bf16[32,6,128,128]{3,2,1,0:T(8,128)(2,1)}, u32[]{:S(2)}, u32[]{:S(2)}) async-start(bf16[32,6,128,128]{3,2,1,0:T(8,128)(2,1)} %shard_map.94), calls=%async_computation | async-start | bytes 12582912 | tf_op jit(solution)/shard_map/all_to_all | solution.py:200
  162.0 8.9 %copy-start.3 = (bf16[32,2,64,128]{3,2,1,0:T(8,128)(2,1)S(1)}, bf16[32,2,64,128]{3,2,1,0:T(8,128)(2,1)}, u32[]{:S(2)}) copy-start(bf16[32,2,64,128]{3,2,1,0:T(8,128)(2,1)} %get-tuple-element.7) | copy-start | bytes 3145732
  162.0 59.5 %all-to-all-start.2 = ((bf16[32,2,128,128]{3,2,1,0:T(8,128)(2,1)}), bf16[32,2,128,128]{3,2,1,0:T(8,128)(2,1)S(1)}, u32[]{:S(2)}, u32[]{:S(2)}) async-start(bf16[32,2,128,128]{3,2,1,0:T(8,128)(2,1)} %get-tuple-element.10), calls=%async_computation.2 | async-start | bytes 4194304 | tf_op jit(solution)/shard_map/all_to_all | solution.py:206
  168.8 29.3 %collective-permute-start.1 = (bf16[32,2,64,128]{3,2,1,0:T(8,128)(2,1)}, bf16[32,2,64,128]{3,2,1,0:T(8,128)(2,1)S(1)}, u32[]{:S(2)}, u32[]{:S(2)}) collective-permute-start(bf16[32,2,64,128]{3,2,1,0:T(8,128)(2,1)} %get-tuple-element.9), channel_id=1, source_target_pairs={{32,0},{64,32},{96,64},{128,96},{160,128},{192,160},{224,192},{33,... | collective-permute-start | bytes 3145736 | tf_op jit(solution)/shard_map/ppermute | solution.py:20
  170.9 49.1 %collective-permute-start = (bf16[32,2,64,128]{3,2,1,0:T(8,128)(2,1)S(1)}, bf16[32,2,64,128]{3,2,1,0:T(8,128)(2,1)S(1)}, u32[]{:S(2)}, u32[]{:S(2)}) collective-permute-start(bf16[32,2,64,128]{3,2,1,0:T(8,128)(2,1)S(1)} %copy-done.3), channel_id=1, source_target_pairs={{32,0},{64,32},{96,64},{128,96},{160,128},{192,160},{224,192},{33,... | collective-permute-start | bytes 3145736 | tf_op jit(solution)/shard_map/ppermute | solution.py:20
  221.5 35.5 %all-to-all-start.1 = ((bf16[32,2,128,128]{3,2,1,0:T(8,128)(2,1)}), bf16[32,2,128,128]{3,2,1,0:T(8,128)(2,1)}, u32[]{:S(2)}, u32[]{:S(2)}) async-start(bf16[32,2,128,128]{3,2,1,0:T(8,128)(2,1)} %pad_maximum_fusion), calls=%async_computation.1 | async-start | bytes 4194304 | tf_op jit(solution)/shard_map/all_to_all | solution.py:214
  229.7 17.0 %collective-permute-start.2 = (bf16[2,128,1024]{1,2,0:T(8,128)(2,1)S(1)}, bf16[2,128,1024]{1,2,0:T(8,128)(2,1)S(1)}, u32[]{:S(2)}, u32[]{:S(2)}) collective-permute-start(bf16[2,128,1024]{1,2,0:T(8,128)(2,1)S(1)} %bitcast.5), channel_id=1, source_target_pairs={{32,0},{64,32},{96,64},{128,96},{160,128},{192,160},{224,192},{33,... | collective-permute-start | bytes 1572872 | tf_op jit(solution)/shard_map/ppermute | solution.py:20
